TPU v7x, 768 devices: a whole 4x8x12 slice. The times are simulated.
768 devices in a mesh: enc: 12 (over z), grp: 64 (over y, x, core).
Axes of the slice: x: 4, y: 8, z: 12, core: 2. Of those that a mesh axis runs over, the one named last changes fastest.
Arguments:
- query_raw: bfloat16 [147456, 1024], P(('enc', 'grp')), may hold values from -6 to 6
- key_raw: bfloat16 [147456, 1024], P(('enc', 'grp')), may hold values from -6 to 6
- value_rows: bfloat16 [147456, 1024], P(('enc', 'grp')), may hold values from -6 to 6
- out_cotangent: bfloat16 [147456, 1024], P(('enc', 'grp')), may hold values from -6 to 6
- image_ids: int32 [147456], P(('enc', 'grp')), may hold values from 0 to 15, as said below
- owners: int32 [64, 12, 12], P('grp'), may hold values from -1 to 11, as said below
- gains: float32 [2, 1024], replicated, may hold values from 0.1 to 1.9
Outputs:
- query_grad: bfloat16 [98304, 1024], P(('enc', 'grp'))
- key_grad: bfloat16 [98304, 1024], P(('enc', 'grp'))
- value_grad: bfloat16 [98304, 1024], P(('enc', 'grp'))
- gain_grad: float32 [2, 1024], P(None, 'grp')
Inputs may be any that keep to these rules, and one draw needn't show every extreme that they name: `image_ids`: inside each piece of 16 rows the number is 0 at the first row and rises by 0 or 1 from row to row. `owners`: A loader's live slots come first; a loader gives at most 1 pieces to one owner and some loader of each group gives exactly 1 to every owner; every owner receives exactly 8 pieces of its group.
All inputs are finite; a program needn't handle non-finite values.
Results may differ from a plain program's by a relative error of at most 0.0073.
Values may be sent and summed in bfloat16 or wider, within the bound.
No kernel may reach another device: no remote copies, remote signals or barrier semaphores. Data moves between devices by JAX's collectives and lax.ppermute only.
A program may use at most 32 MiB of HBM per device.

v0:
```python
import math

import jax
import jax.numpy as jnp
from jax import lax
from jax.sharding import PartitionSpec as P

HEADS = 16
HD = 64
PIECE = 16
PMAX = 12
P_OWN = 8


epsilon = 1e-05


def normalize(blocks, gain_row):
    num_pieces = blocks.shape[0]
    values_four = blocks.astype(jnp.float32).reshape(num_pieces, PIECE, HEADS, HD)
    centred = values_four - jnp.mean(values_four, -1, keepdims=True)
    inv_scale = lax.rsqrt(jnp.mean(centred * centred, -1, keepdims=True) + epsilon)
    normed = centred * inv_scale
    return (normed, inv_scale, (normed * gain_row).astype(jnp.bfloat16))


def norm_back(d_hat, normed, inv_scale, gain_row, live_flags):
    d_norm = d_hat * gain_row
    d_input = inv_scale * (
        d_norm
        - jnp.mean(d_norm, -1, keepdims=True)
        - normed * jnp.mean(d_norm * normed, -1, keepdims=True)
    )
    gain_term = jnp.sum(d_hat * normed * live_flags[:, None, None, None], (0, 1))
    return (d_input, gain_term.reshape(-1))


def piece_grads(query_rows, key_rows, value_rows, cotangent, image_num, gains, live_flags):
    num_pieces = query_rows.shape[0]
    four_shape = (num_pieces, PIECE, HEADS, HD)
    gain_query = gains[0].reshape(HEADS, HD)
    gain_key = gains[1].reshape(HEADS, HD)
    q_norm, q_scale, q_hat = normalize(query_rows, gain_query)
    k_norm, k_scale, k_hat = normalize(key_rows, gain_key)
    values_four = value_rows.reshape(four_shape)
    cot_four = cotangent.reshape(four_shape)
    factor = HD ** (-0.5)
    scores = (
        jnp.einsum("bihd,bjhd->bhij", q_hat, k_hat, preferred_element_type=jnp.float32) * factor
    )
    same_image = image_num[:, None, :, None] == image_num[:, None, None, :]
    weights = jnp.where(same_image, jnp.exp(scores), 0.0)
    probs = weights / jnp.sum(weights, -1, keepdims=True)
    probs_b = probs.astype(jnp.bfloat16)
    attended = jnp.einsum(
        "bhij,bjhd->bihd", probs_b, values_four, preferred_element_type=jnp.float32
    )
    row_delta = jnp.sum(cot_four.astype(jnp.float32) * attended, -1)
    d_value = jnp.einsum(
        "bhij,bihd->bjhd", probs_b, cot_four, preferred_element_type=jnp.float32
    ).astype(jnp.bfloat16)
    d_prob = jnp.einsum(
        "bihd,bjhd->bhij", cot_four, values_four, preferred_element_type=jnp.float32
    )
    d_score = (probs * (d_prob - jnp.transpose(row_delta, (0, 2, 1))[..., None]) * factor).astype(
        jnp.bfloat16
    )
    d_qhat = jnp.einsum("bhij,bjhd->bihd", d_score, k_hat, preferred_element_type=jnp.float32)
    d_khat = jnp.einsum("bhij,bihd->bjhd", d_score, q_hat, preferred_element_type=jnp.float32)
    d_query, term_query = norm_back(d_qhat, q_norm, q_scale, gain_query, live_flags)
    d_key, term_key = norm_back(d_khat, k_norm, k_scale, gain_key, live_flags)
    flat_shape = (num_pieces, PIECE, HEADS * HD)
    return (
        d_query.reshape(flat_shape).astype(jnp.bfloat16),
        d_key.reshape(flat_shape).astype(jnp.bfloat16),
        d_value.reshape(flat_shape),
        jnp.stack([term_query, term_key]),
    )


def send_slots(own_plan, enc_count, per_slot):
    owner_hit = (own_plan[:, None] == jnp.arange(enc_count, dtype=jnp.int32)[None, :]).astype(
        jnp.int32
    )
    slot_rank = jnp.sum((jnp.cumsum(owner_hit, 0) - owner_hit) * owner_hit, 1)
    slot_target = jnp.where(own_plan >= 0, own_plan * per_slot + slot_rank, -1)
    slot_ids = jnp.arange(enc_count * per_slot, dtype=jnp.int32)
    matches = (slot_target[None, :] == slot_ids[:, None]).astype(jnp.int32)
    slot_source = jnp.sum(matches * jnp.arange(PMAX, dtype=jnp.int32)[None, :], 1)
    slot_filled = jnp.sum(matches, 1) > 0
    return (slot_source, slot_filled)


def receive_order(group_plan, enc_rank, enc_count, per_slot):
    arrived = jnp.sum((group_plan == enc_rank).astype(jnp.int32), 1)
    live_slots = (
        (jnp.arange(per_slot, dtype=jnp.int32)[None, :] < arrived[:, None])
        .reshape(-1)
        .astype(jnp.int32)
    )
    live_order = jnp.cumsum(live_slots) - 1
    wanted = jnp.arange(P_OWN, dtype=jnp.int32)
    matches = ((live_order[None, :] == wanted[:, None]) & (live_slots[None, :] > 0)).astype(
        jnp.int32
    )
    return jnp.sum(matches * jnp.arange(enc_count * per_slot, dtype=jnp.int32)[None, :], 1)


def to_slots(pieces, slot_source, slot_filled):
    taken = jnp.take(pieces, slot_source, axis=0)
    mask_shape = (slot_filled.shape[0],) + (1,) * (pieces.ndim - 1)
    taken = jnp.where(slot_filled.reshape(mask_shape), taken, jnp.zeros_like(taken))
    return taken


def from_slots(received, arrival_order):
    return jnp.take(received, arrival_order, axis=0)


def local(query_raw, key_raw, value_rows, out_cotangent, image_ids, owners, gains):
    enc_count = lax.axis_size("enc")
    enc_rank = lax.axis_index("enc")
    per_slot = PMAX // enc_count
    feat = HEADS * HD
    group_plan = owners[0]
    own_plan = lax.dynamic_index_in_dim(group_plan, enc_rank, 0, keepdims=False)
    slot_source, slot_filled = send_slots(own_plan, enc_count, per_slot)
    arrival_order = receive_order(group_plan, enc_rank, enc_count, per_slot)
    piece_shape = (PMAX, PIECE, feat)
    packed = tuple(
        (
            to_slots(array.reshape(piece_shape), slot_source, slot_filled)
            for array in (query_raw, key_raw, value_rows, out_cotangent)
        )
    )
    image_slots = to_slots(
        image_ids.astype(jnp.bfloat16).reshape(PMAX, PIECE), slot_source, slot_filled
    )
    received = (
        lax.all_to_all(packed[0], "enc", split_axis=0, concat_axis=0, tiled=True),
        lax.all_to_all(packed[1], "enc", split_axis=0, concat_axis=0, tiled=True),
        lax.all_to_all(packed[2], "enc", split_axis=0, concat_axis=0, tiled=True),
        lax.all_to_all(packed[3], "enc", split_axis=0, concat_axis=0, tiled=True),
        lax.all_to_all(image_slots, "enc", split_axis=0, concat_axis=0, tiled=True),
    )
    mine_q, mine_k, mine_v, mine_d, mine_i = (
        from_slots(array, arrival_order) for array in received
    )
    d_query, d_key, d_value, gain_terms = piece_grads(
        mine_q, mine_k, mine_v, mine_d, mine_i, gains, jnp.ones((P_OWN,), jnp.float32)
    )
    group_total = lax.psum(gain_terms, "enc")
    shares = lax.psum_scatter(group_total, "grp", scatter_dimension=1, tiled=True)
    total_live = enc_count * lax.axis_size("grp") * P_OWN * PIECE
    gain_grad = shares / math.sqrt(total_live)
    own_rows = P_OWN * PIECE
    return (
        d_query.reshape(own_rows, feat),
        d_key.reshape(own_rows, feat),
        d_value.reshape(own_rows, feat),
        gain_grad,
    )


def solution(mesh):
    return jax.shard_map(
        local,
        mesh=mesh,
        in_specs=(
            P(("enc", "grp"), None),
            P(("enc", "grp"), None),
            P(("enc", "grp"), None),
            P(("enc", "grp"), None),
            P(("enc", "grp")),
            P("grp", None, None),
            P(),
        ),
        out_specs=(
            P(("enc", "grp"), None),
            P(("enc", "grp"), None),
            P(("enc", "grp"), None),
            P(None, "grp"),
        ),
        check_vma=False,
    )
```

profile of v0, /device:TPU:32, one launch (start us, length us, event | category | flops | bytes accessed | tf_op | source)
XLA Modules:
  0.0 302.5 jit_solution(15597987454328838856)
XLA Ops:
  3.2 15.2 %all-to-all-start.2 = ((bf16[12,1,16]{2,1,0:T(2,128)(2,1)}), bf16[12,1,16]{2,1,0:T(2,128)(2,1)S(1)}, u32[]{:S(2)}, u32[]{:S(2)}) async-start(bf16[12,1,16]{2,1,0:T(2,128)(2,1)} %copy.107), calls=%async_computation.2 | async-start | bytes 12288 | tf_op jit(solution)/shard_map/all_to_all | solution.py:144
  22.0 1.1 select_select_fusion.1
  23.1 5.3 %all-to-all-done.2 = bf16[12,1,16]{2,1,0:T(2,128)(2,1)S(1)} async-done(((bf16[12,1,16]{2,1,0:T(2,128)(2,1)}), bf16[12,1,16]{2,1,0:T(2,128)(2,1)S(1)}, u32[]{:S(2)}, u32[]{:S(2)}) %all-to-all-start.2) | async-done | bytes 416 | tf_op jit(solution)/shard_map/all_to_all | solution.py:144
  28.4 23.3 %all_to_all.29 = bf16[12,16,1024]{2,1,0:T(8,128)(2,1)S(1)} all-to-all(bf16[12,16,1024]{2,1,0:T(8,128)(2,1)S(1)} %get-tuple-element.16), channel_id=1, replica_groups=mesh['enc'=12,'grp'=64] {'enc'}, dimensions={0} | all-to-all | bytes 786432 | tf_op jit(solution)/shard_map/all_to_all | solution.py:143
  51.7 23.0 %all_to_all.30 = bf16[12,16,1024]{2,1,0:T(8,128)(2,1)S(1)} all-to-all(bf16[12,16,1024]{2,1,0:T(8,128)(2,1)S(1)} %get-tuple-element.17), channel_id=1, replica_groups=mesh['enc'=12,'grp'=64] {'enc'}, dimensions={0} | all-to-all | bytes 786432 | tf_op jit(solution)/shard_map/all_to_all | solution.py:141
  74.7 3.6 %all-to-all-start.4 = ((bf16[12,16,1024]{2,1,0:T(8,128)(2,1)}), bf16[12,16,1024]{2,1,0:T(8,128)(2,1)S(1)}, u32[]{:S(2)}, u32[]{:S(2)}) async-start(bf16[12,16,1024]{2,1,0:T(8,128)(2,1)} %get-tuple-element.18), calls=%async_computation.4 | async-start | bytes 786432 | tf_op jit(solution)/shard_map/all_to_all | solution.py:142
  79.2 1.3 dynamic-slice.1
  81.2 16.8 %all-to-all-done.4 = bf16[12,16,1024]{2,1,0:T(8,128)(2,1)S(1)} async-done(((bf16[12,16,1024]{2,1,0:T(8,128)(2,1)}), bf16[12,16,1024]{2,1,0:T(8,128)(2,1)S(1)}, u32[]{:S(2)}, u32[]{:S(2)}) %all-to-all-start.4) | async-done | bytes 393248 | tf_op jit(solution)/shard_map/all_to_all | solution.py:142
  98.0 4.0 %all-to-all-start = ((bf16[12,16,1024]{2,1,0:T(8,128)(2,1)}), bf16[12,16,1024]{2,1,0:T(8,128)(2,1)S(1)}, u32[]{:S(2)}, u32[]{:S(2)}) async-start(bf16[12,16,1024]{2,1,0:T(8,128)(2,1)} %get-tuple-element.19), calls=%async_computation | async-start | bytes 786432 | tf_op jit(solution)/shard_map/all_to_all | solution.py:140
  105.1 16.6 %all-to-all-done = bf16[12,16,1024]{2,1,0:T(8,128)(2,1)S(1)} async-done(((bf16[12,16,1024]{2,1,0:T(8,128)(2,1)}), bf16[12,16,1024]{2,1,0:T(8,128)(2,1)S(1)}, u32[]{:S(2)}, u32[]{:S(2)}) %all-to-all-start) | async-done | bytes 393248 | tf_op jit(solution)/shard_map/all_to_all | solution.py:140
  122.5 1.2 reshape.302
  123.6 1.1 reshape.304
  125.5 0.8 multiply_reduce_fusion.4
  129.4 2.2 fusion.11
  131.7 1.5 fusion.7
  134.7 3.4 %multiply_reduce_fusion = (f32[16,64]{1,0:T(8,128)S(1)}, f32[8,16,16]{1,2,0:T(8,128)S(1)}, f32[8,16,16]{1,2,0:T(8,128)S(1)}, f32[8,16,16,64]{3,1,2,0:T(8,128)}) fusion(f32[8,16,16]{1,2,0:T(8,128)S(1)} %copy-done.15, f32[8,16,16]{1,2,0:T(8,128)S(1)} %copy-done.8, f32[8,16,16,64]{3,2,1,0:T(8,128)S(1)} %reshape.309, f32[16,64]{1,0:T(8,128)S(1)} %mul.132, ...), kind=kOutput, calls=%fused_computation.26 | convolution fusion | flops 5762048 | bytes 1699840 | tf_op jit(solution)/shard_map/bhij,bihd->bjhd/dot_general | solution.py:69
  138.1 3.9 %multiply_reduce_fusion.1 = (f32[16,64]{1,0:T(8,128)S(1)}, f32[8,16,16]{1,2,0:T(8,128)S(1)}, f32[8,16,16]{1,2,0:T(8,128)S(1)}, f32[8,16,16,64]{3,1,2,0:T(8,128)}) fusion(f32[8,16,16]{1,2,0:T(8,128)S(1)} %copy-done.13, f32[8,16,16]{1,2,0:T(8,128)S(1)} %copy-done.5, f32[8,16,16,64]{3,2,1,0:T(8,128)S(1)} %reshape.307, f32[16,64]{1,0:T(8,128)S(1)} %mul.136, ...), kind=kOutput, calls=%fused_computation.27 | convolution fusion | flops 5762048 | bytes 1699840 | tf_op jit(solution)/shard_map/bhij,bjhd->bihd/dot_general | solution.py:68
  142.2 1.1 reshape_reshape.3
  143.8 127.0 %all-reduce = f32[2,1024]{1,0:T(2,128)S(1)} all-reduce(f32[2,1024]{1,0:T(2,128)S(1)} %pad_maximum_fusion), channel_id=2, replica_groups=mesh['enc'=12,'grp'=64] {'grp'}, use_global_device_ids=true, to_apply=%region_20.23.clone | all-reduce | flops 2048 | bytes 16384
  270.8 23.9 %psum.8 = f32[2,16]{1,0:T(2,128)S(1)} all-reduce(f32[2,16]{1,0:T(2,128)S(1)} %constant_dynamic-slice_fusion), channel_id=1, replica_groups=mesh['enc'=12,'grp'=64] {'enc'}, use_global_device_ids=true, to_apply=%region_19.22 | all-reduce | flops 32 | bytes 256 | tf_op jit(solution)/shard_map/psum | solution.py:152
  295.3 2.3 multiply_convert_fusion
  297.8 1.1 convert_element_type.87
  300.0 1.3 multiply_convert_fusion.1
  301.4 1.1 convert_element_type.85
  (123 shorter events, 18.7 us)
Async XLA Ops:
  0.6 17.8 %copy-start = (bf16[192,1024]{1,0:T(8,128)(2,1)S(1)}, bf16[192,1024]{1,0:T(8,128)(2,1)}, u32[]{:S(2)}) copy-start(bf16[192,1024]{1,0:T(8,128)(2,1)} %param.13) | copy-start | bytes 1179652
  0.7 0.7 copy-start.21
  0.7 0.8 copy-start.18
  3.2 25.2 %all-to-all-start.2 = ((bf16[12,1,16]{2,1,0:T(2,128)(2,1)}), bf16[12,1,16]{2,1,0:T(2,128)(2,1)S(1)}, u32[]{:S(2)}, u32[]{:S(2)}) async-start(bf16[12,1,16]{2,1,0:T(2,128)(2,1)} %copy.107), calls=%async_computation.2 | async-start | bytes 12288 | tf_op jit(solution)/shard_map/all_to_all | solution.py:144
  18.4 1.0 copy-start.10
  19.4 1.0 copy-start.11
  20.4 1.0 copy-start.12
  74.7 23.3 %all-to-all-start.4 = ((bf16[12,16,1024]{2,1,0:T(8,128)(2,1)}), bf16[12,16,1024]{2,1,0:T(8,128)(2,1)S(1)}, u32[]{:S(2)}, u32[]{:S(2)}) async-start(bf16[12,16,1024]{2,1,0:T(8,128)(2,1)} %get-tuple-element.18), calls=%async_computation.4 | async-start | bytes 786432 | tf_op jit(solution)/shard_map/all_to_all | solution.py:142
  78.3 0.7 copy-start.17
  98.0 23.7 %all-to-all-start = ((bf16[12,16,1024]{2,1,0:T(8,128)(2,1)}), bf16[12,16,1024]{2,1,0:T(8,128)(2,1)S(1)}, u32[]{:S(2)}, u32[]{:S(2)}) async-start(bf16[12,16,1024]{2,1,0:T(8,128)(2,1)} %get-tuple-element.19), calls=%async_computation | async-start | bytes 786432 | tf_op jit(solution)/shard_map/all_to_all | solution.py:140
  105.1 17.2 %copy-start.20 = (pred[8]{0:T(512)(128)(4,1)S(1)}, pred[8]{0:T(512)(128)(4,1)}, u32[]{:S(2)}) copy-start(pred[8]{0:T(512)(128)(4,1)} %copy-done.19) | copy-start | bytes 28
  125.5 0.8 copy-start.7
  127.8 0.8 copy-start.4
  131.6 1.6 copy-start.1
  131.6 1.6 copy-start.2
  133.8 0.8 copy-start.5
  133.8 0.9 copy-start.8
  133.8 0.9 copy-start.13
  133.8 0.9 copy-start.15
  143.6 151.8 %copy-start.9 = (f32[8,16,16]{1,2,0:T(8,128)S(1)}, f32[8,16,16]{1,2,0:T(8,128)}, u32[]{:S(2)}) copy-start(f32[8,16,16]{1,2,0:T(8,128)} %copy-done.7) | copy-start | bytes 24580
  143.6 151.8 %copy-start.16 = (f32[8,16,16]{1,2,0:T(8,128)S(1)}, f32[8,16,16]{1,2,0:T(8,128)}, u32[]{:S(2)}) copy-start(f32[8,16,16]{1,2,0:T(8,128)} %copy.106) | copy-start | bytes 24580
  297.8 1.4 copy-start.3
  299.2 0.8 copy-start.6
  299.2 0.9 copy-start.14
  (1 other events, 0.6 us)
where the time goes:
time: 303 us; the launch traced here: 302 us
  blocking collectives  197 us (65%)
  waiting for transfers between devices  38.6 us (13%)
  starting transfers between devices  22.7 us (7%)
  local copies, waits for them, and re-layouts  20.2 us (7%)
  matrix products  12 us (4%)
  other arithmetic  9.75 us (3%)
    unnamed x1, blocking collectives  127 us
    psum x1, blocking collectives, local(): group_total = lax.psum(gain_terms, 'enc')  23.9 us
    all_to_all x1, blocking collectives, local(): lax.all_to_all(packed[3], 'enc', split_axis=0, concat_axis=0, tiled=True)  23.3 us
    all_to_all x1, blocking collectives, local(): lax.all_to_all(packed[1], 'enc', split_axis=0, concat_axis=0, tiled=True)  23 us
    all_to_all x1, waiting for transfers between devices, local(): lax.all_to_all(packed[2], 'enc', split_axis=0, concat_axis=0, tiled=True)  16.8 us
    all_to_all x1, waiting for transfers between devices, local(): lax.all_to_all(packed[0], 'enc', split_axis=0, concat_axis=0, tiled=True)  16.6 us
    all_to_all x1, starting transfers between devices, local(): lax.all_to_all(image_slots, 'enc', split_axis=0, concat_axis=0, tiled=True)  15.2 us
  transfers between devices with their start and end apart: 3, of which 3 were waited for; matrix products, arithmetic and copies ran while one was open for 3% of the time, Pallas kernels for 0%

commit v1 on v0

--- a/solution.py
+++ b/solution.py
@@ -114,11 +114,12 @@
 
 
 def from_slots(received, arrival_order):
-    return jnp.take(received, arrival_order, axis=0)
+    return jnp.take(received, arrival_order, axis=0, mode="clip")
 
 
 def local(query_raw, key_raw, value_rows, out_cotangent, image_ids, owners, gains):
     enc_count = lax.axis_size("enc")
+    grp_count = lax.axis_size("grp")
     enc_rank = lax.axis_index("enc")
     per_slot = PMAX // enc_count
     feat = HEADS * HD
@@ -127,37 +128,37 @@
     slot_source, slot_filled = send_slots(own_plan, enc_count, per_slot)
     arrival_order = receive_order(group_plan, enc_rank, enc_count, per_slot)
     piece_shape = (PMAX, PIECE, feat)
-    packed = tuple(
-        (
-            to_slots(array.reshape(piece_shape), slot_source, slot_filled)
-            for array in (query_raw, key_raw, value_rows, out_cotangent)
-        )
+    live_flags = (own_plan >= 0).astype(jnp.float32)
+    d_query, d_key, d_value, gain_terms = piece_grads(
+        query_raw.reshape(piece_shape),
+        key_raw.reshape(piece_shape),
+        value_rows.reshape(piece_shape),
+        out_cotangent.reshape(piece_shape),
+        image_ids.reshape(PMAX, PIECE),
+        gains,
+        live_flags,
     )
-    image_slots = to_slots(
-        image_ids.astype(jnp.bfloat16).reshape(PMAX, PIECE), slot_source, slot_filled
+    grads = jnp.concatenate((d_query, d_key, d_value), axis=-1)
+    packed = jnp.take(grads, slot_source, axis=0, mode="clip")
+    received = lax.all_to_all(packed, "enc", split_axis=0, concat_axis=0, tiled=True)
+    mine = from_slots(received, arrival_order)
+    cols = feat // grp_count
+    by_grp = jnp.transpose(gain_terms.reshape(2, grp_count, cols), (1, 0, 2))
+    grp_sum = jnp.sum(
+        lax.all_to_all(by_grp, "grp", split_axis=0, concat_axis=0, tiled=True), axis=0
     )
-    received = (
-        lax.all_to_all(packed[0], "enc", split_axis=0, concat_axis=0, tiled=True),
-        lax.all_to_all(packed[1], "enc", split_axis=0, concat_axis=0, tiled=True),
-        lax.all_to_all(packed[2], "enc", split_axis=0, concat_axis=0, tiled=True),
-        lax.all_to_all(packed[3], "enc", split_axis=0, concat_axis=0, tiled=True),
-        lax.all_to_all(image_slots, "enc", split_axis=0, concat_axis=0, tiled=True),
+    by_enc = jnp.broadcast_to(grp_sum[None], (enc_count, 2, cols))
+    shares = jnp.sum(
+        lax.all_to_all(by_enc, "enc", split_axis=0, concat_axis=0, tiled=True), axis=0
     )
-    mine_q, mine_k, mine_v, mine_d, mine_i = (
-        from_slots(array, arrival_order) for array in received
-    )
-    d_query, d_key, d_value, gain_terms = piece_grads(
-        mine_q, mine_k, mine_v, mine_d, mine_i, gains, jnp.ones((P_OWN,), jnp.float32)
-    )
-    group_total = lax.psum(gain_terms, "enc")
-    shares = lax.psum_scatter(group_total, "grp", scatter_dimension=1, tiled=True)
-    total_live = enc_count * lax.axis_size("grp") * P_OWN * PIECE
+    total_live = enc_count * grp_count * P_OWN * PIECE
     gain_grad = shares / math.sqrt(total_live)
     own_rows = P_OWN * PIECE
+    mine = mine.reshape(own_rows, 3 * feat)
     return (
-        d_query.reshape(own_rows, feat),
-        d_key.reshape(own_rows, feat),
-        d_value.reshape(own_rows, feat),
+        mine[:, :feat],
+        mine[:, feat : 2 * feat],
+        mine[:, 2 * feat :],
         gain_grad,
     )
 

time: 303 us -> 154 us (0.51)
  the two profiles are of different devices: /device:TPU:32 before, /device:TPU:2 now
where the time goes in v1:
time: 154 us; the launch traced here: 153 us
  waiting for transfers between devices  52.8 us (34%)
  local copies, waits for them, and re-layouts  29.8 us (19%)
  starting transfers between devices  29.7 us (19%)
  matrix products  21.5 us (14%)
  other arithmetic  18.1 us (12%)
    all_to_all x1, waiting for transfers between devices, local(): lax.all_to_all(packed, 'enc', split_axis=0, concat_axis=0, tiled=True)  44.3 us
    all_to_all x1, starting transfers between devices, local(): lax.all_to_all(by_grp, 'grp', split_axis=0, concat_axis=0, tiled=True)  14.3 us
    all_to_all x1, starting transfers between devices, local(): lax.all_to_all(by_enc, 'enc', split_axis=0, concat_axis=0, tiled=True)  11.7 us
    dot_general x1, matrix products, piece_grads(): jnp.einsum('bhij,bjhd->bihd', d_score, k_hat, preferred_element_type=jnp....  9.43 us
    all_to_all x1, waiting for transfers between devices, local(): lax.all_to_all(by_enc, 'enc', split_axis=0, concat_axis=0, tiled=True)  8.44 us
    div x1, matrix products, piece_grads(): probs = weights / jnp.sum(weights, -1, keepdims=True)  4.38 us
    convert_element_type x1, other arithmetic, piece_grads(): d_key.reshape(flat_shape).astype(jnp.bfloat16)  3.72 us
    all_to_all x1, starting transfers between devices, local(): lax.all_to_all(packed, 'enc', split_axis=0, concat_axis=0, tiled=True)  3.7 us
  transfers between devices with their start and end apart: 3, of which 2 were waited for; matrix products, arithmetic and copies ran while one was open for 18% of the time, Pallas kernels for 0%

profile of v1, /device:TPU:2, one launch (start us, length us, event | category | flops | bytes accessed | tf_op | source)
XLA Modules:
  0.0 152.9 jit_solution(12876872388129537317)
XLA Ops:
  0.6 2.4 %reshape_reshape.6 = bf16[12,16,16,64]{3,2,1,0:T(8,128)(2,1)} reshape(bf16[192,1024]{1,0:T(8,128)(2,1)} %param.10) | data formatting | bytes 786432 | tf_op jit(solution)/shard_map/reshape;reshape | solution.py:46
  5.4 1.5 %reshape.160 = f32[12,16,16,64]{3,2,1,0:T(8,128)S(1)} reshape(bf16[192,1024]{1,0:T(8,128)(2,1)} %param.8) | data formatting | bytes 1179648 | tf_op jit(solution)/shard_map/convert_element_type | solution.py:20
  9.5 1.5 %reshape.159 = f32[12,16,16,64]{3,2,1,0:T(8,128)S(1)} reshape(bf16[192,1024]{1,0:T(8,128)(2,1)} %param.7) | data formatting | bytes 1179648 | tf_op jit(solution)/shard_map/convert_element_type | solution.py:20
  13.0 2.4 %reshape_reshape.7 = bf16[12,16,16,64]{3,2,1,0:T(8,128)(2,1)} reshape(bf16[192,1024]{1,0:T(8,128)(2,1)} %param.9) | data formatting | bytes 786432 | tf_op jit(solution)/shard_map/reshape;reshape | solution.py:45
  15.4 4.4 %fusion.11 = f32[12,16,16,16]{2,3,1,0:T(8,128)} fusion(pred[12,16,16]{1,2,0:T(8,128)(4,1)} %broadcast_compare_fusion, f32[16,64]{1,0:T(8,128)S(1)} %mul.142, f32[12,16,16]{1,2,0:T(8,128)} %copy.90, f32[12,16,16]{1,2,0:T(8,128)S(1)} %copy.87, f32[12,16,16,64]{3,2,1,0:T(8,128)S(1)} %reshape.160, f32[16,64]{1,0:T(8,128)S(1)} %mul.146, ...), kind=kOutput, calls=%fused_computation.32 | convolution fusion | flops 8014863 | bytes 1829888 | tf_op jit(solution)/shard_map/div | solution.py:53
  19.8 2.8 %fusion.4 = f32[12,16,16]{1,2,0:T(8,128)S(1)} fusion(bf16[12,16,16,64]{3,2,1,0:T(8,128)(2,1)} %reshape_reshape.7, bf16[12,16,16,64]{3,2,1,0:T(8,128)(2,1)} %reshape_reshape.6, f32[12,16,16,16]{2,3,1,0:T(8,128)} %fusion.11), kind=kOutput, calls=%fused_computation.11 | convolution fusion | flops 6927360 | bytes 995328 | tf_op jit(solution)/shard_map/bhij,bjhd->bihd/dot_general | solution.py:55
  24.1 2.2 %fusion.24 = f32[12,16,64,16]{2,3,1,0:T(8,128)} fusion(bf16[12,16,16,16]{2,3,1,0:T(8,128)(2,1)S(1)} %multiply_convert_fusion.2, f32[16,64]{1,0:T(8,128)S(1)} %mul.146, f32[12,16,16]{1,2,0:T(8,128)S(1)} %copy.86, f32[12,16,16]{1,2,0:T(8,128)S(1)} %copy.83, f32[12,16,16,64]{3,2,1,0:T(8,128)S(1)} %reshape.159), kind=kOutput, calls=%fused_computation.72 | convolution fusion | flops 7077888 | bytes 1699840 | tf_op jit(solution)/shard_map/bhij,bihd->bjhd/dot_general | solution.py:69
  27.4 9.4 %fusion.3 = (f32[16,64]{1,0:T(8,128)}, f32[12,16,16]{1,2,0:T(8,128)}, f32[12,16,16]{1,2,0:T(8,128)}, f32[12,16,16]{1,2,0:T(8,128)}, f32[12,16,16]{1,2,0:T(8,128)...) fusion(f32[12]{0:T(128)S(1)} %get-tuple-element.15, f32[12,16,16]{1,2,0:T(8,128)S(1)} %copy.86, ...), kind=kOutput, calls=%fused_computation.9 | convolution fusion | flops 10602496 | bytes 3358768 | tf_op jit(solution)/shard_map/bhij,bjhd->bihd/dot_general | solution.py:68
  39.1 14.3 %all-to-all-start.1 = ((f32[64,2,16]{2,1,0:T(2,128)}), f32[64,2,16]{2,1,0:T(2,128)}, u32[]{:S(2)}, u32[]{:S(2)}) async-start(f32[64,2,16]{2,1,0:T(2,128)} %copy.110), calls=%async_computation.1 | async-start | bytes 131072 | tf_op jit(solution)/shard_map/all_to_all | solution.py:148
  53.5 2.2 %fusion.9 = bf16[12,16,16,64]{3,1,2,0:T(8,128)(2,1)S(1)} fusion(bf16[12,16,16,64]{3,2,1,0:T(8,128)(2,1)} %reshape_reshape.6, f32[12,16,16,16]{2,3,1,0:T(8,128)} %fusion.11), kind=kOutput, calls=%fused_computation.29 | convolution fusion | flops 6537216 | bytes 983040 | tf_op jit(solution)/shard_map/bhij,bihd->bjhd/dot_general | solution.py:59
  56.7 1.8 %reshape.157 = bf16[12,16,1024]{2,1,0:T(8,128)(2,1)S(1)} reshape(bf16[12,16,16,64]{3,2,1,0:T(8,128)(2,1)} %copy.109) | data formatting | bytes 786432 | tf_op jit(solution)/shard_map/reshape | solution.py:76
  58.5 1.6 %copy.105 = f32[12,16,16]{2,1,0:T(8,128)} copy(f32[12,16,16]{1,2,0:T(8,128)} %get-tuple-element.13) | data formatting | bytes 24576 | tf_op jit(solution)/shard_map/reduce_sum | solution.py:32
  60.1 1.5 %broadcast_multiply_fusion = f32[12,16,16]{2,1,0:T(8,128)} fusion(f32[12,16,16]{2,1,0:T(8,128)} %copy.105), kind=kLoop, calls=%fused_computation.43 | loop fusion | flops 3072 | bytes 24576 | tf_op jit(solution)/shard_map/div | solution.py:32
  61.6 1.6 %copy.106 = f32[12,16,16]{1,2,0:T(8,128)} copy(f32[12,16,16]{2,1,0:T(8,128)} %broadcast_multiply_fusion) | data formatting | bytes 24576 | tf_op jit(solution)/shard_map/div | solution.py:32
  63.3 1.6 %copy.103 = f32[12,16,16]{2,1,0:T(8,128)} copy(f32[12,16,16]{1,2,0:T(8,128)} %get-tuple-element.12) | data formatting | bytes 24576 | tf_op jit(solution)/shard_map/reduce_sum | solution.py:31
  64.9 1.5 %broadcast_multiply_fusion.1 = f32[12,16,16]{2,1,0:T(8,128)} fusion(f32[12,16,16]{2,1,0:T(8,128)} %copy.103), kind=kLoop, calls=%fused_computation.44 | loop fusion | flops 3072 | bytes 24576 | tf_op jit(solution)/shard_map/div | solution.py:31
  66.4 1.6 %copy.104 = f32[12,16,16]{1,2,0:T(8,128)} copy(f32[12,16,16]{2,1,0:T(8,128)} %broadcast_multiply_fusion.1) | data formatting | bytes 24576 | tf_op jit(solution)/shard_map/div | solution.py:31
  68.0 3.7 %multiply_convert_fusion = bf16[12,16,16,64]{3,1,2,0:T(8,128)(2,1)S(1)} fusion(f32[12,16,64,16]{2,3,1,0:T(8,128)} %fusion.24, f32[12,16,16]{1,2,0:T(8,128)} %copy.106, f32[12,16,16]{1,2,0:T(8,128)} %copy.104, f32[16,64]{1,0:T(8,128)S(1)} %mul.142, f32[12,16,16]{1,2,0:T(8,128)} %copy.90, f32[12,16,16]{1,2,0:T(8,128)} %copy-done.6, ...), kind=kLoop, calls=%fused_computation.14 | loop fusion | flops 1572864 | bytes 2019328 | tf_op jit(solution)/shard_map/convert_element_type | solution.py:75
  73.9 3.5 %multiply_convert_fusion.1 = bf16[12,16,16,64]{3,1,2,0:T(8,128)(2,1)S(1)} fusion(f32[12,16,64,16]{2,3,1,0:T(8,128)} %get-tuple-element.22, f32[12,16,16]{1,2,0:T(8,128)S(1)} %copy.101, f32[12,16,16]{1,2,0:T(8,128)S(1)} %copy.99, f32[16,64]{1,0:T(8,128)S(1)} %mul.146, f32[12,16,16]{1,2,0:T(8,128)S(1)} %copy-done.8, f32[12,16,16]{1,2,0:T(8,128)S(1)} %copy-done.5, ...), kind=kLoop, calls=%fused_computation.16 | loop fusion | flops 1572864 | bytes 2019328 | tf_op jit(solution)/shard_map/convert_element_type | solution.py:74
  80.3 11.7 %all-to-all-start.2 = ((f32[12,2,16]{2,1,0:T(2,128)}), f32[12,2,16]{2,1,0:T(2,128)S(1)}, u32[]{:S(2)}, u32[]{:S(2)}) async-start(f32[12,2,16]{2,1,0:T(2,128)} %broadcast_in_dim.32), calls=%async_computation.2 | async-start | bytes 24576 | tf_op jit(solution)/shard_map/all_to_all | solution.py:152
  92.0 1.7 %gather_fusion = bf16[12,16,3072]{2,1,0:T(8,128)(2,1)} fusion(bf16[12,16,3072]{2,1,0:T(8,128)(2,1)S(1)} %pad_maximum_fusion, s32[1024]{0:T(1024)S(1)} %pad_clamp_fusion.1), kind=kCustom, calls=%fused_computation | custom fusion | bytes 2359344 | tf_op jit(solution)/shard_map/jit(_take)/gather | solution.py:142
  93.7 8.4 %all-to-all-done.2 = f32[12,2,16]{2,1,0:T(2,128)S(1)} async-done(((f32[12,2,16]{2,1,0:T(2,128)}), f32[12,2,16]{2,1,0:T(2,128)S(1)}, u32[]{:S(2)}, u32[]{:S(2)}) %all-to-all-start.2) | async-done | bytes 1568 | tf_op jit(solution)/shard_map/all_to_all | solution.py:152
  102.1 3.7 %all-to-all-start = ((bf16[12,16,3072]{2,1,0:T(8,128)(2,1)}), bf16[12,16,3072]{2,1,0:T(8,128)(2,1)S(1)}, u32[]{:S(2)}, u32[]{:S(2)}) async-start(bf16[12,16,3072]{2,1,0:T(8,128)(2,1)} %gather_fusion), calls=%async_computation | async-start | bytes 2359296 | tf_op jit(solution)/shard_map/all_to_all | solution.py:143
  107.1 44.3 %all-to-all-done = bf16[12,16,3072]{2,1,0:T(8,128)(2,1)S(1)} async-done(((bf16[12,16,3072]{2,1,0:T(8,128)(2,1)}), bf16[12,16,3072]{2,1,0:T(8,128)(2,1)S(1)}, u32[]{:S(2)}, u32[]{:S(2)}) %all-to-all-start) | async-done | bytes 1179680 | tf_op jit(solution)/shard_map/all_to_all | solution.py:143
  (82 shorter events, 20.3 us)
Async XLA Ops:
  7.5 19.9 %copy-start.6 = (f32[12,16,16]{1,2,0:T(8,128)}, f32[12,16,16]{1,2,0:T(8,128)S(1)}, u32[]{:S(2)}) copy-start(f32[12,16,16]{1,2,0:T(8,128)S(1)} %copy.87) | copy-start | bytes 36868
  11.7 15.8 %copy-start.4 = (f32[12,16,16]{1,2,0:T(8,128)}, f32[12,16,16]{1,2,0:T(8,128)S(1)}, u32[]{:S(2)}) copy-start(f32[12,16,16]{1,2,0:T(8,128)S(1)} %copy.83) | copy-start | bytes 36868
  13.0 14.5 %copy-start.7 = (f32[12,16,16]{1,2,0:T(8,128)}, f32[12,16,16]{1,2,0:T(8,128)S(1)}, u32[]{:S(2)}) copy-start(f32[12,16,16]{1,2,0:T(8,128)S(1)} %copy.86) | copy-start | bytes 36868
  19.8 2.8 %copy-start = (f32[12,16,16,16]{2,3,1,0:T(8,128)S(1)}, f32[12,16,16,16]{2,3,1,0:T(8,128)}, u32[]{:S(2)}) copy-start(f32[12,16,16,16]{2,3,1,0:T(8,128)} %fusion.11) | copy-start | bytes 589828
  19.8 2.8 %copy-start.1 = (bf16[12,16,16,64]{3,2,1,0:T(8,128)(2,1)S(1)}, bf16[12,16,16,64]{3,2,1,0:T(8,128)(2,1)}, u32[]{:S(2)}) copy-start(bf16[12,16,16,64]{3,2,1,0:T(8,128)(2,1)} %reshape_reshape.6) | copy-start | bytes 1179652
  19.8 2.8 %copy-start.2 = (bf16[12,16,16,64]{3,2,1,0:T(8,128)(2,1)S(1)}, bf16[12,16,16,64]{3,2,1,0:T(8,128)(2,1)}, u32[]{:S(2)}) copy-start(bf16[12,16,16,64]{3,2,1,0:T(8,128)(2,1)} %reshape_reshape.7) | copy-start | bytes 1179652
  23.1 0.9 copy-start.3
  24.1 3.4 %copy-start.9 = (f32[12,16,16]{1,2,0:T(8,128)S(1)}, f32[12,16,16]{1,2,0:T(8,128)}, u32[]{:S(2)}) copy-start(f32[12,16,16]{1,2,0:T(8,128)} %copy.90) | copy-start | bytes 36868
  39.1 39.7 %all-to-all-start.1 = ((f32[64,2,16]{2,1,0:T(2,128)}), f32[64,2,16]{2,1,0:T(2,128)}, u32[]{:S(2)}, u32[]{:S(2)}) async-start(f32[64,2,16]{2,1,0:T(2,128)} %copy.110), calls=%async_computation.1 | async-start | bytes 131072 | tf_op jit(solution)/shard_map/all_to_all | solution.py:148
  71.7 0.9 copy-start.10
  72.0 2.0 %copy-start.5 = (f32[12,16,16]{1,2,0:T(8,128)S(1)}, f32[12,16,16]{1,2,0:T(8,128)}, u32[]{:S(2)}) copy-start(f32[12,16,16]{1,2,0:T(8,128)} %copy-done.4) | copy-start | bytes 36868
  72.0 2.0 %copy-start.8 = (f32[12,16,16]{1,2,0:T(8,128)S(1)}, f32[12,16,16]{1,2,0:T(8,128)}, u32[]{:S(2)}) copy-start(f32[12,16,16]{1,2,0:T(8,128)} %copy-done.7) | copy-start | bytes 36868
  77.5 0.8 copy-start.12
  80.3 21.8 %all-to-all-start.2 = ((f32[12,2,16]{2,1,0:T(2,128)}), f32[12,2,16]{2,1,0:T(2,128)S(1)}, u32[]{:S(2)}, u32[]{:S(2)}) async-start(f32[12,2,16]{2,1,0:T(2,128)} %broadcast_in_dim.32), calls=%async_computation.2 | async-start | bytes 24576 | tf_op jit(solution)/shard_map/all_to_all | solution.py:152
  93.7 12.2 %copy-start.11 = (s32[1,12,12]{2,0,1:T(1,128)S(1)}, s32[1,12,12]{2,0,1:T(1,128)}, u32[]{:S(2)}) copy-start(s32[1,12,12]{2,0,1:T(1,128)} %param.12) | copy-start | bytes 1732
  102.1 49.3 %all-to-all-start = ((bf16[12,16,3072]{2,1,0:T(8,128)(2,1)}), bf16[12,16,3072]{2,1,0:T(8,128)(2,1)S(1)}, u32[]{:S(2)}, u32[]{:S(2)}) async-start(bf16[12,16,3072]{2,1,0:T(8,128)(2,1)} %gather_fusion), calls=%async_computation | async-start | bytes 2359296 | tf_op jit(solution)/shard_map/all_to_all | solution.py:143

commit v2 on v1

--- a/solution.py
+++ b/solution.py
@@ -138,19 +138,22 @@
         gains,
         live_flags,
     )
-    grads = jnp.concatenate((d_query, d_key, d_value), axis=-1)
-    packed = jnp.take(grads, slot_source, axis=0, mode="clip")
-    received = lax.all_to_all(packed, "enc", split_axis=0, concat_axis=0, tiled=True)
-    mine = from_slots(received, arrival_order)
     cols = feat // grp_count
     by_grp = jnp.transpose(gain_terms.reshape(2, grp_count, cols), (1, 0, 2))
     grp_sum = jnp.sum(
         lax.all_to_all(by_grp, "grp", split_axis=0, concat_axis=0, tiled=True), axis=0
     )
-    by_enc = jnp.broadcast_to(grp_sum[None], (enc_count, 2, cols))
-    shares = jnp.sum(
-        lax.all_to_all(by_enc, "enc", split_axis=0, concat_axis=0, tiled=True), axis=0
-    )
+    grp_hi = grp_sum.astype(jnp.bfloat16)
+    grp_lo = (grp_sum - grp_hi.astype(jnp.float32)).astype(jnp.bfloat16)
+    extra = jnp.concatenate((grp_hi, grp_lo), axis=0)
+    extra = jnp.pad(extra, ((0, PIECE - 4), (0, 128 - cols)))
+    extra = jnp.broadcast_to(extra[None], (PMAX, PIECE, 128))
+    grads = jnp.concatenate((d_query, d_key, d_value, extra), axis=-1)
+    packed = jnp.take(grads, slot_source, axis=0, mode="clip")
+    received = lax.all_to_all(packed, "enc", split_axis=0, concat_axis=0, tiled=True)
+    mine = from_slots(received[:, :, : 3 * feat], arrival_order)
+    parts = received[:, 0:4, 3 * feat : 3 * feat + cols].astype(jnp.float32)
+    shares = jnp.sum(parts[:, 0:2] + parts[:, 2:4], axis=0)
     total_live = enc_count * grp_count * P_OWN * PIECE
     gain_grad = shares / math.sqrt(total_live)
     own_rows = P_OWN * PIECE

time: 154 us -> 145 us (0.942)
  the two profiles are of different devices: /device:TPU:2 before, /device:TPU:66 now
where the time goes in v2:
time: 145 us; the launch traced here: 144 us
  waiting for transfers between devices  46.3 us (32%)
  local copies, waits for them, and re-layouts  29.6 us (20%)
  starting transfers between devices  25.8 us (18%)
  matrix products  22.3 us (15%)
  other arithmetic  18.7 us (13%)
    all_to_all x1, waiting for transfers between devices, local(): lax.all_to_all(packed, 'enc', split_axis=0, concat_axis=0, tiled=True)  46.3 us
    all_to_all x1, starting transfers between devices, local(): lax.all_to_all(packed, 'enc', split_axis=0, concat_axis=0, tiled=True)  14.9 us
    all_to_all x1, starting transfers between devices, local(): lax.all_to_all(by_grp, 'grp', split_axis=0, concat_axis=0, tiled=True)  10.9 us
    dot_general x1, matrix products, piece_grads(): jnp.einsum('bhij,bjhd->bihd', d_score, k_hat, preferred_element_type=jnp....  9.46 us
    convert_element_type x1, other arithmetic, piece_grads(): d_key.reshape(flat_shape).astype(jnp.bfloat16)  4.56 us
    div x1, matrix products, piece_grads(): probs = weights / jnp.sum(weights, -1, keepdims=True)  4.29 us
    div x2, local copies, waits for them, and re-layouts, norm_back(): jnp.mean(d_norm, -1, keepdims=True)  3.24 us
    dot_general x1, matrix products, piece_grads(): jnp.einsum('bhij,bihd->bjhd', probs_b, cot_four, preferred_element_type=j...  3.1 us
  transfers between devices with their start and end apart: 2, of which 1 were waited for; matrix products, arithmetic and copies ran while one was open for 18% of the time, Pallas kernels for 0%

profile of v2, /device:TPU:66, one launch (start us, length us, event | category | flops | bytes accessed | tf_op | source)
XLA Modules:
  0.0 143.8 jit_solution(1602545199751763186)
XLA Ops:
  3.1 2.4 %reshape_reshape.6 = bf16[12,16,16,64]{3,2,1,0:T(8,128)(2,1)} reshape(bf16[192,1024]{1,0:T(8,128)(2,1)} %param.10) | data formatting | bytes 786432 | tf_op jit(solution)/shard_map/reshape;reshape | solution.py:46
  5.5 2.4 %reshape_reshape.7 = bf16[12,16,16,64]{3,2,1,0:T(8,128)(2,1)} reshape(bf16[192,1024]{1,0:T(8,128)(2,1)} %param.9) | data formatting | bytes 786432 | tf_op jit(solution)/shard_map/reshape;reshape | solution.py:45
  8.9 1.1 multiply_reduce_fusion.3
  10.2 1.6 %reshape.160 = f32[12,16,16,64]{3,2,1,0:T(8,128)S(1)} reshape(bf16[192,1024]{1,0:T(8,128)(2,1)} %param.8) | data formatting | bytes 1179648 | tf_op jit(solution)/shard_map/convert_element_type | solution.py:20
  12.3 1.7 %multiply_reduce_fusion.2 = f32[12,16,16]{1,2,0:T(8,128)} fusion(f32[12,16,16,64]{3,2,1,0:T(8,128)S(1)} %reshape.160, f32[12,16,16]{1,2,0:T(8,128)S(1)} %copy.87), kind=kLoop, calls=%fused_computation.22 | loop fusion | flops 586752 | bytes 811008 | tf_op jit(solution)/shard_map/reduce_sum | solution.py:22
  14.1 1.0 copy.89
  15.7 1.0 copy.90
  16.7 4.3 %fusion.11 = f32[12,16,16,16]{2,3,1,0:T(8,128)} fusion(pred[12,16,16]{1,2,0:T(8,128)(4,1)} %broadcast_compare_fusion, f32[16,64]{1,0:T(8,128)S(1)} %mul.142, f32[12,16,16]{1,2,0:T(8,128)S(1)} %copy.90, f32[12,16,16]{1,2,0:T(8,128)S(1)} %copy.87, f32[12,16,16,64]{3,2,1,0:T(8,128)S(1)} %reshape.160, f32[16,64]{1,0:T(8,128)S(1)} %mul.146, ...), kind=kOutput, calls=%fused_computation.32 | convolution fusion | flops 8014863 | bytes 1829888 | tf_op jit(solution)/shard_map/div | solution.py:53
  21.0 2.7 %fusion.4 = f32[12,16,16]{1,2,0:T(8,128)S(1)} fusion(bf16[12,16,16,64]{3,2,1,0:T(8,128)(2,1)} %reshape_reshape.7, bf16[12,16,16,64]{3,2,1,0:T(8,128)(2,1)} %reshape_reshape.6, f32[12,16,16,16]{2,3,1,0:T(8,128)} %fusion.11), kind=kOutput, calls=%fused_computation.11 | convolution fusion | flops 6927360 | bytes 995328 | tf_op jit(solution)/shard_map/bhij,bjhd->bihd/dot_general | solution.py:55
  25.3 2.2 %fusion.31 = f32[12,16,64,16]{2,3,1,0:T(8,128)} fusion(bf16[12,16,16,16]{2,3,1,0:T(8,128)(2,1)S(1)} %multiply_convert_fusion.2, f32[16,64]{1,0:T(8,128)S(1)} %mul.146, f32[12,16,16]{1,2,0:T(8,128)S(1)} %copy.86, f32[12,16,16]{1,2,0:T(8,128)S(1)} %copy.83, f32[12,16,16,64]{3,2,1,0:T(8,128)S(1)} %reshape.159), kind=kOutput, calls=%fused_computation.84 | convolution fusion | flops 7077888 | bytes 1699840 | tf_op jit(solution)/shard_map/bhij,bihd->bjhd/dot_general | solution.py:69
  27.5 1.2 compare_convert_fusion.2
  28.6 9.5 %multiply_reduce_fusion.1 = (f32[12,16,16]{1,2,0:T(8,128)}, f32[16,64]{1,0:T(8,128)}, f32[12,16,16]{1,2,0:T(8,128)}, f32[12,16,16]{1,2,0:T(8,128)}, f32[16,64]{1...) fusion(f32[16,64]{1,0:T(8,128)S(1)} %mul.146, f32[12,16,16]{1,2,0:T(8,128)S(1)} %copy.86, ...), kind=kOutput, calls=%fused_computation.17 | convolution fusion | flops 10602496 | bytes 3358768 | tf_op jit(solution)/shard_map/bhij,bjhd->bihd/dot_general | solution.py:68
  40.3 10.9 %all-to-all-start = ((f32[64,2,16]{2,1,0:T(2,128)}), f32[64,2,16]{2,1,0:T(2,128)}, u32[]{:S(2)}, u32[]{:S(2)}) async-start(f32[64,2,16]{2,1,0:T(2,128)} %copy.110), calls=%async_computation | async-start | bytes 131072 | tf_op jit(solution)/shard_map/all_to_all | solution.py:144
  51.2 3.1 %fusion.9 = bf16[12,16,16,64]{3,1,2,0:T(8,128)(2,1)} fusion(bf16[12,16,16,64]{3,2,1,0:T(8,128)(2,1)} %reshape_reshape.6, f32[12,16,16,16]{2,3,1,0:T(8,128)} %fusion.11), kind=kOutput, calls=%fused_computation.29 | convolution fusion | flops 6537216 | bytes 983040 | tf_op jit(solution)/shard_map/bhij,bihd->bjhd/dot_general | solution.py:59
  55.2 1.0 copy.100
  56.9 1.6 %copy.101 = f32[12,16,16]{1,2,0:T(8,128)} copy(f32[12,16,16]{2,1,0:T(8,128)} %broadcast_multiply_fusion.2) | data formatting | bytes 24576 | tf_op jit(solution)/shard_map/div | solution.py:32
  60.1 1.6 %copy.99 = f32[12,16,16]{1,2,0:T(8,128)} copy(f32[12,16,16]{2,1,0:T(8,128)} %broadcast_multiply_fusion.3) | data formatting | bytes 24576 | tf_op jit(solution)/shard_map/div | solution.py:31
  61.7 1.0 copy.103
  63.3 1.6 %copy.104 = f32[12,16,16]{1,2,0:T(8,128)} copy(f32[12,16,16]{2,1,0:T(8,128)} %broadcast_multiply_fusion.1) | data formatting | bytes 24576 | tf_op jit(solution)/shard_map/div | solution.py:31
  67.6 4.6 %multiply_convert_fusion = bf16[12,16,16,64]{3,1,2,0:T(8,128)(2,1)} fusion(f32[12,16,64,16]{2,3,1,0:T(8,128)} %fusion.31, f32[12,16,16]{1,2,0:T(8,128)S(1)} %copy.106, f32[12,16,16]{1,2,0:T(8,128)} %copy.104, f32[16,64]{1,0:T(8,128)S(1)} %mul.142, f32[12,16,16]{1,2,0:T(8,128)} %copy-done.8, f32[12,16,16]{1,2,0:T(8,128)S(1)} %copy.87, ...), kind=kLoop, calls=%fused_computation.14 | loop fusion | flops 1572864 | bytes 2019328 | tf_op jit(solution)/shard_map/convert_element_type | solution.py:75
  72.2 2.0 %multiply_convert_fusion.1 = bf16[12,16,16,64]{3,1,2,0:T(8,128)(2,1)S(1)} fusion(f32[12,16,64,16]{2,3,1,0:T(8,128)S(1)} %copy-done.6, f32[12,16,16]{1,2,0:T(8,128)S(1)} %copy-done.9, f32[12,16,16]{1,2,0:T(8,128)S(1)} %copy-done.10, f32[16,64]{1,0:T(8,128)S(1)} %mul.146, f32[12,16,16]{1,2,0:T(8,128)S(1)} %copy.86, f32[12,16,16]{1,2,0:T(8,128)S(1)} %copy.83, ...), kind=kLoop, calls=%fused_computation.16 | loop fusion | flops 1572864 | bytes 2019328 | tf_op jit(solution)/shard_map/convert_element_type | solution.py:74
  77.9 1.7 %gather_fusion = bf16[12,16,3200]{2,1,0:T(8,128)(2,1)} fusion(bf16[12,16,3200]{2,1,0:T(8,128)(2,1)S(1)} %pad_maximum_fusion, s32[1024]{0:T(1024)S(1)} %pad_clamp_fusion.1), kind=kCustom, calls=%fused_computation | custom fusion | bytes 2457648 | tf_op jit(solution)/shard_map/jit(_take)/gather | solution.py:152
  79.7 14.9 %all-to-all-start.1 = ((bf16[12,16,3200]{2,1,0:T(8,128)(2,1)}), bf16[12,16,3200]{2,1,0:T(8,128)(2,1)S(1)}, u32[]{:S(2)}, u32[]{:S(2)}) async-start(bf16[12,16,3200]{2,1,0:T(8,128)(2,1)} %gather_fusion), calls=%async_computation.1 | async-start | bytes 2457600 | tf_op jit(solution)/shard_map/all_to_all | solution.py:153
  95.2 46.3 %all-to-all-done.1 = bf16[12,16,3200]{2,1,0:T(8,128)(2,1)S(1)} async-done(((bf16[12,16,3200]{2,1,0:T(8,128)(2,1)}), bf16[12,16,3200]{2,1,0:T(8,128)(2,1)S(1)}, u32[]{:S(2)}, u32[]{:S(2)}) %all-to-all-start.1) | async-done | bytes 1228832 | tf_op jit(solution)/shard_map/all_to_all | solution.py:153
  (86 shorter events, 21.6 us)
Async XLA Ops:
  0.6 7.2 %copy-start.7 = (bf16[192,1024]{1,0:T(8,128)(2,1)S(1)}, bf16[192,1024]{1,0:T(8,128)(2,1)}, u32[]{:S(2)}) copy-start(bf16[192,1024]{1,0:T(8,128)(2,1)} %param.7) | copy-start | bytes 1179652
  16.7 11.9 %copy-start.8 = (f32[12,16,16]{1,2,0:T(8,128)}, f32[12,16,16]{1,2,0:T(8,128)S(1)}, u32[]{:S(2)}) copy-start(f32[12,16,16]{1,2,0:T(8,128)S(1)} %copy.90) | copy-start | bytes 36868
  21.0 2.8 %copy-start = (f32[12,16,16,16]{2,3,1,0:T(8,128)S(1)}, f32[12,16,16,16]{2,3,1,0:T(8,128)}, u32[]{:S(2)}) copy-start(f32[12,16,16,16]{2,3,1,0:T(8,128)} %fusion.11) | copy-start | bytes 589828
  21.0 2.8 %copy-start.1 = (bf16[12,16,16,64]{3,2,1,0:T(8,128)(2,1)S(1)}, bf16[12,16,16,64]{3,2,1,0:T(8,128)(2,1)}, u32[]{:S(2)}) copy-start(bf16[12,16,16,64]{3,2,1,0:T(8,128)(2,1)} %reshape_reshape.6) | copy-start | bytes 1179652
  21.0 2.8 %copy-start.2 = (bf16[12,16,16,64]{3,2,1,0:T(8,128)(2,1)S(1)}, bf16[12,16,16,64]{3,2,1,0:T(8,128)(2,1)}, u32[]{:S(2)}) copy-start(bf16[12,16,16,64]{3,2,1,0:T(8,128)(2,1)} %reshape_reshape.7) | copy-start | bytes 1179652
  24.3 0.9 copy-start.5
  40.3 36.6 %all-to-all-start = ((f32[64,2,16]{2,1,0:T(2,128)}), f32[64,2,16]{2,1,0:T(2,128)}, u32[]{:S(2)}, u32[]{:S(2)}) async-start(f32[64,2,16]{2,1,0:T(2,128)} %copy.110), calls=%async_computation | async-start | bytes 131072 | tf_op jit(solution)/shard_map/all_to_all | solution.py:144
  51.2 3.1 %copy-start.12 = (s32[12]{0:T(128)S(1)}, s32[12]{0:T(128)}, u32[]{:S(2)}) copy-start(s32[12]{0:T(128)} %get-tuple-element.15) | copy-start | bytes 148
  67.6 4.6 %copy-start.6 = (f32[12,16,64,16]{2,3,1,0:T(8,128)S(1)}, f32[12,16,64,16]{2,3,1,0:T(8,128)}, u32[]{:S(2)}) copy-start(f32[12,16,64,16]{2,3,1,0:T(8,128)} %get-tuple-element.24) | copy-start | bytes 2359300
  67.6 4.6 %copy-start.9 = (f32[12,16,16]{1,2,0:T(8,128)S(1)}, f32[12,16,16]{1,2,0:T(8,128)}, u32[]{:S(2)}) copy-start(f32[12,16,16]{1,2,0:T(8,128)} %copy.101) | copy-start | bytes 36868
  67.6 4.6 %copy-start.10 = (f32[12,16,16]{1,2,0:T(8,128)S(1)}, f32[12,16,16]{1,2,0:T(8,128)}, u32[]{:S(2)}) copy-start(f32[12,16,16]{1,2,0:T(8,128)} %copy.99) | copy-start | bytes 36868
  72.2 2.0 %copy-start.13 = (s32[12]{0:T(128)S(1)}, s32[12]{0:T(128)}, u32[]{:S(2)}) copy-start(s32[12]{0:T(128)} %select_reduce_fusion) | copy-start | bytes 148
  72.2 2.0 %copy-start.3 = (bf16[12,16,16,64]{3,1,2,0:T(8,128)(2,1)S(1)}, bf16[12,16,16,64]{3,1,2,0:T(8,128)(2,1)}, u32[]{:S(2)}) copy-start(bf16[12,16,16,64]{3,1,2,0:T(8,128)(2,1)} %fusion.9) | copy-start | bytes 1179652
  75.0 1.1 copy-start.4
  79.7 14.9 %copy-start.11 = (s32[1,12,12]{2,0,1:T(1,128)S(1)}, s32[1,12,12]{2,0,1:T(1,128)}, u32[]{:S(2)}) copy-start(s32[1,12,12]{2,0,1:T(1,128)} %param.12) | copy-start | bytes 1732
  79.7 61.9 %all-to-all-start.1 = ((bf16[12,16,3200]{2,1,0:T(8,128)(2,1)}), bf16[12,16,3200]{2,1,0:T(8,128)(2,1)S(1)}, u32[]{:S(2)}, u32[]{:S(2)}) async-start(bf16[12,16,3200]{2,1,0:T(8,128)(2,1)} %gather_fusion), calls=%async_computation.1 | async-start | bytes 2457600 | tf_op jit(solution)/shard_map/all_to_all | solution.py:153

commit v3 on v2

--- a/solution.py
+++ b/solution.py
@@ -78,6 +78,61 @@
     )
 
 
+def normalize_rows(rows, gain_row):
+    values = rows.astype(jnp.float32).reshape(rows.shape[0], HEADS, HD)
+    centred = values - jnp.mean(values, -1, keepdims=True)
+    inv_scale = lax.rsqrt(jnp.mean(centred * centred, -1, keepdims=True) + epsilon)
+    normed = centred * inv_scale
+    return (normed, inv_scale, (normed * gain_row).astype(jnp.bfloat16))
+
+
+def row_norm_back(d_hat, normed, inv_scale, gain_row, live_rows):
+    d_norm = d_hat * gain_row
+    d_input = inv_scale * (
+        d_norm
+        - jnp.mean(d_norm, -1, keepdims=True)
+        - normed * jnp.mean(d_norm * normed, -1, keepdims=True)
+    )
+    gain_term = jnp.sum(d_hat * normed * live_rows[:, None, None], 0)
+    return (d_input, gain_term.reshape(-1))
+
+
+def block_grads(query_rows, key_rows, value_rows, cotangent, piece_of, image_num, gains, live_rows):
+    rows = query_rows.shape[0]
+    three = (rows, HEADS, HD)
+    gain_query = gains[0].reshape(HEADS, HD)
+    gain_key = gains[1].reshape(HEADS, HD)
+    q_norm, q_scale, q_hat = normalize_rows(query_rows, gain_query)
+    k_norm, k_scale, k_hat = normalize_rows(key_rows, gain_key)
+    values = value_rows.reshape(three)
+    cot = cotangent.reshape(three)
+    factor = HD ** (-0.5)
+    f32 = jnp.float32
+    scores = jnp.einsum("ihd,jhd->hij", q_hat, k_hat, preferred_element_type=f32) * factor
+    same = (piece_of[:, None] == piece_of[None, :]) & (image_num[:, None] == image_num[None, :])
+    weights = jnp.where(same[None], jnp.exp(scores), 0.0)
+    probs = weights / jnp.sum(weights, -1, keepdims=True)
+    probs_b = probs.astype(jnp.bfloat16)
+    attended = jnp.einsum("hij,jhd->ihd", probs_b, values, preferred_element_type=f32)
+    row_delta = jnp.sum(cot.astype(f32) * attended, -1)
+    d_value = jnp.einsum("hij,ihd->jhd", probs_b, cot, preferred_element_type=f32)
+    d_prob = jnp.einsum("ihd,jhd->hij", cot, values, preferred_element_type=f32)
+    d_score = (probs * (d_prob - jnp.transpose(row_delta)[..., None]) * factor).astype(
+        jnp.bfloat16
+    )
+    d_qhat = jnp.einsum("hij,jhd->ihd", d_score, k_hat, preferred_element_type=f32)
+    d_khat = jnp.einsum("hij,ihd->jhd", d_score, q_hat, preferred_element_type=f32)
+    d_query, term_query = row_norm_back(d_qhat, q_norm, q_scale, gain_query, live_rows)
+    d_key, term_key = row_norm_back(d_khat, k_norm, k_scale, gain_key, live_rows)
+    flat = (rows, HEADS * HD)
+    return (
+        d_query.reshape(flat).astype(jnp.bfloat16),
+        d_key.reshape(flat).astype(jnp.bfloat16),
+        d_value.reshape(flat).astype(jnp.bfloat16),
+        jnp.stack([term_query, term_key]),
+    )
+
+
 def send_slots(own_plan, enc_count, per_slot):
     owner_hit = (own_plan[:, None] == jnp.arange(enc_count, dtype=jnp.int32)[None, :]).astype(
         jnp.int32
@@ -129,22 +184,22 @@
     arrival_order = receive_order(group_plan, enc_rank, enc_count, per_slot)
     piece_shape = (PMAX, PIECE, feat)
     live_flags = (own_plan >= 0).astype(jnp.float32)
-    d_query, d_key, d_value, gain_terms = piece_grads(
-        query_raw.reshape(piece_shape),
-        key_raw.reshape(piece_shape),
-        value_rows.reshape(piece_shape),
-        out_cotangent.reshape(piece_shape),
-        image_ids.reshape(PMAX, PIECE),
-        gains,
-        live_flags,
-    )
+    live_rows = jnp.repeat(live_flags, PIECE)
+    piece_of = jnp.repeat(jnp.arange(PMAX, dtype=jnp.int32), PIECE)
+    d_query, d_key, d_value, gain_terms = block_grads(
+        query_raw, key_raw, value_rows, out_cotangent, piece_of, image_ids, gains, live_rows
+    )
+    d_query = d_query.reshape(piece_shape)
+    d_key = d_key.reshape(piece_shape)
+    d_value = d_value.reshape(piece_shape)
     cols = feat // grp_count
     by_grp = jnp.transpose(gain_terms.reshape(2, grp_count, cols), (1, 0, 2))
     grp_sum = jnp.sum(
         lax.all_to_all(by_grp, "grp", split_axis=0, concat_axis=0, tiled=True), axis=0
     )
-    grp_hi = grp_sum.astype(jnp.bfloat16)
-    grp_lo = (grp_sum - grp_hi.astype(jnp.float32)).astype(jnp.bfloat16)
+    grp_top = lax.reduce_precision(grp_sum, exponent_bits=8, mantissa_bits=7)
+    grp_hi = grp_top.astype(jnp.bfloat16)
+    grp_lo = (grp_sum - grp_top).astype(jnp.bfloat16)
     extra = jnp.concatenate((grp_hi, grp_lo), axis=0)
     extra = jnp.pad(extra, ((0, PIECE - 4), (0, 128 - cols)))
     extra = jnp.broadcast_to(extra[None], (PMAX, PIECE, 128))

time: 145 us -> 104 us (0.72)
  other arithmetic: 18.7 us -> 5.07 us
  local copies, waits for them, and re-layouts: 29.6 us -> 16.1 us
  matrix products: 22.3 us -> 9.75 us
    dot_general x5 -> x6, matrix products: 18.1 us -> 9.75 us  [the longest x1 3.74 us: block_grads(): jnp.einsum('hij,ihd->jhd', probs_b, cot, preferred_element_type=f32)]
    another operation x4 -> x2, local copies, waits for them, and re-layouts: 6.3 us -> 0.14 us  [block_grads(): jnp.stack([term_query, term_key])]
    div x6 -> x0, local copies, waits for them, and re-layouts: 5.97 us -> none  [the longest x2 3.24 us: norm_back(): jnp.mean(d_norm, -1, keepdims=True)]
    convert_element_type x3, other arithmetic: 6.57 us -> 1.53 us  [the longest x1 1.16 us: block_grads(): d_key.reshape(flat).astype(jnp.bfloat16)]
    reduce_sum x6 -> x0, local copies, waits for them, and re-layouts: 4.93 us -> none  [the longest x2 1.94 us: norm_back(): jnp.mean(d_norm, -1, keepdims=True)]
    div x1 -> x0, matrix products: 4.29 us -> none  [piece_grads(): probs = weights / jnp.sum(weights, -1, keepdims=True)]
    unnamed x28 -> x22, local copies, waits for them, and re-layouts: 1.36 us -> 4.77 us
    reduce_sum x4, other arithmetic: 3.77 us -> 0.5 us  [the longest x2 0.3 us: normalize_rows(): jnp.mean(centred * centred, -1, keepdims=True) + epsilon]
  transfers between devices with their start and end apart: 2 -> 2, of which waited for: 1 -> 1; matrix products, arithmetic and copies ran while one was open for 18% -> 11% of each run, Pallas kernels for 0% -> 0%
where the time goes in v3:
time: 104 us
  waiting for transfers between devices  46.3 us (45%)
  starting transfers between devices  25.4 us (24%)
  local copies, waits for them, and re-layouts  16.1 us (15%)
  matrix products  9.75 us (9%)
  other arithmetic  5.07 us (5%)
    all_to_all x1, waiting for transfers between devices, local(): lax.all_to_all(packed, 'enc', split_axis=0, concat_axis=0, tiled=True)  46.3 us
    all_to_all x1, starting transfers between devices, local(): lax.all_to_all(packed, 'enc', split_axis=0, concat_axis=0, tiled=True)  14.8 us
    all_to_all x1, starting transfers between devices, local(): lax.all_to_all(by_grp, 'grp', split_axis=0, concat_axis=0, tiled=True)  10.7 us
    unnamed x22, local copies, waits for them, and re-layouts  4.77 us
    dot_general x1, matrix products, block_grads(): jnp.einsum('hij,ihd->jhd', probs_b, cot, preferred_element_type=f32)  3.74 us
    convert_element_type x2, local copies, waits for them, and re-layouts, block_grads(): d_value.reshape(flat).astype(jnp.bfloat16)  2.22 us
  transfers between devices with their start and end apart: 2, of which 1 were waited for; matrix products, arithmetic and copies ran while one was open for 11% of the time, Pallas kernels for 0%

profile of v3, /device:TPU:66, one launch (start us, length us, event | category | flops | bytes accessed | tf_op | source)
XLA Modules:
  0.0 103.7 jit_solution(4289490903864009011)
XLA Ops:
  0.6 0.7 compare_convert_fusion.2
  1.6 0.8 slice_reduce_fusion
  2.5 2.0 %copy.52 = bf16[192,1024]{0,1:T(8,128)(2,1)} copy(bf16[192,1024]{1,0:T(8,128)(2,1)} %param.9) | data formatting | bytes 786432 | tf_op args[2]
  4.5 2.0 %copy.51 = bf16[192,1024]{0,1:T(8,128)(2,1)} copy(bf16[192,1024]{1,0:T(8,128)(2,1)} %param.10) | data formatting | bytes 786432 | tf_op args[3]
  6.5 1.2 %copy.49 = f32[192,1024]{0,1:T(8,128)S(1)} copy(bf16[192,1024]{1,0:T(8,128)(2,1)} %param.7) | data formatting | bytes 1179648 | tf_op jit(solution)/shard_map/reshape | solution.py:82
  9.1 1.2 %fusion.1 = (f32[16,192]{1,0:T(8,128)S(1)}, f32[16,192,192]{1,2,0:T(8,128)S(1)}) fusion(pred[192,192]{0,1:T(8,128)(4,1)S(1)} %compare_and_fusion, f32[192,16,64]{0,2,1:T(8,128)S(1)} %get-tuple-element.28, f32[16,64]{1,0:T(8,128)S(1)} %mul.144, f32[192,16,64]{0,2,1:T(8,128)S(1)} %get-tuple-element.27, f32[16,64]{1,0:T(8,128)S(1)} %mul.148), kind=kOutput, calls=%fused_computation.5 | convolution fusion | flops 78050304 | bytes 3989504 | tf_op jit(solution)/shard_map/ihd,jhd->hij/dot_general | solution.py:111
  10.6 0.9 fusion.3
  11.9 1.2 %multiply_convert_fusion = bf16[16,192,192]{1,2,0:T(8,128)(2,1)S(1)} fusion(bf16[192,16,64]{0,2,1:T(8,128)(2,1)S(1)} %bitcast.48, bf16[192,16,64]{0,2,1:T(8,128)(2,1)S(1)} %bitcast.50, f32[16,192]{1,0:T(8,128)S(1)} %bitcast.51, f32[16,192]{1,0:T(8,128)S(1)} %get-tuple-element.24, f32[16,192,192]{1,2,0:T(8,128)S(1)} %get-tuple-element.25, ...), kind=kOutput, calls=%fused_computation.2 | convolution fusion | flops 79626240 | bytes 4386816 | tf_op jit(solution)/shard_map/ihd,jhd->hij/dot_general | solution.py:119
  13.1 0.7 convolution_bitcast_fusion.1
  13.8 2.1 %multiply_reduce_fusion.3 = (f32[192,16]{0,1:T(8,128)S(1)}, f32[16,64]{1,0:T(8,128)S(1)}, f32[192,16]{0,1:T(8,128)S(1)}, f32[192,16]{0,1:T(8,128)S(1)}, f32[16,6...) fusion(f32[192,16,64]{0,2,1:T(8,128)S(1)} %get-tuple-element.27, f32[16,64]{1,0:T(8,128)S(1)} %mul.148, ...), kind=kOutput, calls=%fused_computation.23 | convolution fusion | flops 78628864 | bytes 4391680 | tf_op jit(solution)/shard_map/hij,jhd->ihd/dot_general | solution.py:123
  16.0 0.7 copy.61
  16.7 10.7 %all-to-all-start = ((f32[64,2,16]{2,1,0:T(2,128)}), f32[64,2,16]{2,1,0:T(2,128)S(1)}, u32[]{:S(2)}, u32[]{:S(2)}) async-start(f32[64,2,16]{2,1,0:T(2,128)} %copy.61), calls=%async_computation | async-start | bytes 131072 | tf_op jit(solution)/shard_map/all_to_all | solution.py:198
  27.4 3.7 %fusion.4 = bf16[192,16,64]{0,2,1:T(8,128)(2,1)} fusion(bf16[192,16,64]{0,2,1:T(8,128)(2,1)} %bitcast.46, f32[16,192,192]{1,2,0:T(8,128)} %copy-done.3, f32[16,192]{1,0:T(8,128)S(1)} %get-tuple-element.24, pred[192,192]{0,1:T(8,128)(4,1)S(1)} %compare_and_fusion), kind=kOutput, calls=%fused_computation.12 | convolution fusion | flops 78053376 | bytes 3194880 | tf_op jit(solution)/shard_map/hij,ihd->jhd/dot_general | solution.py:118
  31.6 1.2 %multiply_convert_fusion.1 = bf16[192,16,64]{0,2,1:T(8,128)(2,1)} fusion(f32[192,16,64]{0,2,1:T(8,128)S(1)} %copy-done.1, f32[192,16,64]{0,2,1:T(8,128)S(1)} %convolution_bitcast_fusion.1, f32[192,16]{0,1:T(8,128)S(1)} %broadcast_multiply_fusion, f32[192,16]{0,1:T(8,128)S(1)} %broadcast_multiply_fusion.1, f32[16,64]{1,0:T(8,128)S(1)} %mul.144, ...), kind=kLoop, calls=%fused_computation.20 | loop fusion | flops 1179648 | bytes 2007040 | tf_op jit(solution)/shard_map/convert_element_type | solution.py:130
  33.1 1.7 %copy.60 = bf16[192,16,64]{2,1,0:T(8,128)(2,1)S(1)} copy(bf16[192,16,64]{0,2,1:T(8,128)(2,1)} %fusion.4) | data formatting | bytes 786432 | tf_op jit(solution)/shard_map/convert_element_type | solution.py:131
  34.8 0.5 convert_element_type.96
  35.4 0.6 copy.58
  36.5 0.6 copy.56
  38.0 1.7 %gather_fusion = bf16[12,16,3200]{2,1,0:T(8,128)(2,1)} fusion(bf16[12,16,3200]{2,1,0:T(8,128)(2,1)S(1)} %pad_maximum_fusion, s32[1024]{0:T(1024)S(1)} %pad_clamp_fusion.1), kind=kCustom, calls=%fused_computation | custom fusion | bytes 2457648 | tf_op jit(solution)/shard_map/jit(_take)/gather | solution.py:207
  39.7 14.8 %all-to-all-start.1 = ((bf16[12,16,3200]{2,1,0:T(8,128)(2,1)}), bf16[12,16,3200]{2,1,0:T(8,128)(2,1)S(1)}, u32[]{:S(2)}, u32[]{:S(2)}) async-start(bf16[12,16,3200]{2,1,0:T(8,128)(2,1)} %gather_fusion), calls=%async_computation.1 | async-start | bytes 2457600 | tf_op jit(solution)/shard_map/all_to_all | solution.py:208
  55.2 46.3 %all-to-all-done.1 = bf16[12,16,3200]{2,1,0:T(8,128)(2,1)S(1)} async-done(((bf16[12,16,3200]{2,1,0:T(8,128)(2,1)}), bf16[12,16,3200]{2,1,0:T(8,128)(2,1)S(1)}, u32[]{:S(2)}, u32[]{:S(2)}) %all-to-all-start.1) | async-done | bytes 1228832 | tf_op jit(solution)/shard_map/all_to_all | solution.py:208
  101.5 0.6 broadcast_multiply_fusion.6
  102.2 0.6 gather_fusion.1
  102.8 0.9 fusion.25
  (68 shorter events, 5.3 us)
Async XLA Ops:
  0.6 7.4 %copy-start.7 = (bf16[192,1024]{1,0:T(8,128)(2,1)S(1)}, bf16[192,1024]{1,0:T(8,128)(2,1)}, u32[]{:S(2)}) copy-start(bf16[192,1024]{1,0:T(8,128)(2,1)} %param.8) | copy-start | bytes 1179652
  7.8 0.8 copy-start.9
  9.0 4.7 %copy-start = (f32[192,16,64]{0,2,1:T(8,128)}, f32[192,16,64]{0,2,1:T(8,128)S(1)}, u32[]{:S(2)}) copy-start(f32[192,16,64]{0,2,1:T(8,128)S(1)} %get-tuple-element.28) | copy-start | bytes 2359300
  9.1 1.4 %copy-start.5 = (bf16[192,1024]{0,1:T(8,128)(2,1)S(1)}, bf16[192,1024]{0,1:T(8,128)(2,1)}, u32[]{:S(2)}) copy-start(bf16[192,1024]{0,1:T(8,128)(2,1)} %copy.51) | copy-start | bytes 1179652
  9.1 1.6 %copy-start.6 = (bf16[192,1024]{0,1:T(8,128)(2,1)S(1)}, bf16[192,1024]{0,1:T(8,128)(2,1)}, u32[]{:S(2)}) copy-start(bf16[192,1024]{0,1:T(8,128)(2,1)} %copy.52) | copy-start | bytes 1179652
  10.3 1.7 %copy-start.3 = (f32[16,192,192]{1,2,0:T(8,128)}, f32[16,192,192]{1,2,0:T(8,128)S(1)}, u32[]{:S(2)}) copy-start(f32[16,192,192]{1,2,0:T(8,128)S(1)} %get-tuple-element.25) | copy-start | bytes 7077892
  16.7 21.1 %all-to-all-start = ((f32[64,2,16]{2,1,0:T(2,128)}), f32[64,2,16]{2,1,0:T(2,128)S(1)}, u32[]{:S(2)}, u32[]{:S(2)}) async-start(f32[64,2,16]{2,1,0:T(2,128)} %copy.61), calls=%async_computation | async-start | bytes 131072 | tf_op jit(solution)/shard_map/all_to_all | solution.py:198
  27.3 4.2 %copy-start.1 = (f32[192,16,64]{0,2,1:T(8,128)S(1)}, f32[192,16,64]{0,2,1:T(8,128)}, u32[]{:S(2)}) copy-start(f32[192,16,64]{0,2,1:T(8,128)} %copy-done) | copy-start | bytes 2359300
  31.2 1.5 %copy-start.2 = (f32[192,16,64]{0,2,1:T(8,128)S(1)}, f32[192,16,64]{0,2,1:T(8,128)}, u32[]{:S(2)}) copy-start(f32[192,16,64]{0,2,1:T(8,128)} %get-tuple-element.26) | copy-start | bytes 2359300
  32.7 2.6 %copy-start.4 = (bf16[192,16,64]{0,2,1:T(8,128)(2,1)S(1)}, bf16[192,16,64]{0,2,1:T(8,128)(2,1)}, u32[]{:S(2)}) copy-start(bf16[192,16,64]{0,2,1:T(8,128)(2,1)} %multiply_convert_fusion.1) | copy-start | bytes 1179652
  37.9 16.6 %copy-start.8 = (s32[1,12,12]{2,0,1:T(1,128)S(1)}, s32[1,12,12]{2,0,1:T(1,128)}, u32[]{:S(2)}) copy-start(s32[1,12,12]{2,0,1:T(1,128)} %param.12) | copy-start | bytes 1732
  39.7 61.8 %all-to-all-start.1 = ((bf16[12,16,3200]{2,1,0:T(8,128)(2,1)}), bf16[12,16,3200]{2,1,0:T(8,128)(2,1)S(1)}, u32[]{:S(2)}, u32[]{:S(2)}) async-start(bf16[12,16,3200]{2,1,0:T(8,128)(2,1)} %gather_fusion), calls=%async_computation.1 | async-start | bytes 2457600 | tf_op jit(solution)/shard_map/all_to_all | solution.py:208

commit v4 on v3

v4 whole, which is shorter than its diff:
```python
import math

import jax
import jax.numpy as jnp
from jax import lax
from jax.sharding import PartitionSpec as P


HEADS = 16
HD = 64
PIECE = 16
PMAX = 12
P_OWN = 8


epsilon = 1e-05


def normalize_rows(rows, gain_row):
    values = rows.astype(jnp.float32).reshape(rows.shape[0], rows.shape[1] // HD, HD)
    centred = values - jnp.mean(values, -1, keepdims=True)
    inv_scale = lax.rsqrt(jnp.mean(centred * centred, -1, keepdims=True) + epsilon)
    normed = centred * inv_scale
    return (normed, inv_scale, (normed * gain_row).astype(jnp.bfloat16))


def row_norm_back(d_hat, normed, inv_scale, gain_row, live_rows):
    d_norm = d_hat * gain_row
    d_input = inv_scale * (
        d_norm
        - jnp.mean(d_norm, -1, keepdims=True)
        - normed * jnp.mean(d_norm * normed, -1, keepdims=True)
    )
    gain_term = jnp.sum(d_hat * normed * live_rows[:, None, None], 0)
    return (d_input, gain_term.reshape(-1))


def block_grads(query_rows, key_rows, value_rows, cotangent, piece_of, image_num, gains, live_rows):
    rows = query_rows.shape[0]
    heads = query_rows.shape[1] // HD
    three = (rows, heads, HD)
    gain_query = gains[0].reshape(heads, HD)
    gain_key = gains[1].reshape(heads, HD)
    q_norm, q_scale, q_hat = normalize_rows(query_rows, gain_query)
    k_norm, k_scale, k_hat = normalize_rows(key_rows, gain_key)
    values = value_rows.reshape(three)
    cot = cotangent.reshape(three)
    factor = HD ** (-0.5)
    f32 = jnp.float32
    scores = jnp.einsum("ihd,jhd->hij", q_hat, k_hat, preferred_element_type=f32) * factor
    same = (piece_of[:, None] == piece_of[None, :]) & (image_num[:, None] == image_num[None, :])
    weights = jnp.where(same[None], jnp.exp(scores), 0.0)
    probs = weights / jnp.sum(weights, -1, keepdims=True)
    probs_b = probs.astype(jnp.bfloat16)
    attended = jnp.einsum("hij,jhd->ihd", probs_b, values, preferred_element_type=f32)
    row_delta = jnp.sum(cot.astype(f32) * attended, -1)
    d_value = jnp.einsum("hij,ihd->jhd", probs_b, cot, preferred_element_type=f32)
    d_prob = jnp.einsum("ihd,jhd->hij", cot, values, preferred_element_type=f32)
    d_score = (probs * (d_prob - jnp.transpose(row_delta)[..., None]) * factor).astype(
        jnp.bfloat16
    )
    d_qhat = jnp.einsum("hij,jhd->ihd", d_score, k_hat, preferred_element_type=f32)
    d_khat = jnp.einsum("hij,ihd->jhd", d_score, q_hat, preferred_element_type=f32)
    d_query, term_query = row_norm_back(d_qhat, q_norm, q_scale, gain_query, live_rows)
    d_key, term_key = row_norm_back(d_khat, k_norm, k_scale, gain_key, live_rows)
    flat = (rows, heads * HD)
    return (
        d_query.reshape(flat).astype(jnp.bfloat16),
        d_key.reshape(flat).astype(jnp.bfloat16),
        d_value.reshape(flat).astype(jnp.bfloat16),
        jnp.stack([term_query, term_key]),
    )


def send_slots(own_plan, enc_count, per_slot):
    owner_hit = (own_plan[:, None] == jnp.arange(enc_count, dtype=jnp.int32)[None, :]).astype(
        jnp.int32
    )
    slot_rank = jnp.sum((jnp.cumsum(owner_hit, 0) - owner_hit) * owner_hit, 1)
    slot_target = jnp.where(own_plan >= 0, own_plan * per_slot + slot_rank, -1)
    slot_ids = jnp.arange(enc_count * per_slot, dtype=jnp.int32)
    matches = (slot_target[None, :] == slot_ids[:, None]).astype(jnp.int32)
    slot_source = jnp.sum(matches * jnp.arange(PMAX, dtype=jnp.int32)[None, :], 1)
    slot_filled = jnp.sum(matches, 1) > 0
    return (slot_source, slot_filled)


def receive_order(group_plan, enc_rank, enc_count, per_slot):
    arrived = jnp.sum((group_plan == enc_rank).astype(jnp.int32), 1)
    live_slots = (
        (jnp.arange(per_slot, dtype=jnp.int32)[None, :] < arrived[:, None])
        .reshape(-1)
        .astype(jnp.int32)
    )
    live_order = jnp.cumsum(live_slots) - 1
    wanted = jnp.arange(P_OWN, dtype=jnp.int32)
    matches = ((live_order[None, :] == wanted[:, None]) & (live_slots[None, :] > 0)).astype(
        jnp.int32
    )
    return jnp.sum(matches * jnp.arange(enc_count * per_slot, dtype=jnp.int32)[None, :], 1)


def from_slots(received, arrival_order):
    return jnp.take(received, arrival_order, axis=0, mode="clip")


def local_body(query_raw, key_raw, value_rows, out_cotangent, image_ids, owners, gains):
    enc_count = lax.axis_size("enc")
    grp_count = lax.axis_size("grp")
    enc_rank = lax.axis_index("enc")
    per_slot = PMAX // enc_count
    feat = HEADS * HD
    group_plan = owners[0]
    own_plan = lax.dynamic_index_in_dim(group_plan, enc_rank, 0, keepdims=False)
    slot_source, _ = send_slots(own_plan, enc_count, per_slot)
    arrival_order = receive_order(group_plan, enc_rank, enc_count, per_slot)
    live_flags = (own_plan >= 0).astype(jnp.float32)
    live_rows = jnp.repeat(live_flags, PIECE)
    piece_of = jnp.repeat(jnp.arange(PMAX, dtype=jnp.int32), PIECE)
    half = feat // 2
    halves = []
    terms = []
    for part in range(2):
        cut = slice(part * half, (part + 1) * half)
        d_query, d_key, d_value, part_terms = block_grads(
            query_raw[:, cut],
            key_raw[:, cut],
            value_rows[:, cut],
            out_cotangent[:, cut],
            piece_of,
            image_ids,
            gains[:, cut],
            live_rows,
        )
        grads = jnp.concatenate((d_query, d_key, d_value), axis=-1)
        grads = grads.reshape(PMAX, PIECE, 3 * half)
        terms.append(part_terms)
        if part == 1:
            gain_terms = jnp.concatenate(terms, axis=1)
            cols = feat // grp_count
            by_grp = jnp.transpose(gain_terms.reshape(2, grp_count, cols), (1, 0, 2))
            by_grp = lax.all_to_all(by_grp, "grp", split_axis=0, concat_axis=0, tiled=True)
            grp_sum = jnp.sum(by_grp, axis=0)
            grp_top = lax.reduce_precision(grp_sum, exponent_bits=8, mantissa_bits=7)
            grp_hi = grp_top.astype(jnp.bfloat16)
            grp_lo = (grp_sum - grp_top).astype(jnp.bfloat16)
            extra = jnp.concatenate((grp_hi, grp_lo), axis=0)
            extra = jnp.pad(extra, ((0, PIECE - 4), (0, 128 - cols)))
            extra = jnp.broadcast_to(extra[None], (PMAX, PIECE, 128))
            grads = jnp.concatenate((grads, extra), axis=-1)
        packed = jnp.take(grads, slot_source, axis=0, mode="clip")
        if part == 0:
            packed, query_raw, key_raw, value_rows, out_cotangent = lax.optimization_barrier(
                (packed, query_raw, key_raw, value_rows, out_cotangent)
            )
        received = lax.all_to_all(packed, "enc", split_axis=0, concat_axis=0, tiled=True)
        halves.append(from_slots(received[:, :, : 3 * half], arrival_order))
    parts = received[:, 0:4, 3 * half : 3 * half + cols].astype(jnp.float32)
    shares = jnp.sum(parts[:, 0:2] + parts[:, 2:4], axis=0)
    total_live = enc_count * grp_count * P_OWN * PIECE
    gain_grad = shares / math.sqrt(total_live)
    own_rows = P_OWN * PIECE
    outs = []
    for which in range(3):
        outs.append(
            jnp.concatenate(
                [h[:, :, which * half : (which + 1) * half] for h in halves], axis=-1
            ).reshape(own_rows, feat)
        )
    return (outs[0], outs[1], outs[2], gain_grad)


def solution(mesh):
    return jax.shard_map(
        local_body,
        mesh=mesh,
        in_specs=(
            P(("enc", "grp"), None),
            P(("enc", "grp"), None),
            P(("enc", "grp"), None),
            P(("enc", "grp"), None),
            P(("enc", "grp")),
            P("grp", None, None),
            P(),
        ),
        out_specs=(
            P(("enc", "grp"), None),
            P(("enc", "grp"), None),
            P(("enc", "grp"), None),
            P(None, "grp"),
        ),
        check_vma=False,
    )
```

time: 104 us -> 120 us (1.15)
  the two profiles are of different devices: /device:TPU:66 before, /device:TPU:64 now
where the time goes in v4:
time: 120 us; the launch traced here: 119 us
  waiting for transfers between devices  56.7 us (47%)
  starting transfers between devices  28.9 us (24%)
  local copies, waits for them, and re-layouts  17.4 us (14%)
  matrix products  8.83 us (7%)
  other arithmetic  6.35 us (5%)
  between operations  1.36 us (1%)
    all_to_all x2, waiting for transfers between devices, local_body(): lax.all_to_all(packed, 'enc', split_axis=0, concat_axis=0, tiled=True)  47.7 us
    all_to_all x2, starting transfers between devices, local_body(): lax.all_to_all(packed, 'enc', split_axis=0, concat_axis=0, tiled=True)  18.3 us
    all_to_all x1, starting transfers between devices, local_body(): lax.all_to_all(by_grp, 'grp', split_axis=0, concat_axis=0, tiled=True)  10.6 us
    all_to_all x1, waiting for transfers between devices, local_body(): lax.all_to_all(by_grp, 'grp', split_axis=0, concat_axis=0, tiled=True)  8.94 us
    gather x2, local copies, waits for them, and re-layouts, local_body(): packed = jnp.take(grads, slot_source, axis=0, mode='clip')  3.12 us
    convert_element_type x4, local copies, waits for them, and re-layouts, block_grads(): d_value.reshape(flat).astype(jnp.bfloat16)  2.9 us
  transfers between devices with their start and end apart: 3, of which 3 were waited for; matrix products, arithmetic and copies ran while one was open for 6% of the time, Pallas kernels for 0%

profile of v4, /device:TPU:64, one launch (start us, length us, event | category | flops | bytes accessed | tf_op | source)
XLA Modules:
  0.0 119.5 jit_solution(17089538413548497740)
XLA Ops:
  0.7 0.7 compare_convert_fusion.2
  2.0 0.8 slice_reduce_fusion
  3.1 0.9 slice.77
  4.2 1.0 slice.76
  7.0 0.8 fusion.9
  7.7 1.1 fusion.4
  9.1 1.5 %multiply_convert_fusion.1 = bf16[8,192,192]{1,2,0:T(8,128)(2,1)S(1)} fusion(f32[8,192,192]{1,2,0:T(8,128)S(1)} %fusion.9, bf16[192,8,64]{0,2,1:T(8,128)(2,1)} %bitcast.109, bf16[192,8,64]{0,2,1:T(8,128)(2,1)} %bitcast.111, f32[8,192]{1,0:T(8,128)S(1)} %bitcast.118), kind=kOutput, calls=%fused_computation.6 | convolution fusion | flops 38928384 | bytes 2168832 | tf_op jit(solution)/shard_map/ihd,jhd->hij/dot_general | solution.py:58
  10.6 1.2 copy.92
  15.8 1.4 %gather_fusion = bf16[12,16,1536]{2,1,0:T(8,128)(2,1)} fusion(bf16[12,16,1536]{2,1,0:T(8,128)(2,1)S(1)} %pad_maximum_fusion.1, s32[1024]{0:T(1024)S(1)} %pad_clamp_fusion.1), kind=kCustom, calls=%fused_computation | custom fusion | bytes 1179696 | tf_op jit(solution)/shard_map/jit(_take)/gather | solution.py:151
  18.8 0.8 fusion.7
  21.0 1.3 %multiply_reduce_fusion.5 = (f32[192,8]{0,1:T(8,128)S(1)}, f32[8,64]{1,0:T(8,128)S(1)}, f32[192,8]{0,1:T(8,128)S(1)}, f32[192,8]{0,1:T(8,128)S(1)}, f32[8,64]{1,...) fusion(f32[8,64]{1,0:T(8,128)S(1)} %mul.296, f32[192]{0:T(256)S(1)} %copy-done.14, ...), kind=kOutput, calls=%fused_computation.43 | convolution fusion | flops 39904256 | bytes 2220800 | tf_op jit(solution)/shard_map/hij,jhd->ihd/dot_general | solution.py:62
  22.5 0.7 copy.105
  23.2 10.6 %all-to-all-start.1 = ((f32[64,2,16]{2,1,0:T(2,128)}), f32[64,2,16]{2,1,0:T(2,128)S(1)}, u32[]{:S(2)}, u32[]{:S(2)}) async-start(f32[64,2,16]{2,1,0:T(2,128)} %copy.105), calls=%async_computation.1 | async-start | bytes 131072 | tf_op jit(solution)/shard_map/all_to_all | solution.py:142
  33.8 1.1 fusion.5
  34.9 8.9 %all-to-all-done.1 = f32[64,2,16]{2,1,0:T(2,128)S(1)} async-done(((f32[64,2,16]{2,1,0:T(2,128)}), f32[64,2,16]{2,1,0:T(2,128)S(1)}, u32[]{:S(2)}, u32[]{:S(2)}) %all-to-all-start.1) | async-done | bytes 8224 | tf_op jit(solution)/shard_map/all_to_all | solution.py:142
  43.8 14.8 %all-to-all-start = ((bf16[12,16,1536]{2,1,0:T(8,128)(2,1)}), bf16[12,16,1536]{2,1,0:T(8,128)(2,1)S(1)}, u32[]{:S(2)}, u32[]{:S(2)}) async-start(bf16[12,16,1536]{2,1,0:T(8,128)(2,1)} %gather_fusion), calls=%async_computation | async-start | bytes 1179648 | tf_op jit(solution)/shard_map/all_to_all | solution.py:156
  58.6 1.2 copy.104
  61.7 1.7 %gather_fusion.2 = bf16[12,16,1664]{2,1,0:T(8,128)(2,1)} fusion(bf16[12,16,1664]{2,1,0:T(8,128)(2,1)S(1)} %pad_maximum_fusion, s32[1024]{0:T(1024)} %copy-done.12), kind=kCustom, calls=%fused_computation.2 | custom fusion | bytes 1278000 | tf_op jit(solution)/shard_map/jit(_take)/gather | solution.py:151
  63.5 21.6 %all-to-all-done = bf16[12,16,1536]{2,1,0:T(8,128)(2,1)S(1)} async-done(((bf16[12,16,1536]{2,1,0:T(8,128)(2,1)}), bf16[12,16,1536]{2,1,0:T(8,128)(2,1)S(1)}, u32[]{:S(2)}, u32[]{:S(2)}) %all-to-all-start) | async-done | bytes 589856 | tf_op jit(solution)/shard_map/all_to_all | solution.py:156
  85.1 3.5 %all-to-all-start.2 = ((bf16[12,16,1664]{2,1,0:T(8,128)(2,1)}), bf16[12,16,1664]{2,1,0:T(8,128)(2,1)S(1)}, u32[]{:S(2)}, u32[]{:S(2)}) async-start(bf16[12,16,1664]{2,1,0:T(8,128)(2,1)} %gather_fusion.2), calls=%async_computation.2 | async-start | bytes 1277952 | tf_op jit(solution)/shard_map/all_to_all | solution.py:156
  89.9 26.1 %all-to-all-done.2 = bf16[12,16,1664]{2,1,0:T(8,128)(2,1)S(1)} async-done(((bf16[12,16,1664]{2,1,0:T(8,128)(2,1)}), bf16[12,16,1664]{2,1,0:T(8,128)(2,1)S(1)}, u32[]{:S(2)}, u32[]{:S(2)}) %all-to-all-start.2) | async-done | bytes 639008 | tf_op jit(solution)/shard_map/all_to_all | solution.py:156
  117.3 0.7 pad_maximum_fusion.4
  118.0 0.7 pad_maximum_fusion.3
  118.8 0.7 pad_maximum_fusion.2
  (134 shorter events, 14.2 us)
Async XLA Ops:
  0.6 4.8 %copy-start.3 = (bf16[192,1024]{1,0:T(8,128)(2,1)S(1)}, bf16[192,1024]{1,0:T(8,128)(2,1)}, u32[]{:S(2)}) copy-start(bf16[192,1024]{1,0:T(8,128)(2,1)} %param.7) | copy-start | bytes 1179652
  1.5 10.9 %copy-start.13 = (f32[192]{0:T(256)}, f32[192]{0:T(256)S(1)}, u32[]{:S(2)}) copy-start(f32[192]{0:T(256)S(1)} %mul.314) | copy-start | bytes 2308
  1.9 13.9 %copy-start.12 = (s32[1024]{0:T(1024)}, s32[1024]{0:T(1024)S(1)}, u32[]{:S(2)}) copy-start(s32[1024]{0:T(1024)S(1)} %pad_clamp_fusion.1) | copy-start | bytes 12292
  4.2 4.6 %copy-start.1 = (bf16[192,512]{0,1:T(8,128)(2,1)}, bf16[192,512]{0,1:T(8,128)(2,1)S(1)}, u32[]{:S(2)}) copy-start(bf16[192,512]{0,1:T(8,128)(2,1)S(1)} %copy.84) | copy-start | bytes 589828
  5.3 1.0 copy-start.5
  5.4 3.4 %copy-start = (bf16[192,512]{0,1:T(8,128)(2,1)}, bf16[192,512]{0,1:T(8,128)(2,1)S(1)}, u32[]{:S(2)}) copy-start(bf16[192,512]{0,1:T(8,128)(2,1)S(1)} %copy.83) | copy-start | bytes 589828
  5.8 0.9 copy-start.15
  15.5 1.8 %slice-start = ((bf16[192,1024]{1,0:T(8,128)(2,1)}), bf16[192,512]{1,0:T(8,128)(2,1)S(1)}, s32[]{:S(2)}) async-start(bf16[192,1024]{1,0:T(8,128)(2,1)} %param.10), calls=%async_computation.3 | async-start | bytes 393216 | tf_op jit(solution)/shard_map/slice | solution.py:129
  15.7 1.6 %slice-start.1 = ((bf16[192,1024]{1,0:T(8,128)(2,1)}), bf16[192,512]{1,0:T(8,128)(2,1)S(1)}, s32[]{:S(2)}) async-start(bf16[192,1024]{1,0:T(8,128)(2,1)} %param.9), calls=%async_computation.4 | async-start | bytes 393216 | tf_op jit(solution)/shard_map/slice | solution.py:128
  15.8 1.7 %copy-start.4 = (bf16[192,1024]{1,0:T(8,128)(2,1)S(1)}, bf16[192,1024]{1,0:T(8,128)(2,1)}, u32[]{:S(2)}) copy-start(bf16[192,1024]{1,0:T(8,128)(2,1)} %param.7) | copy-start | bytes 1179652
  17.4 1.0 copy-start.6
  18.8 1.9 %copy-start.7 = (f32[192,8]{0,1:T(8,128)}, f32[192,8]{0,1:T(8,128)S(1)}, u32[]{:S(2)}) copy-start(f32[192,8]{0,1:T(8,128)S(1)} %add_rsqrt_fusion) | copy-start | bytes 18436
  20.3 0.7 copy-start.14
  21.0 1.4 %copy-start.9 = (f32[1,512]{1,0:T(1,128)S(1)}, f32[1,512]{1,0:T(1,128)}, u32[]{:S(2)}) copy-start(f32[1,512]{1,0:T(1,128)} %stack_reshape.12) | copy-start | bytes 6148
  21.0 1.4 %copy-start.10 = (f32[1,512]{1,0:T(1,128)S(1)}, f32[1,512]{1,0:T(1,128)}, u32[]{:S(2)}) copy-start(f32[1,512]{1,0:T(1,128)} %stack_reshape.13) | copy-start | bytes 6148
  23.2 20.6 %all-to-all-start.1 = ((f32[64,2,16]{2,1,0:T(2,128)}), f32[64,2,16]{2,1,0:T(2,128)S(1)}, u32[]{:S(2)}, u32[]{:S(2)}) async-start(f32[64,2,16]{2,1,0:T(2,128)} %copy.105), calls=%async_computation.1 | async-start | bytes 131072 | tf_op jit(solution)/shard_map/all_to_all | solution.py:142
  34.9 25.2 %copy-start.8 = (f32[192,8]{0,1:T(8,128)S(1)}, f32[192,8]{0,1:T(8,128)}, u32[]{:S(2)}) copy-start(f32[192,8]{0,1:T(8,128)} %copy-done.7) | copy-start | bytes 18436
  43.8 41.2 %all-to-all-start = ((bf16[12,16,1536]{2,1,0:T(8,128)(2,1)}), bf16[12,16,1536]{2,1,0:T(8,128)(2,1)S(1)}, u32[]{:S(2)}, u32[]{:S(2)}) async-start(bf16[12,16,1536]{2,1,0:T(8,128)(2,1)} %gather_fusion), calls=%async_computation | async-start | bytes 1179648 | tf_op jit(solution)/shard_map/all_to_all | solution.py:156
  59.8 1.0 copy-start.2
  61.7 26.9 %copy-start.11 = (s32[1,12,12]{2,0,1:T(1,128)S(1)}, s32[1,12,12]{2,0,1:T(1,128)}, u32[]{:S(2)}) copy-start(s32[1,12,12]{2,0,1:T(1,128)} %param.12) | copy-start | bytes 1732
  85.1 31.0 %all-to-all-start.2 = ((bf16[12,16,1664]{2,1,0:T(8,128)(2,1)}), bf16[12,16,1664]{2,1,0:T(8,128)(2,1)S(1)}, u32[]{:S(2)}, u32[]{:S(2)}) async-start(bf16[12,16,1664]{2,1,0:T(8,128)(2,1)} %gather_fusion.2), calls=%async_computation.2 | async-start | bytes 1277952 | tf_op jit(solution)/shard_map/all_to_all | solution.py:156

commit v5 on v4

--- a/solution.py
+++ b/solution.py
@@ -17,7 +17,7 @@
 
 
 def normalize_rows(rows, gain_row):
-    values = rows.astype(jnp.float32).reshape(rows.shape[0], rows.shape[1] // HD, HD)
+    values = rows.astype(jnp.float32).reshape(rows.shape[0], HEADS, HD)
     centred = values - jnp.mean(values, -1, keepdims=True)
     inv_scale = lax.rsqrt(jnp.mean(centred * centred, -1, keepdims=True) + epsilon)
     normed = centred * inv_scale
@@ -37,10 +37,9 @@
 
 def block_grads(query_rows, key_rows, value_rows, cotangent, piece_of, image_num, gains, live_rows):
     rows = query_rows.shape[0]
-    heads = query_rows.shape[1] // HD
-    three = (rows, heads, HD)
-    gain_query = gains[0].reshape(heads, HD)
-    gain_key = gains[1].reshape(heads, HD)
+    three = (rows, HEADS, HD)
+    gain_query = gains[0].reshape(HEADS, HD)
+    gain_key = gains[1].reshape(HEADS, HD)
     q_norm, q_scale, q_hat = normalize_rows(query_rows, gain_query)
     k_norm, k_scale, k_hat = normalize_rows(key_rows, gain_key)
     values = value_rows.reshape(three)
@@ -63,13 +62,37 @@
     d_khat = jnp.einsum("hij,ihd->jhd", d_score, q_hat, preferred_element_type=f32)
     d_query, term_query = row_norm_back(d_qhat, q_norm, q_scale, gain_query, live_rows)
     d_key, term_key = row_norm_back(d_khat, k_norm, k_scale, gain_key, live_rows)
-    flat = (rows, heads * HD)
+    flat = (rows, HEADS * HD)
     return (
         d_query.reshape(flat).astype(jnp.bfloat16),
         d_key.reshape(flat).astype(jnp.bfloat16),
         d_value.reshape(flat).astype(jnp.bfloat16),
         jnp.stack([term_query, term_key]),
     )
+
+
+def reduce_gain_terms(gain_terms, enc_count, grp_count):
+    grp_rank = lax.axis_index("grp")
+    current = gain_terms
+    bit = grp_count // 2
+    while bit >= 1:
+        width = current.shape[1] // 2
+        upper = (grp_rank // bit) % 2 == 1
+        low_part = current[:, :width]
+        high_part = current[:, width:]
+        send = jnp.where(upper, low_part, high_part)
+        keep = jnp.where(upper, high_part, low_part)
+        pairs = [(i, i ^ bit) for i in range(grp_count)]
+        current = keep + lax.ppermute(send, "grp", pairs)
+        bit //= 2
+    enc_rank = lax.axis_index("enc")
+    gathered = [current]
+    for shift in range(1, enc_count):
+        pairs = [(i, (i + shift) % enc_count) for i in range(enc_count)]
+        gathered.append(lax.ppermute(current, "enc", pairs))
+    stacked = jnp.stack(gathered)
+    source_order = (enc_rank - jnp.arange(enc_count, dtype=jnp.int32)) % enc_count
+    return jnp.sum(jnp.take(stacked, source_order, axis=0, mode="clip"), axis=0)
 
 
 def send_slots(own_plan, enc_count, per_slot):
@@ -114,60 +137,31 @@
     own_plan = lax.dynamic_index_in_dim(group_plan, enc_rank, 0, keepdims=False)
     slot_source, _ = send_slots(own_plan, enc_count, per_slot)
     arrival_order = receive_order(group_plan, enc_rank, enc_count, per_slot)
+    piece_shape = (PMAX, PIECE, feat)
     live_flags = (own_plan >= 0).astype(jnp.float32)
     live_rows = jnp.repeat(live_flags, PIECE)
     piece_of = jnp.repeat(jnp.arange(PMAX, dtype=jnp.int32), PIECE)
-    half = feat // 2
-    halves = []
-    terms = []
-    for part in range(2):
-        cut = slice(part * half, (part + 1) * half)
-        d_query, d_key, d_value, part_terms = block_grads(
-            query_raw[:, cut],
-            key_raw[:, cut],
-            value_rows[:, cut],
-            out_cotangent[:, cut],
-            piece_of,
-            image_ids,
-            gains[:, cut],
-            live_rows,
-        )
-        grads = jnp.concatenate((d_query, d_key, d_value), axis=-1)
-        grads = grads.reshape(PMAX, PIECE, 3 * half)
-        terms.append(part_terms)
-        if part == 1:
-            gain_terms = jnp.concatenate(terms, axis=1)
-            cols = feat // grp_count
-            by_grp = jnp.transpose(gain_terms.reshape(2, grp_count, cols), (1, 0, 2))
-            by_grp = lax.all_to_all(by_grp, "grp", split_axis=0, concat_axis=0, tiled=True)
-            grp_sum = jnp.sum(by_grp, axis=0)
-            grp_top = lax.reduce_precision(grp_sum, exponent_bits=8, mantissa_bits=7)
-            grp_hi = grp_top.astype(jnp.bfloat16)
-            grp_lo = (grp_sum - grp_top).astype(jnp.bfloat16)
-            extra = jnp.concatenate((grp_hi, grp_lo), axis=0)
-            extra = jnp.pad(extra, ((0, PIECE - 4), (0, 128 - cols)))
-            extra = jnp.broadcast_to(extra[None], (PMAX, PIECE, 128))
-            grads = jnp.concatenate((grads, extra), axis=-1)
-        packed = jnp.take(grads, slot_source, axis=0, mode="clip")
-        if part == 0:
-            packed, query_raw, key_raw, value_rows, out_cotangent = lax.optimization_barrier(
-                (packed, query_raw, key_raw, value_rows, out_cotangent)
-            )
-        received = lax.all_to_all(packed, "enc", split_axis=0, concat_axis=0, tiled=True)
-        halves.append(from_slots(received[:, :, : 3 * half], arrival_order))
-    parts = received[:, 0:4, 3 * half : 3 * half + cols].astype(jnp.float32)
-    shares = jnp.sum(parts[:, 0:2] + parts[:, 2:4], axis=0)
+    d_query, d_key, d_value, gain_terms = block_grads(
+        query_raw, key_raw, value_rows, out_cotangent, piece_of, image_ids, gains, live_rows
+    )
+    d_query = d_query.reshape(piece_shape)
+    d_key = d_key.reshape(piece_shape)
+    d_value = d_value.reshape(piece_shape)
+    grads = jnp.concatenate((d_query, d_key, d_value), axis=-1)
+    packed = jnp.take(grads, slot_source, axis=0, mode="clip")
+    received = lax.all_to_all(packed, "enc", split_axis=0, concat_axis=0, tiled=True)
+    mine = from_slots(received, arrival_order)
+    shares = reduce_gain_terms(gain_terms, enc_count, grp_count)
     total_live = enc_count * grp_count * P_OWN * PIECE
     gain_grad = shares / math.sqrt(total_live)
     own_rows = P_OWN * PIECE
-    outs = []
-    for which in range(3):
-        outs.append(
-            jnp.concatenate(
-                [h[:, :, which * half : (which + 1) * half] for h in halves], axis=-1
-            ).reshape(own_rows, feat)
-        )
-    return (outs[0], outs[1], outs[2], gain_grad)
+    mine = mine.reshape(own_rows, 3 * feat)
+    return (
+        mine[:, :feat],
+        mine[:, feat : 2 * feat],
+        mine[:, 2 * feat :],
+        gain_grad,
+    )
 
 
 def solution(mesh):

time: 120 us -> 142 us (1.18)
  the two profiles are of different devices: /device:TPU:64 before, /device:TPU:52 now
where the time goes in v5:
time: 142 us; the launch traced here: 141 us
  starting transfers between devices  85.6 us (60%)
  waiting for transfers between devices  20 us (14%)
  local copies, waits for them, and re-layouts  18 us (13%)
  matrix products  10.1 us (7%)
  other arithmetic  5.93 us (4%)
  between operations  1.43 us (1%)
    ppermute x11, starting transfers between devices, reduce_gain_terms(): gathered.append(lax.ppermute(current, 'enc', pairs))  52.6 us
    ppermute x6, waiting for transfers between devices, reduce_gain_terms(): current = keep + lax.ppermute(send, 'grp', pairs)  18 us
    ppermute x6, starting transfers between devices, reduce_gain_terms(): current = keep + lax.ppermute(send, 'grp', pairs)  17.8 us
    all_to_all x1, starting transfers between devices, local_body(): lax.all_to_all(packed, 'enc', split_axis=0, concat_axis=0, tiled=True)  15.2 us
    unnamed x42, local copies, waits for them, and re-layouts  6.16 us
    dot_general x1, matrix products, block_grads(): jnp.einsum('hij,jhd->ihd', d_score, k_hat, preferred_element_type=f32)  3.26 us
    convert_element_type x2, local copies, waits for them, and re-layouts, block_grads(): d_key.reshape(flat).astype(jnp.bfloat16)  3.06 us
    dot_general x1, matrix products, block_grads(): jnp.einsum('hij,jhd->ihd', probs_b, values, preferred_element_type=f32)  2.96 us
  transfers between devices with their start and end apart: 18, of which 7 were waited for; matrix products, arithmetic and copies ran while one was open for 2% of the time, Pallas kernels for 0%

profile of v5, /device:TPU:52, one launch (start us, length us, event | category | flops | bytes accessed | tf_op | source)
XLA Modules:
  0.0 141.1 jit_solution(6865671194338349381)
XLA Ops:
  0.6 2.0 %copy.36 = bf16[192,1024]{0,1:T(8,128)(2,1)} copy(bf16[192,1024]{1,0:T(8,128)(2,1)} %param.10) | data formatting | bytes 786432 | tf_op args[3]
  12.4 3.0 %fusion.3 = f32[192,16]{0,1:T(8,128)S(1)} fusion(bf16[192,16,64]{0,2,1:T(8,128)(2,1)S(1)} %bitcast.73, bf16[192,16,64]{0,2,1:T(8,128)(2,1)S(1)} %bitcast.71, f32[16,192,192]{1,2,0:T(8,128)} %copy-done.4, f32[16,192]{1,0:T(8,128)S(1)} %get-tuple-element.24, pred[192,192]{0,1:T(8,128)(4,1)S(1)} %compare_and_fusion), kind=kOutput, calls=%fused_computation.12 | convolution fusion | flops 78443520 | bytes 3207168 | tf_op jit(solution)/shard_map/hij,jhd->ihd/dot_general | solution.py:54
  19.7 3.3 %multiply_reduce_fusion.1 = (f32[16,64]{1,0:T(8,128)S(1)}, f32[192,16]{0,1:T(8,128)S(1)}, f32[192,16]{0,1:T(8,128)S(1)}, f32[192,16]{0,1:T(8,128)S(1)}, f32[192,...) fusion(f32[192,16,64]{0,2,1:T(8,128)S(1)} %get-tuple-element.27, f32[192]{0:T(256)S(1)} %mul.170, ...), kind=kOutput, calls=%fused_computation.20 | convolution fusion | flops 78628864 | bytes 4391680 | tf_op jit(solution)/shard_map/hij,jhd->ihd/dot_general | solution.py:61
  31.0 15.2 %all-to-all-start = ((bf16[12,16,3072]{2,1,0:T(8,128)(2,1)}), bf16[12,16,3072]{2,1,0:T(8,128)(2,1)S(1)}, u32[]{:S(2)}, u32[]{:S(2)}) async-start(bf16[12,16,3072]{2,1,0:T(8,128)(2,1)} %gather_fusion), calls=%async_computation | async-start | bytes 2359296 | tf_op jit(solution)/shard_map/all_to_all | solution.py:152
  46.3 3.8 %collective-permute-start = (f32[2,512]{1,0:T(2,128)S(1)}, f32[2,512]{1,0:T(2,128)S(1)}, u32[]{:S(2)}, u32[]{:S(2)}) collective-permute-start(f32[2,512]{1,0:T(2,128)S(1)} %broadcast_select_fusion), channel_id=1, source_target_pairs={{0,32},{1,33},{2,34},{3,35},{4,36},{5,37},{6,38},{7,39},{8,40},{9,... | collective-permute-start | bytes 12296 | tf_op jit(solution)/shard_map/ppermute | solution.py:86
  50.8 4.9 %collective-permute-done = f32[2,512]{1,0:T(2,128)S(1)} collective-permute-done((f32[2,512]{1,0:T(2,128)S(1)}, f32[2,512]{1,0:T(2,128)S(1)}, u32[]{:S(2)}, u32[]{:S(2)}) %collective-permute-start) | collective-permute-done | bytes 4128 | tf_op jit(solution)/shard_map/ppermute | solution.py:86
  55.8 4.0 %collective-permute-start.1 = (f32[2,256]{1,0:T(2,128)S(1)}, f32[2,256]{1,0:T(2,128)S(1)}, u32[]{:S(2)}, u32[]{:S(2)}) collective-permute-start(f32[2,256]{1,0:T(2,128)S(1)} %broadcast_select_fusion.1), channel_id=1, source_target_pairs={{0,16},{1,17},{2,18},{3,19},{4,20},{5,21},{6,22},{7,23},{8,24},{9,... | collective-permute-start | bytes 6152 | tf_op jit(solution)/shard_map/ppermute | solution.py:86
  59.9 2.3 %collective-permute-done.1 = f32[2,256]{1,0:T(2,128)S(1)} collective-permute-done((f32[2,256]{1,0:T(2,128)S(1)}, f32[2,256]{1,0:T(2,128)S(1)}, u32[]{:S(2)}, u32[]{:S(2)}) %collective-permute-start.1) | collective-permute-done | bytes 2080 | tf_op jit(solution)/shard_map/ppermute | solution.py:86
  62.2 2.6 %collective-permute-start.2 = (f32[2,128]{1,0:T(2,128)S(1)}, f32[2,128]{1,0:T(2,128)S(1)}, u32[]{:S(2)}, u32[]{:S(2)}) collective-permute-start(f32[2,128]{1,0:T(2,128)S(1)} %broadcast_select_fusion.2), channel_id=1, source_target_pairs={{0,8},{1,9},{2,10},{3,11},{4,12},{5,13},{6,14},{7,15},{8,0},{9,1},... | collective-permute-start | bytes 3080 | tf_op jit(solution)/shard_map/ppermute | solution.py:86
  64.8 2.8 %collective-permute-done.2 = f32[2,128]{1,0:T(2,128)S(1)} collective-permute-done((f32[2,128]{1,0:T(2,128)S(1)}, f32[2,128]{1,0:T(2,128)S(1)}, u32[]{:S(2)}, u32[]{:S(2)}) %collective-permute-start.2) | collective-permute-done | bytes 1056 | tf_op jit(solution)/shard_map/ppermute | solution.py:86
  67.7 2.4 %collective-permute-start.3 = (f32[2,64]{1,0:T(2,128)S(1)}, f32[2,64]{1,0:T(2,128)S(1)}, u32[]{:S(2)}, u32[]{:S(2)}) collective-permute-start(f32[2,64]{1,0:T(2,128)S(1)} %broadcast_select_fusion.3), channel_id=1, source_target_pairs={{0,4},{1,5},{2,6},{3,7},{4,0},{5,1},{6,2},{7,3},{8,12},{9,13},{10,... | collective-permute-start | bytes 1544 | tf_op jit(solution)/shard_map/ppermute | solution.py:86
  70.1 4.5 %collective-permute-done.3 = f32[2,64]{1,0:T(2,128)S(1)} collective-permute-done((f32[2,64]{1,0:T(2,128)S(1)}, f32[2,64]{1,0:T(2,128)S(1)}, u32[]{:S(2)}, u32[]{:S(2)}) %collective-permute-start.3) | collective-permute-done | bytes 544 | tf_op jit(solution)/shard_map/ppermute | solution.py:86
  74.8 3.1 %collective-permute-start.4 = (f32[2,32]{1,0:T(2,128)S(1)}, f32[2,32]{1,0:T(2,128)S(1)}, u32[]{:S(2)}, u32[]{:S(2)}) collective-permute-start(f32[2,32]{1,0:T(2,128)S(1)} %broadcast_select_fusion.4), channel_id=1, source_target_pairs={{0,2},{1,3},{2,0},{3,1},{4,6},{5,7},{6,4},{7,5},{8,10},{9,11},{10,... | collective-permute-start | bytes 776 | tf_op jit(solution)/shard_map/ppermute | solution.py:86
  77.9 2.3 %collective-permute-done.4 = f32[2,32]{1,0:T(2,128)S(1)} collective-permute-done((f32[2,32]{1,0:T(2,128)S(1)}, f32[2,32]{1,0:T(2,128)S(1)}, u32[]{:S(2)}, u32[]{:S(2)}) %collective-permute-start.4) | collective-permute-done | bytes 288 | tf_op jit(solution)/shard_map/ppermute | solution.py:86
  83.5 3.9 %collective-permute-start.6 = (f32[2,16]{1,0:T(2,128)S(1)}, f32[2,16]{1,0:T(2,128)S(1)}, u32[]{:S(2)}, u32[]{:S(2)}) collective-permute-start(f32[2,16]{1,0:T(2,128)S(1)} %get-tuple-element.16), channel_id=1, source_target_pairs={{0,64},{64,128},{128,192},{192,256},{256,320},{320,384},{384,448},... | collective-permute-start | bytes 392 | tf_op jit(solution)/shard_map/ppermute | solution.py:92
  87.4 4.3 %collective-permute-start.7 = (f32[2,16]{1,0:T(2,128)S(1)}, f32[2,16]{1,0:T(2,128)S(1)}, u32[]{:S(2)}, u32[]{:S(2)}) collective-permute-start(f32[2,16]{1,0:T(2,128)S(1)} %get-tuple-element.16), channel_id=1, source_target_pairs={{0,128},{64,192},{128,256},{192,320},{256,384},{320,448},{384,512}... | collective-permute-start | bytes 392 | tf_op jit(solution)/shard_map/ppermute | solution.py:92
  91.7 6.4 %collective-permute-start.8 = (f32[2,16]{1,0:T(2,128)S(1)}, f32[2,16]{1,0:T(2,128)S(1)}, u32[]{:S(2)}, u32[]{:S(2)}) collective-permute-start(f32[2,16]{1,0:T(2,128)S(1)} %get-tuple-element.16), channel_id=1, source_target_pairs={{0,192},{64,256},{128,320},{192,384},{256,448},{320,512},{384,576}... | collective-permute-start | bytes 392 | tf_op jit(solution)/shard_map/ppermute | solution.py:92
  98.1 3.1 %collective-permute-start.9 = (f32[2,16]{1,0:T(2,128)S(1)}, f32[2,16]{1,0:T(2,128)S(1)}, u32[]{:S(2)}, u32[]{:S(2)}) collective-permute-start(f32[2,16]{1,0:T(2,128)S(1)} %get-tuple-element.16), channel_id=1, source_target_pairs={{0,256},{64,320},{128,384},{192,448},{256,512},{320,576},{384,640}... | collective-permute-start | bytes 392 | tf_op jit(solution)/shard_map/ppermute | solution.py:92
  101.2 5.2 %collective-permute-start.10 = (f32[2,16]{1,0:T(2,128)S(1)}, f32[2,16]{1,0:T(2,128)S(1)}, u32[]{:S(2)}, u32[]{:S(2)}) collective-permute-start(f32[2,16]{1,0:T(2,128)S(1)} %get-tuple-element.16), channel_id=1, source_target_pairs={{0,320},{64,384},{128,448},{192,512},{256,576},{320,640},{384,704}... | collective-permute-start | bytes 392 | tf_op jit(solution)/shard_map/ppermute | solution.py:92
  106.3 7.6 %collective-permute-start.11 = (f32[2,16]{1,0:T(2,128)S(1)}, f32[2,16]{1,0:T(2,128)S(1)}, u32[]{:S(2)}, u32[]{:S(2)}) collective-permute-start(f32[2,16]{1,0:T(2,128)S(1)} %get-tuple-element.16), channel_id=1, source_target_pairs={{0,384},{64,448},{128,512},{192,576},{256,640},{320,704},{384,0},{... | collective-permute-start | bytes 392 | tf_op jit(solution)/shard_map/ppermute | solution.py:92
  114.0 6.4 %collective-permute-start.12 = (f32[2,16]{1,0:T(2,128)S(1)}, f32[2,16]{1,0:T(2,128)S(1)}, u32[]{:S(2)}, u32[]{:S(2)}) collective-permute-start(f32[2,16]{1,0:T(2,128)S(1)} %get-tuple-element.16), channel_id=1, source_target_pairs={{0,448},{64,512},{128,576},{192,640},{256,704},{320,0},{384,64},{4... | collective-permute-start | bytes 392 | tf_op jit(solution)/shard_map/ppermute | solution.py:92
  122.4 6.3 %collective-permute-start.14 = (f32[2,16]{1,0:T(2,128)S(1)}, f32[2,16]{1,0:T(2,128)S(1)}, u32[]{:S(2)}, u32[]{:S(2)}) collective-permute-start(f32[2,16]{1,0:T(2,128)S(1)} %get-tuple-element.16), channel_id=1, source_target_pairs={{0,576},{64,640},{128,704},{192,0},{256,64},{320,128},{384,192},{4... | collective-permute-start | bytes 392 | tf_op jit(solution)/shard_map/ppermute | solution.py:92
  128.7 4.3 %collective-permute-start.15 = (f32[2,16]{1,0:T(2,128)S(1)}, f32[2,16]{1,0:T(2,128)S(1)}, u32[]{:S(2)}, u32[]{:S(2)}) collective-permute-start(f32[2,16]{1,0:T(2,128)S(1)} %get-tuple-element.16), channel_id=1, source_target_pairs={{0,640},{64,704},{128,0},{192,64},{256,128},{320,192},{384,256},{4... | collective-permute-start | bytes 392 | tf_op jit(solution)/shard_map/ppermute | solution.py:92
  133.0 3.4 %collective-permute-start.16 = (f32[2,16]{1,0:T(2,128)S(1)}, f32[2,16]{1,0:T(2,128)S(1)}, u32[]{:S(2)}, u32[]{:S(2)}) collective-permute-start(f32[2,16]{1,0:T(2,128)S(1)} %get-tuple-element.16), channel_id=1, source_target_pairs={{0,704},{64,0},{128,64},{192,128},{256,192},{320,256},{384,320},{4... | collective-permute-start | bytes 392 | tf_op jit(solution)/shard_map/ppermute | solution.py:92
  (128 shorter events, 32.8 us)
Async XLA Ops:
  0.6 3.7 %copy-start.10 = (bf16[192,1024]{1,0:T(8,128)(2,1)S(1)}, bf16[192,1024]{1,0:T(8,128)(2,1)}, u32[]{:S(2)}) copy-start(bf16[192,1024]{1,0:T(8,128)(2,1)} %param.8) | copy-start | bytes 1179652
  5.5 3.8 %copy-start.8 = (bf16[192,1024]{0,1:T(8,128)(2,1)S(1)}, bf16[192,1024]{0,1:T(8,128)(2,1)}, u32[]{:S(2)}) copy-start(bf16[192,1024]{0,1:T(8,128)(2,1)} %copy.36) | copy-start | bytes 1179652
  12.4 3.0 %copy-start.5 = (f32[16,192,192]{1,2,0:T(8,128)S(1)}, f32[16,192,192]{1,2,0:T(8,128)}, u32[]{:S(2)}) copy-start(f32[16,192,192]{1,2,0:T(8,128)} %copy-done.4) | copy-start | bytes 7077892
  24.1 3.1 %copy-start.3 = (f32[192,16,64]{0,2,1:T(8,128)S(1)}, f32[192,16,64]{0,2,1:T(8,128)}, u32[]{:S(2)}) copy-start(f32[192,16,64]{0,2,1:T(8,128)} %get-tuple-element.26) | copy-start | bytes 2359300
  25.9 3.3 %copy-start.6 = (bf16[12,16,1024]{2,1,0:T(8,128)(2,1)S(1)}, bf16[12,16,1024]{2,1,0:T(8,128)(2,1)}, u32[]{:S(2)}) copy-start(bf16[12,16,1024]{2,1,0:T(8,128)(2,1)} %convert_element_type.85) | copy-start | bytes 1179652
  29.2 21.0 %copy-start.12 = (s32[1,12,12]{2,0,1:T(1,128)S(1)}, s32[1,12,12]{2,0,1:T(1,128)}, u32[]{:S(2)}) copy-start(s32[1,12,12]{2,0,1:T(1,128)} %param.12) | copy-start | bytes 1732
  31.0 108.7 %all-to-all-start = ((bf16[12,16,3072]{2,1,0:T(8,128)(2,1)}), bf16[12,16,3072]{2,1,0:T(8,128)(2,1)S(1)}, u32[]{:S(2)}, u32[]{:S(2)}) async-start(bf16[12,16,3072]{2,1,0:T(8,128)(2,1)} %gather_fusion), calls=%async_computation | async-start | bytes 2359296 | tf_op jit(solution)/shard_map/all_to_all | solution.py:152
  46.3 9.4 %collective-permute-start = (f32[2,512]{1,0:T(2,128)S(1)}, f32[2,512]{1,0:T(2,128)S(1)}, u32[]{:S(2)}, u32[]{:S(2)}) collective-permute-start(f32[2,512]{1,0:T(2,128)S(1)} %broadcast_select_fusion), channel_id=1, source_target_pairs={{0,32},{1,33},{2,34},{3,35},{4,36},{5,37},{6,38},{7,39},{8,40},{9,... | collective-permute-start | bytes 12296 | tf_op jit(solution)/shard_map/ppermute | solution.py:86
  55.8 6.4 %collective-permute-start.1 = (f32[2,256]{1,0:T(2,128)S(1)}, f32[2,256]{1,0:T(2,128)S(1)}, u32[]{:S(2)}, u32[]{:S(2)}) collective-permute-start(f32[2,256]{1,0:T(2,128)S(1)} %broadcast_select_fusion.1), channel_id=1, source_target_pairs={{0,16},{1,17},{2,18},{3,19},{4,20},{5,21},{6,22},{7,23},{8,24},{9,... | collective-permute-start | bytes 6152 | tf_op jit(solution)/shard_map/ppermute | solution.py:86
  62.2 5.5 %collective-permute-start.2 = (f32[2,128]{1,0:T(2,128)S(1)}, f32[2,128]{1,0:T(2,128)S(1)}, u32[]{:S(2)}, u32[]{:S(2)}) collective-permute-start(f32[2,128]{1,0:T(2,128)S(1)} %broadcast_select_fusion.2), channel_id=1, source_target_pairs={{0,8},{1,9},{2,10},{3,11},{4,12},{5,13},{6,14},{7,15},{8,0},{9,1},... | collective-permute-start | bytes 3080 | tf_op jit(solution)/shard_map/ppermute | solution.py:86
  67.7 7.0 %collective-permute-start.3 = (f32[2,64]{1,0:T(2,128)S(1)}, f32[2,64]{1,0:T(2,128)S(1)}, u32[]{:S(2)}, u32[]{:S(2)}) collective-permute-start(f32[2,64]{1,0:T(2,128)S(1)} %broadcast_select_fusion.3), channel_id=1, source_target_pairs={{0,4},{1,5},{2,6},{3,7},{4,0},{5,1},{6,2},{7,3},{8,12},{9,13},{10,... | collective-permute-start | bytes 1544 | tf_op jit(solution)/shard_map/ppermute | solution.py:86
  74.8 5.5 %collective-permute-start.4 = (f32[2,32]{1,0:T(2,128)S(1)}, f32[2,32]{1,0:T(2,128)S(1)}, u32[]{:S(2)}, u32[]{:S(2)}) collective-permute-start(f32[2,32]{1,0:T(2,128)S(1)} %broadcast_select_fusion.4), channel_id=1, source_target_pairs={{0,2},{1,3},{2,0},{3,1},{4,6},{5,7},{6,4},{7,5},{8,10},{9,11},{10,... | collective-permute-start | bytes 776 | tf_op jit(solution)/shard_map/ppermute | solution.py:86
  80.4 3.0 %collective-permute-start.5 = (f32[2,16]{1,0:T(2,128)S(1)}, f32[2,16]{1,0:T(2,128)S(1)}, u32[]{:S(2)}, u32[]{:S(2)}) collective-permute-start(f32[2,16]{1,0:T(2,128)S(1)} %broadcast_select_fusion.5), channel_id=1, source_target_pairs={{0,1},{1,0},{2,3},{3,2},{4,5},{5,4},{6,7},{7,6},{8,9},{9,8},{10,11... | collective-permute-start | bytes 392 | tf_op jit(solution)/shard_map/ppermute | solution.py:86
  83.5 22.8 %collective-permute-start.6 = (f32[2,16]{1,0:T(2,128)S(1)}, f32[2,16]{1,0:T(2,128)S(1)}, u32[]{:S(2)}, u32[]{:S(2)}) collective-permute-start(f32[2,16]{1,0:T(2,128)S(1)} %get-tuple-element.16), channel_id=1, source_target_pairs={{0,64},{64,128},{128,192},{192,256},{256,320},{320,384},{384,448},... | collective-permute-start | bytes 392 | tf_op jit(solution)/shard_map/ppermute | solution.py:92
  87.4 26.6 %collective-permute-start.7 = (f32[2,16]{1,0:T(2,128)S(1)}, f32[2,16]{1,0:T(2,128)S(1)}, u32[]{:S(2)}, u32[]{:S(2)}) collective-permute-start(f32[2,16]{1,0:T(2,128)S(1)} %get-tuple-element.16), channel_id=1, source_target_pairs={{0,128},{64,192},{128,256},{192,320},{256,384},{320,448},{384,512}... | collective-permute-start | bytes 392 | tf_op jit(solution)/shard_map/ppermute | solution.py:92
  91.7 28.7 %collective-permute-start.8 = (f32[2,16]{1,0:T(2,128)S(1)}, f32[2,16]{1,0:T(2,128)S(1)}, u32[]{:S(2)}, u32[]{:S(2)}) collective-permute-start(f32[2,16]{1,0:T(2,128)S(1)} %get-tuple-element.16), channel_id=1, source_target_pairs={{0,192},{64,256},{128,320},{192,384},{256,448},{320,512},{384,576}... | collective-permute-start | bytes 392 | tf_op jit(solution)/shard_map/ppermute | solution.py:92
  98.1 24.3 %collective-permute-start.9 = (f32[2,16]{1,0:T(2,128)S(1)}, f32[2,16]{1,0:T(2,128)S(1)}, u32[]{:S(2)}, u32[]{:S(2)}) collective-permute-start(f32[2,16]{1,0:T(2,128)S(1)} %get-tuple-element.16), channel_id=1, source_target_pairs={{0,256},{64,320},{128,384},{192,448},{256,512},{320,576},{384,640}... | collective-permute-start | bytes 392 | tf_op jit(solution)/shard_map/ppermute | solution.py:92
  101.2 27.5 %collective-permute-start.10 = (f32[2,16]{1,0:T(2,128)S(1)}, f32[2,16]{1,0:T(2,128)S(1)}, u32[]{:S(2)}, u32[]{:S(2)}) collective-permute-start(f32[2,16]{1,0:T(2,128)S(1)} %get-tuple-element.16), channel_id=1, source_target_pairs={{0,320},{64,384},{128,448},{192,512},{256,576},{320,640},{384,704}... | collective-permute-start | bytes 392 | tf_op jit(solution)/shard_map/ppermute | solution.py:92
  106.3 26.6 %collective-permute-start.11 = (f32[2,16]{1,0:T(2,128)S(1)}, f32[2,16]{1,0:T(2,128)S(1)}, u32[]{:S(2)}, u32[]{:S(2)}) collective-permute-start(f32[2,16]{1,0:T(2,128)S(1)} %get-tuple-element.16), channel_id=1, source_target_pairs={{0,384},{64,448},{128,512},{192,576},{256,640},{320,704},{384,0},{... | collective-permute-start | bytes 392 | tf_op jit(solution)/shard_map/ppermute | solution.py:92
  114.0 22.4 %collective-permute-start.12 = (f32[2,16]{1,0:T(2,128)S(1)}, f32[2,16]{1,0:T(2,128)S(1)}, u32[]{:S(2)}, u32[]{:S(2)}) collective-permute-start(f32[2,16]{1,0:T(2,128)S(1)} %get-tuple-element.16), channel_id=1, source_target_pairs={{0,448},{64,512},{128,576},{192,640},{256,704},{320,0},{384,64},{4... | collective-permute-start | bytes 392 | tf_op jit(solution)/shard_map/ppermute | solution.py:92
  120.4 16.0 %collective-permute-start.13 = (f32[2,16]{1,0:T(2,128)S(1)}, f32[2,16]{1,0:T(2,128)S(1)}, u32[]{:S(2)}, u32[]{:S(2)}) collective-permute-start(f32[2,16]{1,0:T(2,128)S(1)} %get-tuple-element.16), channel_id=1, source_target_pairs={{0,512},{64,576},{128,640},{192,704},{256,0},{320,64},{384,128},{4... | collective-permute-start | bytes 392 | tf_op jit(solution)/shard_map/ppermute | solution.py:92
  122.4 14.0 %collective-permute-start.14 = (f32[2,16]{1,0:T(2,128)S(1)}, f32[2,16]{1,0:T(2,128)S(1)}, u32[]{:S(2)}, u32[]{:S(2)}) collective-permute-start(f32[2,16]{1,0:T(2,128)S(1)} %get-tuple-element.16), channel_id=1, source_target_pairs={{0,576},{64,640},{128,704},{192,0},{256,64},{320,128},{384,192},{4... | collective-permute-start | bytes 392 | tf_op jit(solution)/shard_map/ppermute | solution.py:92
  128.7 7.8 %collective-permute-start.15 = (f32[2,16]{1,0:T(2,128)S(1)}, f32[2,16]{1,0:T(2,128)S(1)}, u32[]{:S(2)}, u32[]{:S(2)}) collective-permute-start(f32[2,16]{1,0:T(2,128)S(1)} %get-tuple-element.16), channel_id=1, source_target_pairs={{0,640},{64,704},{128,0},{192,64},{256,128},{320,192},{384,256},{4... | collective-permute-start | bytes 392 | tf_op jit(solution)/shard_map/ppermute | solution.py:92
  133.0 5.5 %collective-permute-start.16 = (f32[2,16]{1,0:T(2,128)S(1)}, f32[2,16]{1,0:T(2,128)S(1)}, u32[]{:S(2)}, u32[]{:S(2)}) collective-permute-start(f32[2,16]{1,0:T(2,128)S(1)} %get-tuple-element.16), channel_id=1, source_target_pairs={{0,704},{64,0},{128,64},{192,128},{256,192},{320,256},{384,320},{4... | collective-permute-start | bytes 392 | tf_op jit(solution)/shard_map/ppermute | solution.py:92
  (9 other events, 15.3 us)

commit v6 on v5

--- a/solution.py
+++ b/solution.py
@@ -85,14 +85,10 @@
         pairs = [(i, i ^ bit) for i in range(grp_count)]
         current = keep + lax.ppermute(send, "grp", pairs)
         bit //= 2
-    enc_rank = lax.axis_index("enc")
-    gathered = [current]
-    for shift in range(1, enc_count):
-        pairs = [(i, (i + shift) % enc_count) for i in range(enc_count)]
-        gathered.append(lax.ppermute(current, "enc", pairs))
-    stacked = jnp.stack(gathered)
-    source_order = (enc_rank - jnp.arange(enc_count, dtype=jnp.int32)) % enc_count
-    return jnp.sum(jnp.take(stacked, source_order, axis=0, mode="clip"), axis=0)
+    current = current + 0.0
+    by_enc = jnp.broadcast_to(current[None], (enc_count,) + current.shape)
+    by_enc = lax.all_to_all(by_enc, "enc", split_axis=0, concat_axis=0, tiled=True)
+    return jnp.sum(by_enc, axis=0)
 
 
 def send_slots(own_plan, enc_count, per_slot):

time: 142 us -> 151 us (1.063)
  the two profiles are of different devices: /device:TPU:52 before, /device:TPU:2 now
where the time goes in v6:
time: 151 us; the launch traced here: 150 us
  waiting for transfers between devices  64.7 us (43%)
  starting transfers between devices  41.7 us (28%)
  local copies, waits for them, and re-layouts  19.2 us (13%)
  other arithmetic  11.4 us (8%)
  matrix products  11.2 us (7%)
    all_to_all x1, waiting for transfers between devices, local_body(): lax.all_to_all(packed, 'enc', split_axis=0, concat_axis=0, tiled=True)  44.4 us
    ppermute x6, starting transfers between devices, reduce_gain_terms(): current = keep + lax.ppermute(send, 'grp', pairs)  24.5 us
    all_to_all x1, starting transfers between devices, reduce_gain_terms(): lax.all_to_all(by_enc, 'enc', split_axis=0, concat_axis=0, tiled=True)  13.5 us
    ppermute x6, waiting for transfers between devices, reduce_gain_terms(): current = keep + lax.ppermute(send, 'grp', pairs)  11.9 us
    all_to_all x1, waiting for transfers between devices, reduce_gain_terms(): lax.all_to_all(by_enc, 'enc', split_axis=0, concat_axis=0, tiled=True)  8.44 us
    unnamed x42, local copies, waits for them, and re-layouts  4.98 us
    convert_element_type x2, local copies, waits for them, and re-layouts, block_grads(): d_value.reshape(flat).astype(jnp.bfloat16)  4.3 us
    all_to_all x1, starting transfers between devices, local_body(): lax.all_to_all(packed, 'enc', split_axis=0, concat_axis=0, tiled=True)  3.7 us
  transfers between devices with their start and end apart: 8, of which 7 were waited for; matrix products, arithmetic and copies ran while one was open for 14% of the time, Pallas kernels for 0%

profile of v6, /device:TPU:2, one launch (start us, length us, event | category | flops | bytes accessed | tf_op | source)
XLA Modules:
  0.0 149.6 jit_solution(7269537331589510791)
XLA Ops:
  0.7 2.1 %copy.36 = bf16[192,1024]{0,1:T(8,128)(2,1)} copy(bf16[192,1024]{1,0:T(8,128)(2,1)} %param.10) | data formatting | bytes 786432 | tf_op args[3]
  2.8 1.2 copy.34
  13.8 3.7 %multiply_reduce_fusion.1 = (f32[16,64]{1,0:T(8,128)S(1)}, f32[192,16]{0,1:T(8,128)}, f32[192,16]{0,1:T(8,128)}, f32[192,16]{0,1:T(8,128)}, f32[192,16]{0,1:T(8,...) fusion(f32[192,16,64]{0,2,1:T(8,128)S(1)} %get-tuple-element.25, f32[192]{0:T(256)S(1)} %mul.170, ...), kind=kOutput, calls=%fused_computation.19 | convolution fusion | flops 78628864 | bytes 4391680 | tf_op jit(solution)/shard_map/hij,jhd->ihd/dot_general | solution.py:61
  18.2 7.7 %collective-permute-start = (f32[2,512]{1,0:T(2,128)}, f32[2,512]{1,0:T(2,128)}, u32[]{:S(2)}, u32[]{:S(2)}) collective-permute-start(f32[2,512]{1,0:T(2,128)} %broadcast_select_fusion), channel_id=1, source_target_pairs={{0,32},{1,33},{2,34},{3,35},{4,36},{5,37},{6,38},{7,39},{8,40},{9,... | collective-permute-start | bytes 12296 | tf_op jit(solution)/shard_map/ppermute | solution.py:86
  25.9 3.6 %fusion.4 = bf16[192,16,64]{0,2,1:T(8,128)(2,1)} fusion(bf16[192,16,64]{0,2,1:T(8,128)(2,1)} %bitcast.44, f32[16,192,192]{1,2,0:T(8,128)} %copy-done.4, f32[16,192]{1,0:T(8,128)S(1)} %get-tuple-element.22, pred[192,192]{0,1:T(8,128)(4,1)S(1)} %compare_and_fusion), kind=kOutput, calls=%fused_computation.12 | convolution fusion | flops 78053376 | bytes 3194880 | tf_op jit(solution)/shard_map/hij,ihd->jhd/dot_general | solution.py:56
  29.6 2.5 %copy.45 = bf16[192,16,64]{2,1,0:T(8,128)(2,1)} copy(bf16[192,16,64]{0,2,1:T(8,128)(2,1)} %fusion.4) | data formatting | bytes 786432 | tf_op jit(solution)/shard_map/convert_element_type | solution.py:69
  32.1 1.8 %convert_element_type.85 = bf16[12,16,1024]{2,1,0:T(8,128)(2,1)S(1)} reshape(bf16[192,16,64]{2,1,0:T(8,128)(2,1)} %copy.45) | data formatting | bytes 786432 | tf_op jit(solution)/shard_map/convert_element_type | solution.py:69
  35.3 1.8 %multiply_convert_fusion.1 = bf16[192,16,64]{0,2,1:T(8,128)(2,1)} fusion(f32[192,16,64]{0,2,1:T(8,128)S(1)} %copy-done.1, f32[192,16,64]{0,2,1:T(8,128)S(1)} %convolution_bitcast_fusion.1, f32[192,16]{0,1:T(8,128)S(1)} %broadcast_multiply_fusion, f32[192,16]{0,1:T(8,128)S(1)} %broadcast_multiply_fusion.1, f32[16,64]{1,0:T(8,128)S(1)} %mul.144, ...), kind=kLoop, calls=%fused_computation.20 | loop fusion | flops 1179648 | bytes 2007040 | tf_op jit(solution)/shard_map/convert_element_type | solution.py:68
  37.1 1.8 %copy.43 = bf16[192,16,64]{2,1,0:T(8,128)(2,1)S(1)} copy(bf16[192,16,64]{0,2,1:T(8,128)(2,1)} %multiply_convert_fusion.1) | data formatting | bytes 786432 | tf_op jit(solution)/shard_map/convert_element_type | solution.py:68
  38.9 1.3 convert_element_type.82
  45.1 2.7 %collective-permute-start.1 = (f32[2,256]{1,0:T(2,128)S(1)}, f32[2,256]{1,0:T(2,128)S(1)}, u32[]{:S(2)}, u32[]{:S(2)}) collective-permute-start(f32[2,256]{1,0:T(2,128)S(1)} %broadcast_select_fusion.1), channel_id=1, source_target_pairs={{0,16},{1,17},{2,18},{3,19},{4,20},{5,21},{6,22},{7,23},{8,24},{9,... | collective-permute-start | bytes 6152 | tf_op jit(solution)/shard_map/ppermute | solution.py:86
  47.8 3.6 %collective-permute-done.1 = f32[2,256]{1,0:T(2,128)S(1)} collective-permute-done((f32[2,256]{1,0:T(2,128)S(1)}, f32[2,256]{1,0:T(2,128)S(1)}, u32[]{:S(2)}, u32[]{:S(2)}) %collective-permute-start.1) | collective-permute-done | bytes 2080 | tf_op jit(solution)/shard_map/ppermute | solution.py:86
  51.5 2.6 %collective-permute-start.2 = (f32[2,128]{1,0:T(2,128)S(1)}, f32[2,128]{1,0:T(2,128)S(1)}, u32[]{:S(2)}, u32[]{:S(2)}) collective-permute-start(f32[2,128]{1,0:T(2,128)S(1)} %broadcast_select_fusion.2), channel_id=1, source_target_pairs={{0,8},{1,9},{2,10},{3,11},{4,12},{5,13},{6,14},{7,15},{8,0},{9,1},... | collective-permute-start | bytes 3080 | tf_op jit(solution)/shard_map/ppermute | solution.py:86
  54.1 2.8 %collective-permute-done.2 = f32[2,128]{1,0:T(2,128)S(1)} collective-permute-done((f32[2,128]{1,0:T(2,128)S(1)}, f32[2,128]{1,0:T(2,128)S(1)}, u32[]{:S(2)}, u32[]{:S(2)}) %collective-permute-start.2) | collective-permute-done | bytes 1056 | tf_op jit(solution)/shard_map/ppermute | solution.py:86
  57.0 4.0 %collective-permute-start.3 = (f32[2,64]{1,0:T(2,128)S(1)}, f32[2,64]{1,0:T(2,128)S(1)}, u32[]{:S(2)}, u32[]{:S(2)}) collective-permute-start(f32[2,64]{1,0:T(2,128)S(1)} %broadcast_select_fusion.3), channel_id=1, source_target_pairs={{0,4},{1,5},{2,6},{3,7},{4,0},{5,1},{6,2},{7,3},{8,12},{9,13},{10,... | collective-permute-start | bytes 1544 | tf_op jit(solution)/shard_map/ppermute | solution.py:86
  61.1 2.9 %collective-permute-done.3 = f32[2,64]{1,0:T(2,128)S(1)} collective-permute-done((f32[2,64]{1,0:T(2,128)S(1)}, f32[2,64]{1,0:T(2,128)S(1)}, u32[]{:S(2)}, u32[]{:S(2)}) %collective-permute-start.3) | collective-permute-done | bytes 544 | tf_op jit(solution)/shard_map/ppermute | solution.py:86
  64.1 5.6 %collective-permute-start.4 = (f32[2,32]{1,0:T(2,128)S(1)}, f32[2,32]{1,0:T(2,128)S(1)}, u32[]{:S(2)}, u32[]{:S(2)}) collective-permute-start(f32[2,32]{1,0:T(2,128)S(1)} %broadcast_select_fusion.4), channel_id=1, source_target_pairs={{0,2},{1,3},{2,0},{3,1},{4,6},{5,7},{6,4},{7,5},{8,10},{9,11},{10,... | collective-permute-start | bytes 776 | tf_op jit(solution)/shard_map/ppermute | solution.py:86
  69.8 1.5 %collective-permute-done.4 = f32[2,32]{1,0:T(2,128)S(1)} collective-permute-done((f32[2,32]{1,0:T(2,128)S(1)}, f32[2,32]{1,0:T(2,128)S(1)}, u32[]{:S(2)}, u32[]{:S(2)}) %collective-permute-start.4) | collective-permute-done | bytes 288 | tf_op jit(solution)/shard_map/ppermute | solution.py:86
  71.4 1.9 %collective-permute-start.5 = (f32[2,16]{1,0:T(2,128)S(1)}, f32[2,16]{1,0:T(2,128)S(1)}, u32[]{:S(2)}, u32[]{:S(2)}) collective-permute-start(f32[2,16]{1,0:T(2,128)S(1)} %broadcast_select_fusion.5), channel_id=1, source_target_pairs={{0,1},{1,0},{2,3},{3,2},{4,5},{5,4},{6,7},{7,6},{8,9},{9,8},{10,11... | collective-permute-start | bytes 392 | tf_op jit(solution)/shard_map/ppermute | solution.py:86
  75.2 13.5 %all-to-all-start.1 = ((f32[12,2,16]{2,1,0:T(2,128)}), f32[12,2,16]{2,1,0:T(2,128)S(1)}, u32[]{:S(2)}, u32[]{:S(2)}) async-start(f32[12,2,16]{2,1,0:T(2,128)} %broadcast_in_dim.40), calls=%async_computation.1 | async-start | bytes 24576 | tf_op jit(solution)/shard_map/all_to_all | solution.py:90
  88.6 1.7 %gather_fusion = bf16[12,16,3072]{2,1,0:T(8,128)(2,1)} fusion(bf16[12,16,3072]{2,1,0:T(8,128)(2,1)S(1)} %pad_maximum_fusion, s32[1024]{0:T(1024)S(1)} %pad_clamp_fusion.1), kind=kCustom, calls=%fused_computation | custom fusion | bytes 2359344 | tf_op jit(solution)/shard_map/jit(_take)/gather | solution.py:147
  90.3 8.4 %all-to-all-done.1 = f32[12,2,16]{2,1,0:T(2,128)S(1)} async-done(((f32[12,2,16]{2,1,0:T(2,128)}), f32[12,2,16]{2,1,0:T(2,128)S(1)}, u32[]{:S(2)}, u32[]{:S(2)}) %all-to-all-start.1) | async-done | bytes 1568 | tf_op jit(solution)/shard_map/all_to_all | solution.py:90
  98.8 3.7 %all-to-all-start = ((bf16[12,16,3072]{2,1,0:T(8,128)(2,1)}), bf16[12,16,3072]{2,1,0:T(8,128)(2,1)S(1)}, u32[]{:S(2)}, u32[]{:S(2)}) async-start(bf16[12,16,3072]{2,1,0:T(8,128)(2,1)} %gather_fusion), calls=%async_computation | async-start | bytes 2359296 | tf_op jit(solution)/shard_map/all_to_all | solution.py:148
  103.7 44.4 %all-to-all-done = bf16[12,16,3072]{2,1,0:T(8,128)(2,1)S(1)} async-done(((bf16[12,16,3072]{2,1,0:T(8,128)(2,1)}), bf16[12,16,3072]{2,1,0:T(8,128)(2,1)S(1)}, u32[]{:S(2)}, u32[]{:S(2)}) %all-to-all-start) | async-done | bytes 1179680 | tf_op jit(solution)/shard_map/all_to_all | solution.py:148
  (105 shorter events, 21.5 us)
Async XLA Ops:
  0.6 3.7 %copy-start.9 = (bf16[192,1024]{1,0:T(8,128)(2,1)S(1)}, bf16[192,1024]{1,0:T(8,128)(2,1)}, u32[]{:S(2)}) copy-start(bf16[192,1024]{1,0:T(8,128)(2,1)} %param.8) | copy-start | bytes 1179652
  4.1 1.9 %copy-start.19 = (s32[192]{0:T(256)S(1)}, s32[192]{0:T(256)}, u32[]{:S(2)}) copy-start(s32[192]{0:T(256)} %param.11) | copy-start | bytes 2308
  4.4 2.2 %copy-start.10 = (f32[192,16]{0,1:T(8,128)}, f32[192,16]{0,1:T(8,128)S(1)}, u32[]{:S(2)}) copy-start(f32[192,16]{0,1:T(8,128)S(1)} %add_rsqrt_fusion.1) | copy-start | bytes 36868
  4.9 2.9 %copy-start.11 = (f32[192,16]{0,1:T(8,128)}, f32[192,16]{0,1:T(8,128)S(1)}, u32[]{:S(2)}) copy-start(f32[192,16]{0,1:T(8,128)S(1)} %add_rsqrt_fusion) | copy-start | bytes 36868
  6.5 2.5 %copy-start = (f32[192,16,64]{0,2,1:T(8,128)}, f32[192,16,64]{0,2,1:T(8,128)S(1)}, u32[]{:S(2)}) copy-start(f32[192,16,64]{0,2,1:T(8,128)S(1)} %get-tuple-element.26) | copy-start | bytes 2359300
  6.6 1.6 %copy-start.7 = (bf16[192,1024]{0,1:T(8,128)(2,1)S(1)}, bf16[192,1024]{0,1:T(8,128)(2,1)}, u32[]{:S(2)}) copy-start(bf16[192,1024]{0,1:T(8,128)(2,1)} %copy.37) | copy-start | bytes 1179652
  7.8 1.7 %copy-start.4 = (f32[16,192,192]{1,2,0:T(8,128)}, f32[16,192,192]{1,2,0:T(8,128)S(1)}, u32[]{:S(2)}) copy-start(f32[16,192,192]{1,2,0:T(8,128)S(1)} %get-tuple-element.23) | copy-start | bytes 7077892
  11.8 2.0 %copy-start.1 = (f32[192,16,64]{0,2,1:T(8,128)S(1)}, f32[192,16,64]{0,2,1:T(8,128)}, u32[]{:S(2)}) copy-start(f32[192,16,64]{0,2,1:T(8,128)} %copy-done) | copy-start | bytes 2359300
  17.5 12.0 %copy-start.12 = (f32[1,1024]{1,0:T(1,128)}, f32[1,1024]{1,0:T(1,128)S(1)}, u32[]{:S(2)}) copy-start(f32[1,1024]{1,0:T(1,128)S(1)} %stack_reshape.7) | copy-start | bytes 12292
  17.6 12.0 %copy-start.14 = (f32[1,1024]{1,0:T(1,128)}, f32[1,1024]{1,0:T(1,128)S(1)}, u32[]{:S(2)}) copy-start(f32[1,1024]{1,0:T(1,128)S(1)} %stack_reshape.6) | copy-start | bytes 12292
  18.2 26.1 %collective-permute-start = (f32[2,512]{1,0:T(2,128)}, f32[2,512]{1,0:T(2,128)}, u32[]{:S(2)}, u32[]{:S(2)}) collective-permute-start(f32[2,512]{1,0:T(2,128)} %broadcast_select_fusion), channel_id=1, source_target_pairs={{0,32},{1,33},{2,34},{3,35},{4,36},{5,37},{6,38},{7,39},{8,40},{9,... | collective-permute-start | bytes 12296 | tf_op jit(solution)/shard_map/ppermute | solution.py:86
  37.1 4.6 %copy-start.3 = (f32[192,16,64]{0,2,1:T(8,128)S(1)}, f32[192,16,64]{0,2,1:T(8,128)}, u32[]{:S(2)}) copy-start(f32[192,16,64]{0,2,1:T(8,128)} %get-tuple-element.24) | copy-start | bytes 2359300
  38.9 5.0 %copy-start.18 = (s32[12]{0:T(128)S(1)}, s32[12]{0:T(128)}, u32[]{:S(2)}) copy-start(s32[12]{0:T(128)} %get-tuple-element.16) | copy-start | bytes 148
  40.2 3.8 %copy-start.5 = (bf16[12,16,1024]{2,1,0:T(8,128)(2,1)S(1)}, bf16[12,16,1024]{2,1,0:T(8,128)(2,1)}, u32[]{:S(2)}) copy-start(bf16[12,16,1024]{2,1,0:T(8,128)(2,1)} %convert_element_type.82) | copy-start | bytes 1179652
  41.7 2.6 %copy-start.13 = (f32[1,1024]{1,0:T(1,128)S(1)}, f32[1,1024]{1,0:T(1,128)}, u32[]{:S(2)}) copy-start(f32[1,1024]{1,0:T(1,128)} %copy-done.12) | copy-start | bytes 12292
  41.7 2.6 %copy-start.15 = (f32[1,1024]{1,0:T(1,128)S(1)}, f32[1,1024]{1,0:T(1,128)}, u32[]{:S(2)}) copy-start(f32[1,1024]{1,0:T(1,128)} %copy-done.14) | copy-start | bytes 12292
  44.0 58.4 %copy-start.17 = (s32[1,12,12]{2,0,1:T(1,128)S(1)}, s32[1,12,12]{2,0,1:T(1,128)}, u32[]{:S(2)}) copy-start(s32[1,12,12]{2,0,1:T(1,128)} %param.12) | copy-start | bytes 1732
  45.1 6.4 %collective-permute-start.1 = (f32[2,256]{1,0:T(2,128)S(1)}, f32[2,256]{1,0:T(2,128)S(1)}, u32[]{:S(2)}, u32[]{:S(2)}) collective-permute-start(f32[2,256]{1,0:T(2,128)S(1)} %broadcast_select_fusion.1), channel_id=1, source_target_pairs={{0,16},{1,17},{2,18},{3,19},{4,20},{5,21},{6,22},{7,23},{8,24},{9,... | collective-permute-start | bytes 6152 | tf_op jit(solution)/shard_map/ppermute | solution.py:86
  51.5 5.5 %collective-permute-start.2 = (f32[2,128]{1,0:T(2,128)S(1)}, f32[2,128]{1,0:T(2,128)S(1)}, u32[]{:S(2)}, u32[]{:S(2)}) collective-permute-start(f32[2,128]{1,0:T(2,128)S(1)} %broadcast_select_fusion.2), channel_id=1, source_target_pairs={{0,8},{1,9},{2,10},{3,11},{4,12},{5,13},{6,14},{7,15},{8,0},{9,1},... | collective-permute-start | bytes 3080 | tf_op jit(solution)/shard_map/ppermute | solution.py:86
  57.0 7.0 %collective-permute-start.3 = (f32[2,64]{1,0:T(2,128)S(1)}, f32[2,64]{1,0:T(2,128)S(1)}, u32[]{:S(2)}, u32[]{:S(2)}) collective-permute-start(f32[2,64]{1,0:T(2,128)S(1)} %broadcast_select_fusion.3), channel_id=1, source_target_pairs={{0,4},{1,5},{2,6},{3,7},{4,0},{5,1},{6,2},{7,3},{8,12},{9,13},{10,... | collective-permute-start | bytes 1544 | tf_op jit(solution)/shard_map/ppermute | solution.py:86
  64.1 7.2 %collective-permute-start.4 = (f32[2,32]{1,0:T(2,128)S(1)}, f32[2,32]{1,0:T(2,128)S(1)}, u32[]{:S(2)}, u32[]{:S(2)}) collective-permute-start(f32[2,32]{1,0:T(2,128)S(1)} %broadcast_select_fusion.4), channel_id=1, source_target_pairs={{0,2},{1,3},{2,0},{3,1},{4,6},{5,7},{6,4},{7,5},{8,10},{9,11},{10,... | collective-permute-start | bytes 776 | tf_op jit(solution)/shard_map/ppermute | solution.py:86
  71.4 3.0 %collective-permute-start.5 = (f32[2,16]{1,0:T(2,128)S(1)}, f32[2,16]{1,0:T(2,128)S(1)}, u32[]{:S(2)}, u32[]{:S(2)}) collective-permute-start(f32[2,16]{1,0:T(2,128)S(1)} %broadcast_select_fusion.5), channel_id=1, source_target_pairs={{0,1},{1,0},{2,3},{3,2},{4,5},{5,4},{6,7},{7,6},{8,9},{9,8},{10,11... | collective-permute-start | bytes 392 | tf_op jit(solution)/shard_map/ppermute | solution.py:86
  75.2 23.6 %all-to-all-start.1 = ((f32[12,2,16]{2,1,0:T(2,128)}), f32[12,2,16]{2,1,0:T(2,128)S(1)}, u32[]{:S(2)}, u32[]{:S(2)}) async-start(f32[12,2,16]{2,1,0:T(2,128)} %broadcast_in_dim.40), calls=%async_computation.1 | async-start | bytes 24576 | tf_op jit(solution)/shard_map/all_to_all | solution.py:90
  98.8 49.4 %all-to-all-start = ((bf16[12,16,3072]{2,1,0:T(8,128)(2,1)}), bf16[12,16,3072]{2,1,0:T(8,128)(2,1)S(1)}, u32[]{:S(2)}, u32[]{:S(2)}) async-start(bf16[12,16,3072]{2,1,0:T(8,128)(2,1)} %gather_fusion), calls=%async_computation | async-start | bytes 2359296 | tf_op jit(solution)/shard_map/all_to_all | solution.py:148
  (4 other events, 4.5 us)

commit v7 on v3

--- a/solution.py
+++ b/solution.py
@@ -78,8 +78,11 @@
     )
 
 
+GROUP_ROWS = 64
+
+
 def normalize_rows(rows, gain_row):
-    values = rows.astype(jnp.float32).reshape(rows.shape[0], HEADS, HD)
+    values = rows.astype(jnp.float32).reshape(rows.shape[:-1] + (HEADS, HD))
     centred = values - jnp.mean(values, -1, keepdims=True)
     inv_scale = lax.rsqrt(jnp.mean(centred * centred, -1, keepdims=True) + epsilon)
     normed = centred * inv_scale
@@ -93,35 +96,42 @@
         - jnp.mean(d_norm, -1, keepdims=True)
         - normed * jnp.mean(d_norm * normed, -1, keepdims=True)
     )
-    gain_term = jnp.sum(d_hat * normed * live_rows[:, None, None], 0)
+    gain_term = jnp.sum(d_hat * normed * live_rows[..., None, None], (0, 1))
     return (d_input, gain_term.reshape(-1))
 
 
 def block_grads(query_rows, key_rows, value_rows, cotangent, piece_of, image_num, gains, live_rows):
     rows = query_rows.shape[0]
-    three = (rows, HEADS, HD)
+    groups = rows // GROUP_ROWS
+    grouped = (groups, GROUP_ROWS, HEADS * HD)
+    four = (groups, GROUP_ROWS, HEADS, HD)
     gain_query = gains[0].reshape(HEADS, HD)
     gain_key = gains[1].reshape(HEADS, HD)
-    q_norm, q_scale, q_hat = normalize_rows(query_rows, gain_query)
-    k_norm, k_scale, k_hat = normalize_rows(key_rows, gain_key)
-    values = value_rows.reshape(three)
-    cot = cotangent.reshape(three)
+    q_norm, q_scale, q_hat = normalize_rows(query_rows.reshape(grouped), gain_query)
+    k_norm, k_scale, k_hat = normalize_rows(key_rows.reshape(grouped), gain_key)
+    values = value_rows.reshape(four)
+    cot = cotangent.reshape(four)
+    piece_of = piece_of.reshape(groups, GROUP_ROWS)
+    image_num = image_num.reshape(groups, GROUP_ROWS)
+    live_rows = live_rows.reshape(groups, GROUP_ROWS)
     factor = HD ** (-0.5)
     f32 = jnp.float32
-    scores = jnp.einsum("ihd,jhd->hij", q_hat, k_hat, preferred_element_type=f32) * factor
-    same = (piece_of[:, None] == piece_of[None, :]) & (image_num[:, None] == image_num[None, :])
-    weights = jnp.where(same[None], jnp.exp(scores), 0.0)
+    scores = jnp.einsum("gihd,gjhd->ghij", q_hat, k_hat, preferred_element_type=f32) * factor
+    same = (piece_of[:, :, None] == piece_of[:, None, :]) & (
+        image_num[:, :, None] == image_num[:, None, :]
+    )
+    weights = jnp.where(same[:, None], jnp.exp(scores), 0.0)
     probs = weights / jnp.sum(weights, -1, keepdims=True)
     probs_b = probs.astype(jnp.bfloat16)
-    attended = jnp.einsum("hij,jhd->ihd", probs_b, values, preferred_element_type=f32)
+    attended = jnp.einsum("ghij,gjhd->gihd", probs_b, values, preferred_element_type=f32)
     row_delta = jnp.sum(cot.astype(f32) * attended, -1)
-    d_value = jnp.einsum("hij,ihd->jhd", probs_b, cot, preferred_element_type=f32)
-    d_prob = jnp.einsum("ihd,jhd->hij", cot, values, preferred_element_type=f32)
-    d_score = (probs * (d_prob - jnp.transpose(row_delta)[..., None]) * factor).astype(
-        jnp.bfloat16
-    )
-    d_qhat = jnp.einsum("hij,jhd->ihd", d_score, k_hat, preferred_element_type=f32)
-    d_khat = jnp.einsum("hij,ihd->jhd", d_score, q_hat, preferred_element_type=f32)
+    d_value = jnp.einsum("ghij,gihd->gjhd", probs_b, cot, preferred_element_type=f32)
+    d_prob = jnp.einsum("gihd,gjhd->ghij", cot, values, preferred_element_type=f32)
+    d_score = (
+        probs * (d_prob - jnp.transpose(row_delta, (0, 2, 1))[..., None]) * factor
+    ).astype(jnp.bfloat16)
+    d_qhat = jnp.einsum("ghij,gjhd->gihd", d_score, k_hat, preferred_element_type=f32)
+    d_khat = jnp.einsum("ghij,gihd->gjhd", d_score, q_hat, preferred_element_type=f32)
     d_query, term_query = row_norm_back(d_qhat, q_norm, q_scale, gain_query, live_rows)
     d_key, term_key = row_norm_back(d_khat, k_norm, k_scale, gain_key, live_rows)
     flat = (rows, HEADS * HD)
@@ -131,7 +141,6 @@
         d_value.reshape(flat).astype(jnp.bfloat16),
         jnp.stack([term_query, term_key]),
     )
-
 
 def send_slots(own_plan, enc_count, per_slot):
     owner_hit = (own_plan[:, None] == jnp.arange(enc_count, dtype=jnp.int32)[None, :]).astype(

time: 104 us -> 118 us (1.13)
  local copies, waits for them, and re-layouts: 16.1 us -> 25.9 us
  other arithmetic: 5.07 us -> 7.47 us
  matrix products: 9.75 us -> 11.6 us
    reshape x2 -> x4, local copies, waits for them, and re-layouts: 1.4 us -> 9.97 us  [the longest x2 4.98 us: block_grads(): cot = cotangent.reshape(four)]
    convert_element_type x0 -> x5, local copies, waits for them, and re-layouts: none -> 5.81 us  [the longest x4 5.72 us: normalize_rows(): values = rows.astype(jnp.float32).reshape(rows.shape[:-1] + (HEADS, HD))]
    unnamed x22, local copies, waits for them, and re-layouts: 4.77 us -> 1.94 us
    div x0 -> x1, matrix products: none -> 2.27 us  [block_grads(): probs = weights / jnp.sum(weights, -1, keepdims=True)]
    convert_element_type x1, other arithmetic: 1.16 us -> 3.13 us  [block_grads(): d_key.reshape(flat).astype(jnp.bfloat16)]
    dot_general x6 -> x5, matrix products: 9.75 us -> 9.35 us  [the longest x1 3.08 us: block_grads(): jnp.einsum('ghij,gihd->gjhd', probs_b, cot, preferred_element_type=f32)]
  transfers between devices with their start and end apart: 2 -> 2, of which waited for: 1 -> 1; matrix products, arithmetic and copies ran while one was open for 11% -> 10% of each run, Pallas kernels for 0% -> 0%
where the time goes in v7:
time: 118 us
  waiting for transfers between devices  46.3 us (39%)
  local copies, waits for them, and re-layouts  25.9 us (22%)
  starting transfers between devices  25.4 us (22%)
  matrix products  11.6 us (10%)
  other arithmetic  7.47 us (6%)
    all_to_all x1, waiting for transfers between devices, local(): lax.all_to_all(packed, 'enc', split_axis=0, concat_axis=0, tiled=True)  46.3 us
    all_to_all x1, starting transfers between devices, local(): lax.all_to_all(packed, 'enc', split_axis=0, concat_axis=0, tiled=True)  14.8 us
    all_to_all x1, starting transfers between devices, local(): lax.all_to_all(by_grp, 'grp', split_axis=0, concat_axis=0, tiled=True)  10.7 us
    convert_element_type x4, local copies, waits for them, and re-layouts, normalize_rows(): values = rows.astype(jnp.float32).reshape(rows.shape[:-1] + (HEADS, HD))  5.72 us
    reshape x2, local copies, waits for them, and re-layouts, block_grads(): cot = cotangent.reshape(four)  4.98 us
    reshape x2, local copies, waits for them, and re-layouts, block_grads(): values = value_rows.reshape(four)  4.98 us
    convert_element_type x1, other arithmetic, block_grads(): d_key.reshape(flat).astype(jnp.bfloat16)  3.13 us
    dot_general x1, matrix products, block_grads(): jnp.einsum('ghij,gihd->gjhd', probs_b, cot, preferred_element_type=f32)  3.08 us
  transfers between devices with their start and end apart: 2, of which 1 were waited for; matrix products, arithmetic and copies ran while one was open for 10% of the time, Pallas kernels for 0%

profile of v7, /device:TPU:66, one launch (start us, length us, event | category | flops | bytes accessed | tf_op | source)
XLA Modules:
  0.0 117.8 jit_solution(1092619935425801776)
XLA Ops:
  0.6 1.6 %reshape.173 = f32[3,64,16,64]{3,2,1,0:T(8,128)S(1)} reshape(bf16[192,1024]{1,0:T(8,128)(2,1)} %param.7) | data formatting | bytes 1179648 | tf_op jit(solution)/shard_map/convert_element_type | solution.py:85
  2.2 0.6 copy.129
  3.3 1.6 %reshape.174 = f32[3,64,16,64]{3,2,1,0:T(8,128)S(1)} reshape(bf16[192,1024]{1,0:T(8,128)(2,1)} %param.8) | data formatting | bytes 1179648 | tf_op jit(solution)/shard_map/convert_element_type | solution.py:85
  4.9 1.1 copy-done.1
  6.5 2.0 %copy.131 = f32[3,64,16,64]{1,3,2,0:T(8,128)S(1)} copy(f32[3,64,16,64]{3,2,1,0:T(8,128)} %copy-done.1) | data formatting | bytes 1572864 | tf_op jit(solution)/shard_map/convert_element_type | solution.py:85
  9.2 2.4 %reshape.171 = bf16[3,64,16,64]{3,2,1,0:T(8,128)(2,1)} reshape(bf16[192,1024]{1,0:T(8,128)(2,1)} %param.9) | data formatting | bytes 786432 | tf_op jit(solution)/shard_map/reshape | solution.py:112
  11.5 2.6 %copy.138 = bf16[3,64,16,64]{1,3,2,0:T(8,128)(2,1)} copy(bf16[3,64,16,64]{3,2,1,0:T(8,128)(2,1)} %reshape.171) | data formatting | bytes 786432 | tf_op jit(solution)/shard_map/reshape | solution.py:112
  14.2 2.4 %reshape.170 = bf16[3,64,16,64]{3,2,1,0:T(8,128)(2,1)} reshape(bf16[192,1024]{1,0:T(8,128)(2,1)} %param.10) | data formatting | bytes 786432 | tf_op jit(solution)/shard_map/reshape | solution.py:113
  16.5 2.6 %copy.136 = bf16[3,64,16,64]{1,3,2,0:T(8,128)(2,1)} copy(bf16[3,64,16,64]{3,2,1,0:T(8,128)(2,1)} %reshape.170) | data formatting | bytes 786432 | tf_op jit(solution)/shard_map/reshape | solution.py:113
  20.1 2.3 %fusion.9 = f32[3,16,64,64]{2,3,1,0:T(8,128)} fusion(pred[3,64,64]{1,2,0:T(8,128)(4,1)S(1)} %compare_and_fusion, f32[3,64,16,64]{1,3,2,0:T(8,128)S(1)} %copy.131, f32[16,64]{1,0:T(8,128)S(1)} %mul.142, f32[3,64,16]{1,2,0:T(8,128)S(1)} %get-tuple-element.23, f32[3,64,16]{1,2,0:T(8,128)S(1)} %broadcast_multiply_fusion.4, f32[3,64,16,64]{1,3,2,0:T(8,128)S(1)} %copy.129, ...), kind=kOutput, calls=%fused_computation.30 | convolution fusion | flops 27331648 | bytes 2428928 | tf_op jit(solution)/shard_map/div | solution.py:124
  22.4 2.4 %fusion.4 = f32[3,64,16]{1,2,0:T(8,128)S(1)} fusion(bf16[3,64,16,64]{1,3,2,0:T(8,128)(2,1)} %copy.136, bf16[3,64,16,64]{1,3,2,0:T(8,128)(2,1)} %copy.138, f32[3,16,64,64]{2,3,1,0:T(8,128)} %fusion.9), kind=kOutput, calls=%fused_computation.11 | convolution fusion | flops 25949184 | bytes 1585152 | tf_op jit(solution)/shard_map/ghij,gjhd->gihd/dot_general | solution.py:126
  26.2 2.8 %multiply_reduce_fusion.1 = (f32[3,64,16]{1,2,0:T(8,128)S(1)}, f32[16,64]{1,0:T(8,128)S(1)}, f32[3,64,16]{1,2,0:T(8,128)S(1)}, f32[3,64,16]{1,2,0:T(8,128)S(1)},...) fusion(f32[3,64,16,64]{1,3,2,0:T(8,128)S(1)} %copy.129, f32[16,64]{1,0:T(8,128)S(1)} %mul.146, ...), kind=kOutput, calls=%fused_computation.15 | convolution fusion | flops 29476864 | bytes 3654400 | tf_op jit(solution)/shard_map/ghij,gjhd->gihd/dot_general | solution.py:133
  29.2 0.7 copy.146
  29.9 10.7 %all-to-all-start = ((f32[64,2,16]{2,1,0:T(2,128)}), f32[64,2,16]{2,1,0:T(2,128)S(1)}, u32[]{:S(2)}, u32[]{:S(2)}) async-start(f32[64,2,16]{2,1,0:T(2,128)} %copy.146), calls=%async_computation | async-start | bytes 131072 | tf_op jit(solution)/shard_map/all_to_all | solution.py:207
  40.6 3.1 %fusion.7 = bf16[3,64,16,64]{3,1,2,0:T(8,128)(2,1)} fusion(bf16[3,64,16,64]{1,3,2,0:T(8,128)(2,1)} %copy.136, f32[3,16,64,64]{2,3,1,0:T(8,128)} %fusion.9), kind=kOutput, calls=%fused_computation.27 | convolution fusion | flops 25559040 | bytes 1572864 | tf_op jit(solution)/shard_map/ghij,gihd->gjhd/dot_general | solution.py:128
  44.1 3.1 %multiply_convert_fusion = bf16[3,64,16,64]{1,3,2,0:T(8,128)(2,1)} fusion(f32[3,16,64,64]{3,2,1,0:T(8,128)} %copy-done.4, f32[3,64,16,64]{1,3,2,0:T(8,128)S(1)} %copy.131, f32[3,64,16]{1,2,0:T(8,128)S(1)} %broadcast_multiply_fusion, f32[3,64,16]{1,2,0:T(8,128)S(1)} %broadcast_multiply_fusion.1, f32[16,64]{1,0:T(8,128)S(1)} %mul.142, ...), kind=kLoop, calls=%fused_computation.12 | loop fusion | flops 1572864 | bytes 2019328 | tf_op jit(solution)/shard_map/convert_element_type | solution.py:140
  47.2 0.7 multiply_convert_fusion.1
  49.4 0.6 copy.141
  50.6 0.6 copy.143
  52.0 1.7 %gather_fusion = bf16[12,16,3200]{2,1,0:T(8,128)(2,1)} fusion(bf16[12,16,3200]{2,1,0:T(8,128)(2,1)S(1)} %pad_maximum_fusion, s32[1024]{0:T(1024)S(1)} %pad_clamp_fusion.1), kind=kCustom, calls=%fused_computation | custom fusion | bytes 2457648 | tf_op jit(solution)/shard_map/jit(_take)/gather | solution.py:216
  53.8 14.8 %all-to-all-start.1 = ((bf16[12,16,3200]{2,1,0:T(8,128)(2,1)}), bf16[12,16,3200]{2,1,0:T(8,128)(2,1)S(1)}, u32[]{:S(2)}, u32[]{:S(2)}) async-start(bf16[12,16,3200]{2,1,0:T(8,128)(2,1)} %gather_fusion), calls=%async_computation.1 | async-start | bytes 2457600 | tf_op jit(solution)/shard_map/all_to_all | solution.py:217
  69.2 46.3 %all-to-all-done.1 = bf16[12,16,3200]{2,1,0:T(8,128)(2,1)S(1)} async-done(((bf16[12,16,3200]{2,1,0:T(8,128)(2,1)}), bf16[12,16,3200]{2,1,0:T(8,128)(2,1)S(1)}, u32[]{:S(2)}, u32[]{:S(2)}) %all-to-all-start.1) | async-done | bytes 1228832 | tf_op jit(solution)/shard_map/all_to_all | solution.py:217
  116.3 0.6 gather_fusion.1
  116.9 0.9 fusion.29
  (77 shorter events, 8.6 us)
Async XLA Ops:
  4.9 1.2 copy-start.1
  6.5 2.0 %copy-start.9 = (s32[1,12,12]{2,0,1:T(1,128)S(1)}, s32[1,12,12]{2,0,1:T(1,128)}, u32[]{:S(2)}) copy-start(s32[1,12,12]{2,0,1:T(1,128)} %param.12) | copy-start | bytes 1732
  6.5 2.2 %copy-start.10 = (s32[192]{0:T(256)S(1)}, s32[192]{0:T(256)}, u32[]{:S(2)}) copy-start(s32[192]{0:T(256)} %param.11) | copy-start | bytes 2308
  6.5 2.5 %copy-start.8 = (f32[2,1024]{1,0:T(2,128)S(1)}, f32[2,1024]{1,0:T(2,128)}, u32[]{:S(2)}) copy-start(f32[2,1024]{1,0:T(2,128)} %param.13) | copy-start | bytes 24580
  22.4 2.4 %copy-start = (f32[3,16,64,64]{2,3,1,0:T(8,128)S(1)}, f32[3,16,64,64]{2,3,1,0:T(8,128)}, u32[]{:S(2)}) copy-start(f32[3,16,64,64]{2,3,1,0:T(8,128)} %fusion.9) | copy-start | bytes 2359300
  22.4 2.5 %copy-start.2 = (bf16[3,64,16,64]{1,3,2,0:T(8,128)(2,1)S(1)}, bf16[3,64,16,64]{1,3,2,0:T(8,128)(2,1)}, u32[]{:S(2)}) copy-start(bf16[3,64,16,64]{1,3,2,0:T(8,128)(2,1)} %copy.136) | copy-start | bytes 1179652
  22.4 2.8 %copy-start.3 = (bf16[3,64,16,64]{1,3,2,0:T(8,128)(2,1)S(1)}, bf16[3,64,16,64]{1,3,2,0:T(8,128)(2,1)}, u32[]{:S(2)}) copy-start(bf16[3,64,16,64]{1,3,2,0:T(8,128)(2,1)} %copy.138) | copy-start | bytes 1179652
  26.2 2.8 %copy-start.4 = (f32[3,16,64,64]{3,2,1,0:T(8,128)}, f32[3,16,64,64]{3,2,1,0:T(8,128)S(1)}, u32[]{:S(2)}) copy-start(f32[3,16,64,64]{3,2,1,0:T(8,128)S(1)} %fusion.13) | copy-start | bytes 2359300
  29.9 21.9 %all-to-all-start = ((f32[64,2,16]{2,1,0:T(2,128)}), f32[64,2,16]{2,1,0:T(2,128)S(1)}, u32[]{:S(2)}, u32[]{:S(2)}) async-start(f32[64,2,16]{2,1,0:T(2,128)} %copy.146), calls=%async_computation | async-start | bytes 131072 | tf_op jit(solution)/shard_map/all_to_all | solution.py:207
  44.1 3.1 %copy-start.7 = (f32[3,16,64,64]{3,2,1,0:T(8,128)S(1)}, f32[3,16,64,64]{3,2,1,0:T(8,128)}, u32[]{:S(2)}) copy-start(f32[3,16,64,64]{3,2,1,0:T(8,128)} %get-tuple-element.22) | copy-start | bytes 2359300
  47.2 1.1 copy-start.5
  49.4 1.2 %copy-start.6 = (bf16[3,64,16,64]{1,3,2,0:T(8,128)(2,1)S(1)}, bf16[3,64,16,64]{1,3,2,0:T(8,128)(2,1)}, u32[]{:S(2)}) copy-start(bf16[3,64,16,64]{1,3,2,0:T(8,128)(2,1)} %multiply_convert_fusion) | copy-start | bytes 1179652
  53.8 61.8 %all-to-all-start.1 = ((bf16[12,16,3200]{2,1,0:T(8,128)(2,1)}), bf16[12,16,3200]{2,1,0:T(8,128)(2,1)S(1)}, u32[]{:S(2)}, u32[]{:S(2)}) async-start(bf16[12,16,3200]{2,1,0:T(8,128)(2,1)} %gather_fusion), calls=%async_computation.1 | async-start | bytes 2457600 | tf_op jit(solution)/shard_map/all_to_all | solution.py:217

commit v8 on v3

--- a/solution.py
+++ b/solution.py
@@ -3,6 +3,8 @@
 import jax
 import jax.numpy as jnp
 from jax import lax
+from jax.experimental import pallas as pl
+from jax.experimental.pallas import tpu as pltpu
 from jax.sharding import PartitionSpec as P
 
 HEADS = 16
@@ -133,6 +135,87 @@
     )
 
 
+PAD_ROWS = 256
+
+
+def _norm(x, gain):
+    mean = jnp.mean(x, axis=1, keepdims=True)
+    centred = x - mean
+    inv_scale = lax.rsqrt(jnp.mean(centred * centred, axis=1, keepdims=True) + epsilon)
+    normed = centred * inv_scale
+    return normed, inv_scale, (normed * gain).astype(jnp.bfloat16)
+
+
+def _back(d_hat, normed, inv_scale, gain):
+    d_norm = d_hat * gain
+    return inv_scale * (
+        d_norm
+        - jnp.mean(d_norm, axis=1, keepdims=True)
+        - normed * jnp.mean(d_norm * normed, axis=1, keepdims=True)
+    )
+
+
+def _kernel(q_ref, k_ref, v_ref, c_ref, mask_ref, live_ref, gain_ref, dq_ref, dk_ref, dv_ref, gt_ref):
+    f32 = jnp.float32
+    nt = (((1,), (1,)), ((), ()))
+    factor = HD ** (-0.5)
+    attend = mask_ref[...] > 0.5
+    live = live_ref[...]
+    gt_ref[...] = jnp.zeros(gt_ref.shape, f32)
+    for head in range(HEADS):
+        cut = slice(head * HD, (head + 1) * HD)
+        gain_q = gain_ref[0:1, cut]
+        gain_k = gain_ref[1:2, cut]
+        q_norm, q_scale, q_hat = _norm(q_ref[:, cut].astype(f32), gain_q)
+        k_norm, k_scale, k_hat = _norm(k_ref[:, cut].astype(f32), gain_k)
+        values = v_ref[:, cut]
+        cot = c_ref[:, cut]
+        scores = lax.dot_general(q_hat, k_hat, nt, preferred_element_type=f32) * factor
+        weights = jnp.where(attend, jnp.exp(scores), 0.0)
+        probs = weights / jnp.sum(weights, axis=1, keepdims=True)
+        probs_b = probs.astype(jnp.bfloat16)
+        attended = jnp.dot(probs_b, values, preferred_element_type=f32)
+        row_delta = jnp.sum(cot.astype(f32) * attended, axis=1, keepdims=True)
+        probs_t = jnp.transpose(probs).astype(jnp.bfloat16)
+        dv_ref[:, cut] = jnp.dot(probs_t, cot, preferred_element_type=f32).astype(jnp.bfloat16)
+        d_prob = lax.dot_general(cot, values, nt, preferred_element_type=f32)
+        d_score_f = probs * (d_prob - row_delta) * factor
+        d_score = d_score_f.astype(jnp.bfloat16)
+        d_score_t = jnp.transpose(d_score_f).astype(jnp.bfloat16)
+        d_qhat = jnp.dot(d_score, k_hat, preferred_element_type=f32)
+        d_khat = jnp.dot(d_score_t, q_hat, preferred_element_type=f32)
+        dq_ref[:, cut] = _back(d_qhat, q_norm, q_scale, gain_q).astype(jnp.bfloat16)
+        dk_ref[:, cut] = _back(d_khat, k_norm, k_scale, gain_k).astype(jnp.bfloat16)
+        gt_ref[0:1, cut] = jnp.sum(d_qhat * q_norm * live, axis=0, keepdims=True)
+        gt_ref[1:2, cut] = jnp.sum(d_khat * k_norm * live, axis=0, keepdims=True)
+
+
+def kernel_grads(query_rows, key_rows, value_rows, cotangent, piece_of, image_num, gains, live_rows):
+    rows, feat = query_rows.shape
+    extra = PAD_ROWS - rows
+    pad = lambda a: jnp.pad(a, ((0, extra), (0, 0)))
+    piece_pad = jnp.concatenate([piece_of, -1 - jnp.arange(extra, dtype=piece_of.dtype)])
+    image_pad = jnp.pad(image_num, (0, extra))
+    same = (piece_pad[:, None] == piece_pad[None, :]) & (image_pad[:, None] == image_pad[None, :])
+    mask = same.astype(jnp.float32)
+    live = jnp.pad(live_rows, (0, extra)).reshape(PAD_ROWS, 1)
+    vmem = pltpu.MemorySpace.VMEM if hasattr(pltpu, "MemorySpace") else pltpu.VMEM
+    spec = pl.BlockSpec(memory_space=vmem)
+    out_shape = (
+        jax.ShapeDtypeStruct((PAD_ROWS, feat), jnp.bfloat16),
+        jax.ShapeDtypeStruct((PAD_ROWS, feat), jnp.bfloat16),
+        jax.ShapeDtypeStruct((PAD_ROWS, feat), jnp.bfloat16),
+        jax.ShapeDtypeStruct((8, feat), jnp.float32),
+    )
+    dq, dk, dv, gt = pl.pallas_call(
+        _kernel,
+        out_shape=out_shape,
+        in_specs=[spec] * 7,
+        out_specs=(spec, spec, spec, spec),
+    )(pad(query_rows), pad(key_rows), pad(value_rows), pad(cotangent), mask, live, gains)
+    return dq[:rows], dk[:rows], dv[:rows], gt[0:2]
+
+
 def send_slots(own_plan, enc_count, per_slot):
     owner_hit = (own_plan[:, None] == jnp.arange(enc_count, dtype=jnp.int32)[None, :]).astype(
         jnp.int32
@@ -186,7 +269,7 @@
     live_flags = (own_plan >= 0).astype(jnp.float32)
     live_rows = jnp.repeat(live_flags, PIECE)
     piece_of = jnp.repeat(jnp.arange(PMAX, dtype=jnp.int32), PIECE)
-    d_query, d_key, d_value, gain_terms = block_grads(
+    d_query, d_key, d_value, gain_terms = kernel_grads(
         query_raw, key_raw, value_rows, out_cotangent, piece_of, image_ids, gains, live_rows
     )
     d_query = d_query.reshape(piece_shape)

time: 104 us -> 129 us (1.24)
  the two profiles are of different devices: /device:TPU:66 before, /device:TPU:64 now
where the time goes in v8:
time: 129 us
  waiting for transfers between devices  54.8 us (42%)
  Pallas kernels  32.8 us (25%)
  starting transfers between devices  25.5 us (20%)
  local copies, waits for them, and re-layouts  11.6 us (9%)
  other arithmetic  3.49 us (3%)
    all_to_all x1, waiting for transfers between devices, local(): lax.all_to_all(packed, 'enc', split_axis=0, concat_axis=0, tiled=True)  46.3 us
    pallas_call x1, Pallas kernels, kernel_grads(): pl.pallas_call(_kernel, out_shape=out_shape, in_specs=[spec] * 7, out_spe...  32.8 us
    all_to_all x1, starting transfers between devices, local(): lax.all_to_all(packed, 'enc', split_axis=0, concat_axis=0, tiled=True)  14.9 us
    all_to_all x1, starting transfers between devices, local(): lax.all_to_all(by_grp, 'grp', split_axis=0, concat_axis=0, tiled=True)  10.6 us
    all_to_all x1, waiting for transfers between devices, local(): lax.all_to_all(by_grp, 'grp', split_axis=0, concat_axis=0, tiled=True)  8.48 us
    pad x4, local copies, waits for them, and re-layouts, kernel_grads(): pad = lambda a: jnp.pad(a, ((0, extra), (0, 0)))  4.48 us
  transfers between devices with their start and end apart: 2, of which 2 were waited for; matrix products, arithmetic and copies ran while one was open for 2% of the time, Pallas kernels for 0%

profile of v8, /device:TPU:64, one launch (start us, length us, event | category | flops | bytes accessed | tf_op | source)
XLA Modules:
  0.0 129.0 jit_solution(16965909383380579793)
XLA Ops:
  0.7 0.7 compare_convert_fusion.2
  1.6 0.8 copy.14.live_ref
  2.4 1.9 %pad.25.q_ref = bf16[256,1024]{1,0:T(8,128)(2,1)} pad(bf16[192,1024]{1,0:T(8,128)(2,1)} %param.7, bf16[]{:T(256)} %constant.30.clone.1), padding=0_64x0_0 | pad | bytes 917506 | tf_op jit(solution)/shard_map/jit(_pad)/pad | solution.py:196
  4.3 0.9 pad.26.k_ref
  5.1 0.9 pad.27.v_ref
  6.0 0.9 pad.28.c_ref
  7.0 0.8 and_convert_fusion.mask_ref
  7.9 32.8 %shard_map.102 = (bf16[256,1024]{1,0:T(8,128)(2,1)}, bf16[256,1024]{1,0:T(8,128)(2,1)}, bf16[256,1024]{1,0:T(8,128)(2,1)}, f32[8,1024]{1,0:T(8,128)}) custom-call(bf16[256,1024]{1,0:T(8,128)(2,1)} %pad.25.q_ref, bf16[256,1024]{1,0:T(8,128)(2,1)} %pad.26.k_ref, bf16[256,1024]{1,0:T(8,128)(2,1)} %pad.27.v_ref, bf16[256,1024]{1,0:T(8,128)(2,1)} %pad.28.c_ref, ...), custom_call_target="tpu_custom_call" | custom-call | tf_op jit(solution)/shard_map/pallas_call | solution.py:210
  40.7 0.9 slice.36
  41.7 0.7 copy.15
  42.3 10.6 %all-to-all-start = ((f32[64,2,16]{2,1,0:T(2,128)}), f32[64,2,16]{2,1,0:T(2,128)S(1)}, u32[]{:S(2)}, u32[]{:S(2)}) async-start(f32[64,2,16]{2,1,0:T(2,128)} %copy.15), calls=%async_computation | async-start | bytes 131072 | tf_op jit(solution)/shard_map/all_to_all | solution.py:281
  53.0 0.2 select_reduce_fusion.1
  53.3 1.0 slice.33
  54.5 8.5 %all-to-all-done = f32[64,2,16]{2,1,0:T(2,128)S(1)} async-done(((f32[64,2,16]{2,1,0:T(2,128)}), f32[64,2,16]{2,1,0:T(2,128)S(1)}, u32[]{:S(2)}, u32[]{:S(2)}) %all-to-all-start) | async-done | bytes 8224 | tf_op jit(solution)/shard_map/all_to_all | solution.py:281
  63.2 1.7 %gather_fusion = bf16[12,16,3200]{2,1,0:T(8,128)(2,1)} fusion(bf16[12,16,3200]{2,1,0:T(8,128)(2,1)S(1)} %pad_maximum_fusion, s32[1024]{0:T(1024)S(1)} %pad_clamp_fusion.1), kind=kCustom, calls=%fused_computation | custom fusion | bytes 2457648 | tf_op jit(solution)/shard_map/jit(_take)/gather | solution.py:290
  64.9 14.9 %all-to-all-start.1 = ((bf16[12,16,3200]{2,1,0:T(8,128)(2,1)}), bf16[12,16,3200]{2,1,0:T(8,128)(2,1)S(1)}, u32[]{:S(2)}, u32[]{:S(2)}) async-start(bf16[12,16,3200]{2,1,0:T(8,128)(2,1)} %gather_fusion), calls=%async_computation.1 | async-start | bytes 2457600 | tf_op jit(solution)/shard_map/all_to_all | solution.py:291
  79.8 0.3 fusion.7
  80.1 0.2 reduce-window.8
  80.3 0.1 select_reduce_fusion.2
  80.5 46.3 %all-to-all-done.1 = bf16[12,16,3200]{2,1,0:T(8,128)(2,1)S(1)} async-done(((bf16[12,16,3200]{2,1,0:T(8,128)(2,1)}), bf16[12,16,3200]{2,1,0:T(8,128)(2,1)S(1)}, u32[]{:S(2)}, u32[]{:S(2)}) %all-to-all-start.1) | async-done | bytes 1228832 | tf_op jit(solution)/shard_map/all_to_all | solution.py:291
  126.8 0.1 slice.48
  126.9 0.6 gather_fusion.1
  127.5 0.9 fusion.13
  128.5 0.6 broadcast_multiply_fusion
  (40 shorter events, 1.0 us)
Async XLA Ops:
  0.6 3.6 %copy-start = (bf16[192,1024]{1,0:T(8,128)(2,1)S(1)}, bf16[192,1024]{1,0:T(8,128)(2,1)}, u32[]{:S(2)}) copy-start(bf16[192,1024]{1,0:T(8,128)(2,1)} %param.8) | copy-start | bytes 1179652
  0.6 4.5 %copy-start.1 = (bf16[192,1024]{1,0:T(8,128)(2,1)S(1)}, bf16[192,1024]{1,0:T(8,128)(2,1)}, u32[]{:S(2)}) copy-start(bf16[192,1024]{1,0:T(8,128)(2,1)} %param.9) | copy-start | bytes 1179652
  2.4 3.6 %copy-start.2 = (bf16[192,1024]{1,0:T(8,128)(2,1)S(1)}, bf16[192,1024]{1,0:T(8,128)(2,1)}, u32[]{:S(2)}) copy-start(bf16[192,1024]{1,0:T(8,128)(2,1)} %param.10) | copy-start | bytes 1179652
  4.3 2.7 %copy-start.6 = (s32[192]{0:T(256)S(1)}, s32[192]{0:T(256)}, u32[]{:S(2)}) copy-start(s32[192]{0:T(256)} %param.11) | copy-start | bytes 2308
  40.7 13.7 %copy-start.4 = (bf16[256,1024]{1,0:T(8,128)(2,1)S(1)}, bf16[256,1024]{1,0:T(8,128)(2,1)}, u32[]{:S(2)}) copy-start(bf16[256,1024]{1,0:T(8,128)(2,1)} %get-tuple-element.9) | copy-start | bytes 1572868
  40.7 13.7 %copy-start.3 = (bf16[256,1024]{1,0:T(8,128)(2,1)S(1)}, bf16[256,1024]{1,0:T(8,128)(2,1)}, u32[]{:S(2)}) copy-start(bf16[256,1024]{1,0:T(8,128)(2,1)} %get-tuple-element.10) | copy-start | bytes 1572868
  42.3 20.6 %all-to-all-start = ((f32[64,2,16]{2,1,0:T(2,128)}), f32[64,2,16]{2,1,0:T(2,128)S(1)}, u32[]{:S(2)}, u32[]{:S(2)}) async-start(f32[64,2,16]{2,1,0:T(2,128)} %copy.15), calls=%async_computation | async-start | bytes 131072 | tf_op jit(solution)/shard_map/all_to_all | solution.py:281
  64.9 14.9 %copy-start.5 = (s32[1,12,12]{2,0,1:T(1,128)S(1)}, s32[1,12,12]{2,0,1:T(1,128)}, u32[]{:S(2)}) copy-start(s32[1,12,12]{2,0,1:T(1,128)} %param.12) | copy-start | bytes 1732
  64.9 61.9 %all-to-all-start.1 = ((bf16[12,16,3200]{2,1,0:T(8,128)(2,1)}), bf16[12,16,3200]{2,1,0:T(8,128)(2,1)S(1)}, u32[]{:S(2)}, u32[]{:S(2)}) async-start(bf16[12,16,3200]{2,1,0:T(8,128)(2,1)} %gather_fusion), calls=%async_computation.1 | async-start | bytes 2457600 | tf_op jit(solution)/shard_map/all_to_all | solution.py:291

commit v9 on v6

--- a/solution.py
+++ b/solution.py
@@ -85,10 +85,20 @@
         pairs = [(i, i ^ bit) for i in range(grp_count)]
         current = keep + lax.ppermute(send, "grp", pairs)
         bit //= 2
-    current = current + 0.0
-    by_enc = jnp.broadcast_to(current[None], (enc_count,) + current.shape)
-    by_enc = lax.all_to_all(by_enc, "enc", split_axis=0, concat_axis=0, tiled=True)
-    return jnp.sum(by_enc, axis=0)
+    enc_rank = lax.axis_index("enc")
+    block = enc_count // 3
+    for bit in (1, 2):
+        pairs = [(i, i ^ bit) for i in range(enc_count)]
+        current = current + lax.ppermute(current, "enc", pairs)
+    ring = [current]
+    for step in (1, 2):
+        pairs = [(i, (i + step * block) % enc_count) for i in range(enc_count)]
+        ring.append(lax.ppermute(current, "enc", pairs))
+    stacked = jnp.stack(ring)
+    third = enc_rank // block
+    source_order = (third - jnp.arange(3, dtype=jnp.int32)) % 3
+    ordered = jnp.take(stacked, source_order, axis=0, mode="clip")
+    return (ordered[0] + ordered[1]) + ordered[2]
 
 
 def send_slots(own_plan, enc_count, per_slot):

time: 151 us -> 116 us (0.77)
  the two profiles are of different devices: /device:TPU:2 before, /device:TPU:52 now
where the time goes in v9:
time: 116 us; the launch traced here: 115 us
  starting transfers between devices  51.3 us (44%)
  waiting for transfers between devices  28.6 us (25%)
  local copies, waits for them, and re-layouts  17.9 us (15%)
  matrix products  10.1 us (9%)
  other arithmetic  5.91 us (5%)
  between operations  1.31 us (1%)
    ppermute x6, waiting for transfers between devices, reduce_gain_terms(): current = keep + lax.ppermute(send, 'grp', pairs)  18 us
    ppermute x6, starting transfers between devices, reduce_gain_terms(): current = keep + lax.ppermute(send, 'grp', pairs)  17.8 us
    all_to_all x1, starting transfers between devices, local_body(): lax.all_to_all(packed, 'enc', split_axis=0, concat_axis=0, tiled=True)  15.2 us
    ppermute x2, starting transfers between devices, reduce_gain_terms(): ring.append(lax.ppermute(current, 'enc', pairs))  9.74 us
    ppermute x2, starting transfers between devices, reduce_gain_terms(): current = current + lax.ppermute(current, 'enc', pairs)  8.6 us
    ppermute x2, waiting for transfers between devices, reduce_gain_terms(): ring.append(lax.ppermute(current, 'enc', pairs))  7.38 us
    unnamed x32, local copies, waits for them, and re-layouts  6.07 us
    dot_general x1, matrix products, block_grads(): jnp.einsum('hij,jhd->ihd', d_score, k_hat, preferred_element_type=f32)  3.26 us
  transfers between devices with their start and end apart: 11, of which 9 were waited for; matrix products, arithmetic and copies ran while one was open for 2% of the time, Pallas kernels for 0%

profile of v9, /device:TPU:52, one launch (start us, length us, event | category | flops | bytes accessed | tf_op | source)
XLA Modules:
  0.0 115.2 jit_solution(8221552698034195088)
XLA Ops:
  0.6 2.0 %copy.36 = bf16[192,1024]{0,1:T(8,128)(2,1)} copy(bf16[192,1024]{1,0:T(8,128)(2,1)} %param.10) | data formatting | bytes 786432 | tf_op args[3]
  7.7 1.7 %copy-done.4 = f32[16,192,192]{1,2,0:T(8,128)} copy-done((f32[16,192,192]{1,2,0:T(8,128)}, f32[16,192,192]{1,2,0:T(8,128)S(1)}, u32[]{:S(2)}) %copy-start.4) | copy-done | bytes 2359320
  12.4 3.0 %fusion.3 = f32[192,16]{0,1:T(8,128)S(1)} fusion(bf16[192,16,64]{0,2,1:T(8,128)(2,1)S(1)} %bitcast.54, bf16[192,16,64]{0,2,1:T(8,128)(2,1)S(1)} %bitcast.52, f32[16,192,192]{1,2,0:T(8,128)} %copy-done.4, f32[16,192]{1,0:T(8,128)S(1)} %get-tuple-element.22, pred[192,192]{0,1:T(8,128)(4,1)S(1)} %compare_and_fusion), kind=kOutput, calls=%fused_computation.12 | convolution fusion | flops 78443520 | bytes 3207168 | tf_op jit(solution)/shard_map/hij,jhd->ihd/dot_general | solution.py:54
  19.7 3.3 %multiply_reduce_fusion.1 = (f32[16,64]{1,0:T(8,128)S(1)}, f32[192,16]{0,1:T(8,128)S(1)}, f32[192,16]{0,1:T(8,128)S(1)}, f32[192,16]{0,1:T(8,128)S(1)}, f32[192,...) fusion(f32[192,16,64]{0,2,1:T(8,128)S(1)} %get-tuple-element.25, f32[192]{0:T(256)S(1)} %mul.170, ...), kind=kOutput, calls=%fused_computation.20 | convolution fusion | flops 78628864 | bytes 4391680 | tf_op jit(solution)/shard_map/hij,jhd->ihd/dot_general | solution.py:61
  24.1 1.8 %copy.43 = bf16[192,16,64]{2,1,0:T(8,128)(2,1)S(1)} copy(bf16[192,16,64]{0,2,1:T(8,128)(2,1)} %multiply_convert_fusion.1) | data formatting | bytes 786432 | tf_op jit(solution)/shard_map/convert_element_type | solution.py:68
  29.3 1.7 %gather_fusion = bf16[12,16,3072]{2,1,0:T(8,128)(2,1)} fusion(bf16[12,16,3072]{2,1,0:T(8,128)(2,1)S(1)} %pad_maximum_fusion, s32[1024]{0:T(1024)S(1)} %pad_clamp_fusion.2), kind=kCustom, calls=%fused_computation | custom fusion | bytes 2359344 | tf_op jit(solution)/shard_map/jit(_take)/gather | solution.py:157
  31.0 15.2 %all-to-all-start = ((bf16[12,16,3072]{2,1,0:T(8,128)(2,1)}), bf16[12,16,3072]{2,1,0:T(8,128)(2,1)S(1)}, u32[]{:S(2)}, u32[]{:S(2)}) async-start(bf16[12,16,3072]{2,1,0:T(8,128)(2,1)} %gather_fusion), calls=%async_computation | async-start | bytes 2359296 | tf_op jit(solution)/shard_map/all_to_all | solution.py:158
  46.3 3.8 %collective-permute-start = (f32[2,512]{1,0:T(2,128)S(1)}, f32[2,512]{1,0:T(2,128)S(1)}, u32[]{:S(2)}, u32[]{:S(2)}) collective-permute-start(f32[2,512]{1,0:T(2,128)S(1)} %broadcast_select_fusion), channel_id=1, source_target_pairs={{0,32},{1,33},{2,34},{3,35},{4,36},{5,37},{6,38},{7,39},{8,40},{9,... | collective-permute-start | bytes 12296 | tf_op jit(solution)/shard_map/ppermute | solution.py:86
  50.8 4.9 %collective-permute-done = f32[2,512]{1,0:T(2,128)S(1)} collective-permute-done((f32[2,512]{1,0:T(2,128)S(1)}, f32[2,512]{1,0:T(2,128)S(1)}, u32[]{:S(2)}, u32[]{:S(2)}) %collective-permute-start) | collective-permute-done | bytes 4128 | tf_op jit(solution)/shard_map/ppermute | solution.py:86
  55.8 4.0 %collective-permute-start.1 = (f32[2,256]{1,0:T(2,128)S(1)}, f32[2,256]{1,0:T(2,128)S(1)}, u32[]{:S(2)}, u32[]{:S(2)}) collective-permute-start(f32[2,256]{1,0:T(2,128)S(1)} %broadcast_select_fusion.1), channel_id=1, source_target_pairs={{0,16},{1,17},{2,18},{3,19},{4,20},{5,21},{6,22},{7,23},{8,24},{9,... | collective-permute-start | bytes 6152 | tf_op jit(solution)/shard_map/ppermute | solution.py:86
  59.9 2.3 %collective-permute-done.1 = f32[2,256]{1,0:T(2,128)S(1)} collective-permute-done((f32[2,256]{1,0:T(2,128)S(1)}, f32[2,256]{1,0:T(2,128)S(1)}, u32[]{:S(2)}, u32[]{:S(2)}) %collective-permute-start.1) | collective-permute-done | bytes 2080 | tf_op jit(solution)/shard_map/ppermute | solution.py:86
  62.2 2.6 %collective-permute-start.2 = (f32[2,128]{1,0:T(2,128)S(1)}, f32[2,128]{1,0:T(2,128)S(1)}, u32[]{:S(2)}, u32[]{:S(2)}) collective-permute-start(f32[2,128]{1,0:T(2,128)S(1)} %broadcast_select_fusion.2), channel_id=1, source_target_pairs={{0,8},{1,9},{2,10},{3,11},{4,12},{5,13},{6,14},{7,15},{8,0},{9,1},... | collective-permute-start | bytes 3080 | tf_op jit(solution)/shard_map/ppermute | solution.py:86
  64.8 2.8 %collective-permute-done.2 = f32[2,128]{1,0:T(2,128)S(1)} collective-permute-done((f32[2,128]{1,0:T(2,128)S(1)}, f32[2,128]{1,0:T(2,128)S(1)}, u32[]{:S(2)}, u32[]{:S(2)}) %collective-permute-start.2) | collective-permute-done | bytes 1056 | tf_op jit(solution)/shard_map/ppermute | solution.py:86
  67.7 2.4 %collective-permute-start.3 = (f32[2,64]{1,0:T(2,128)S(1)}, f32[2,64]{1,0:T(2,128)S(1)}, u32[]{:S(2)}, u32[]{:S(2)}) collective-permute-start(f32[2,64]{1,0:T(2,128)S(1)} %broadcast_select_fusion.3), channel_id=1, source_target_pairs={{0,4},{1,5},{2,6},{3,7},{4,0},{5,1},{6,2},{7,3},{8,12},{9,13},{10,... | collective-permute-start | bytes 1544 | tf_op jit(solution)/shard_map/ppermute | solution.py:86
  70.1 4.5 %collective-permute-done.3 = f32[2,64]{1,0:T(2,128)S(1)} collective-permute-done((f32[2,64]{1,0:T(2,128)S(1)}, f32[2,64]{1,0:T(2,128)S(1)}, u32[]{:S(2)}, u32[]{:S(2)}) %collective-permute-start.3) | collective-permute-done | bytes 544 | tf_op jit(solution)/shard_map/ppermute | solution.py:86
  74.8 3.1 %collective-permute-start.4 = (f32[2,32]{1,0:T(2,128)S(1)}, f32[2,32]{1,0:T(2,128)S(1)}, u32[]{:S(2)}, u32[]{:S(2)}) collective-permute-start(f32[2,32]{1,0:T(2,128)S(1)} %broadcast_select_fusion.4), channel_id=1, source_target_pairs={{0,2},{1,3},{2,0},{3,1},{4,6},{5,7},{6,4},{7,5},{8,10},{9,11},{10,... | collective-permute-start | bytes 776 | tf_op jit(solution)/shard_map/ppermute | solution.py:86
  77.9 2.3 %collective-permute-done.4 = f32[2,32]{1,0:T(2,128)S(1)} collective-permute-done((f32[2,32]{1,0:T(2,128)S(1)}, f32[2,32]{1,0:T(2,128)S(1)}, u32[]{:S(2)}, u32[]{:S(2)}) %collective-permute-start.4) | collective-permute-done | bytes 288 | tf_op jit(solution)/shard_map/ppermute | solution.py:86
  80.4 1.9 %collective-permute-start.5 = (f32[2,16]{1,0:T(2,128)S(1)}, f32[2,16]{1,0:T(2,128)S(1)}, u32[]{:S(2)}, u32[]{:S(2)}) collective-permute-start(f32[2,16]{1,0:T(2,128)S(1)} %broadcast_select_fusion.5), channel_id=1, source_target_pairs={{0,1},{1,0},{2,3},{3,2},{4,5},{5,4},{6,7},{7,6},{8,9},{9,8},{10,11... | collective-permute-start | bytes 392 | tf_op jit(solution)/shard_map/ppermute | solution.py:86
  83.5 3.9 %collective-permute-start.6 = (f32[2,16]{1,0:T(2,128)S(1)}, f32[2,16]{1,0:T(2,128)S(1)}, u32[]{:S(2)}, u32[]{:S(2)}) collective-permute-start(f32[2,16]{1,0:T(2,128)S(1)} %select_add_fusion.2), channel_id=1, source_target_pairs={{0,64},{64,0},{128,192},{192,128},{256,320},{320,256},{384,448},{4... | collective-permute-start | bytes 392 | tf_op jit(solution)/shard_map/ppermute | solution.py:92
  87.4 1.6 %collective-permute-done.6 = f32[2,16]{1,0:T(2,128)S(1)} collective-permute-done((f32[2,16]{1,0:T(2,128)S(1)}, f32[2,16]{1,0:T(2,128)S(1)}, u32[]{:S(2)}, u32[]{:S(2)}) %collective-permute-start.6) | collective-permute-done | bytes 160 | tf_op jit(solution)/shard_map/ppermute | solution.py:92
  89.0 4.7 %collective-permute-start.7 = (f32[2,16]{1,0:T(2,128)S(1)}, f32[2,16]{1,0:T(2,128)S(1)}, u32[]{:S(2)}, u32[]{:S(2)}) collective-permute-start(f32[2,16]{1,0:T(2,128)S(1)} %add.120), channel_id=1, source_target_pairs={{0,128},{64,192},{128,0},{192,64},{256,384},{320,448},{384,256},{4... | collective-permute-start | bytes 392 | tf_op jit(solution)/shard_map/ppermute | solution.py:92
  95.4 7.8 %collective-permute-start.9 = (f32[2,16]{1,0:T(2,128)S(1)}, f32[2,16]{1,0:T(2,128)S(1)}, u32[]{:S(2)}, u32[]{:S(2)}) collective-permute-start(f32[2,16]{1,0:T(2,128)S(1)} %add.121), channel_id=1, source_target_pairs={{0,512},{64,576},{128,640},{192,704},{256,0},{320,64},{384,128},{4... | collective-permute-start | bytes 392 | tf_op jit(solution)/shard_map/ppermute | solution.py:96
  103.1 2.0 %collective-permute-start.8 = (f32[2,16]{1,0:T(2,128)S(1)}, f32[2,16]{1,0:T(2,128)S(1)}, u32[]{:S(2)}, u32[]{:S(2)}) collective-permute-start(f32[2,16]{1,0:T(2,128)S(1)} %add.121), channel_id=1, source_target_pairs={{0,256},{64,320},{128,384},{192,448},{256,512},{320,576},{384,640}... | collective-permute-start | bytes 392 | tf_op jit(solution)/shard_map/ppermute | solution.py:96
  105.1 7.4 %collective-permute-done.8 = f32[2,16]{1,0:T(2,128)S(1)} collective-permute-done((f32[2,16]{1,0:T(2,128)S(1)}, f32[2,16]{1,0:T(2,128)S(1)}, u32[]{:S(2)}, u32[]{:S(2)}) %collective-permute-start.8) | collective-permute-done | bytes 160 | tf_op jit(solution)/shard_map/ppermute | solution.py:96
  (105 shorter events, 23.3 us)
Async XLA Ops:
  0.6 3.7 %copy-start.10 = (bf16[192,1024]{1,0:T(8,128)(2,1)S(1)}, bf16[192,1024]{1,0:T(8,128)(2,1)}, u32[]{:S(2)}) copy-start(bf16[192,1024]{1,0:T(8,128)(2,1)} %param.8) | copy-start | bytes 1179652
  4.0 1.0 copy-start.14
  5.5 3.8 %copy-start.8 = (bf16[192,1024]{0,1:T(8,128)(2,1)S(1)}, bf16[192,1024]{0,1:T(8,128)(2,1)}, u32[]{:S(2)}) copy-start(bf16[192,1024]{0,1:T(8,128)(2,1)} %copy.36) | copy-start | bytes 1179652
  7.7 1.7 %copy-start.4 = (f32[16,192,192]{1,2,0:T(8,128)}, f32[16,192,192]{1,2,0:T(8,128)S(1)}, u32[]{:S(2)}) copy-start(f32[16,192,192]{1,2,0:T(8,128)S(1)} %get-tuple-element.23) | copy-start | bytes 7077892
  9.3 2.8 %copy-start.9 = (bf16[192,1024]{1,0:T(8,128)(2,1)S(1)}, bf16[192,1024]{1,0:T(8,128)(2,1)}, u32[]{:S(2)}) copy-start(bf16[192,1024]{1,0:T(8,128)(2,1)} %param.9) | copy-start | bytes 1179652
  12.4 3.0 %copy-start.5 = (f32[16,192,192]{1,2,0:T(8,128)S(1)}, f32[16,192,192]{1,2,0:T(8,128)}, u32[]{:S(2)}) copy-start(f32[16,192,192]{1,2,0:T(8,128)} %copy-done.4) | copy-start | bytes 7077892
  16.5 1.2 %copy-start.2 = (bf16[16,192,192]{1,2,0:T(8,128)(2,1)}, bf16[16,192,192]{1,2,0:T(8,128)(2,1)S(1)}, u32[]{:S(2)}) copy-start(bf16[16,192,192]{1,2,0:T(8,128)(2,1)S(1)} %multiply_convert_fusion) | copy-start | bytes 3538948
  17.7 2.0 %copy-start.1 = (f32[192,16,64]{0,2,1:T(8,128)S(1)}, f32[192,16,64]{0,2,1:T(8,128)}, u32[]{:S(2)}) copy-start(f32[192,16,64]{0,2,1:T(8,128)} %copy-done) | copy-start | bytes 2359300
  24.1 3.1 %copy-start.3 = (f32[192,16,64]{0,2,1:T(8,128)S(1)}, f32[192,16,64]{0,2,1:T(8,128)}, u32[]{:S(2)}) copy-start(f32[192,16,64]{0,2,1:T(8,128)} %get-tuple-element.24) | copy-start | bytes 2359300
  25.9 2.9 %copy-start.13 = (s32[12]{0:T(128)S(1)}, s32[12]{0:T(128)}, u32[]{:S(2)}) copy-start(s32[12]{0:T(128)} %get-tuple-element.16) | copy-start | bytes 148
  25.9 3.3 %copy-start.6 = (bf16[12,16,1024]{2,1,0:T(8,128)(2,1)S(1)}, bf16[12,16,1024]{2,1,0:T(8,128)(2,1)}, u32[]{:S(2)}) copy-start(bf16[12,16,1024]{2,1,0:T(8,128)(2,1)} %convert_element_type.85) | copy-start | bytes 1179652
  27.2 2.0 %copy-start.7 = (bf16[12,16,1024]{2,1,0:T(8,128)(2,1)S(1)}, bf16[12,16,1024]{2,1,0:T(8,128)(2,1)}, u32[]{:S(2)}) copy-start(bf16[12,16,1024]{2,1,0:T(8,128)(2,1)} %convert_element_type.82) | copy-start | bytes 1179652
  29.2 21.0 %copy-start.12 = (s32[1,12,12]{2,0,1:T(1,128)S(1)}, s32[1,12,12]{2,0,1:T(1,128)}, u32[]{:S(2)}) copy-start(s32[1,12,12]{2,0,1:T(1,128)} %param.12) | copy-start | bytes 1732
  31.0 82.7 %all-to-all-start = ((bf16[12,16,3072]{2,1,0:T(8,128)(2,1)}), bf16[12,16,3072]{2,1,0:T(8,128)(2,1)S(1)}, u32[]{:S(2)}, u32[]{:S(2)}) async-start(bf16[12,16,3072]{2,1,0:T(8,128)(2,1)} %gather_fusion), calls=%async_computation | async-start | bytes 2359296 | tf_op jit(solution)/shard_map/all_to_all | solution.py:158
  46.3 9.4 %collective-permute-start = (f32[2,512]{1,0:T(2,128)S(1)}, f32[2,512]{1,0:T(2,128)S(1)}, u32[]{:S(2)}, u32[]{:S(2)}) collective-permute-start(f32[2,512]{1,0:T(2,128)S(1)} %broadcast_select_fusion), channel_id=1, source_target_pairs={{0,32},{1,33},{2,34},{3,35},{4,36},{5,37},{6,38},{7,39},{8,40},{9,... | collective-permute-start | bytes 12296 | tf_op jit(solution)/shard_map/ppermute | solution.py:86
  55.8 6.4 %collective-permute-start.1 = (f32[2,256]{1,0:T(2,128)S(1)}, f32[2,256]{1,0:T(2,128)S(1)}, u32[]{:S(2)}, u32[]{:S(2)}) collective-permute-start(f32[2,256]{1,0:T(2,128)S(1)} %broadcast_select_fusion.1), channel_id=1, source_target_pairs={{0,16},{1,17},{2,18},{3,19},{4,20},{5,21},{6,22},{7,23},{8,24},{9,... | collective-permute-start | bytes 6152 | tf_op jit(solution)/shard_map/ppermute | solution.py:86
  62.2 5.5 %collective-permute-start.2 = (f32[2,128]{1,0:T(2,128)S(1)}, f32[2,128]{1,0:T(2,128)S(1)}, u32[]{:S(2)}, u32[]{:S(2)}) collective-permute-start(f32[2,128]{1,0:T(2,128)S(1)} %broadcast_select_fusion.2), channel_id=1, source_target_pairs={{0,8},{1,9},{2,10},{3,11},{4,12},{5,13},{6,14},{7,15},{8,0},{9,1},... | collective-permute-start | bytes 3080 | tf_op jit(solution)/shard_map/ppermute | solution.py:86
  67.7 7.0 %collective-permute-start.3 = (f32[2,64]{1,0:T(2,128)S(1)}, f32[2,64]{1,0:T(2,128)S(1)}, u32[]{:S(2)}, u32[]{:S(2)}) collective-permute-start(f32[2,64]{1,0:T(2,128)S(1)} %broadcast_select_fusion.3), channel_id=1, source_target_pairs={{0,4},{1,5},{2,6},{3,7},{4,0},{5,1},{6,2},{7,3},{8,12},{9,13},{10,... | collective-permute-start | bytes 1544 | tf_op jit(solution)/shard_map/ppermute | solution.py:86
  74.8 5.5 %collective-permute-start.4 = (f32[2,32]{1,0:T(2,128)S(1)}, f32[2,32]{1,0:T(2,128)S(1)}, u32[]{:S(2)}, u32[]{:S(2)}) collective-permute-start(f32[2,32]{1,0:T(2,128)S(1)} %broadcast_select_fusion.4), channel_id=1, source_target_pairs={{0,2},{1,3},{2,0},{3,1},{4,6},{5,7},{6,4},{7,5},{8,10},{9,11},{10,... | collective-permute-start | bytes 776 | tf_op jit(solution)/shard_map/ppermute | solution.py:86
  80.4 3.0 %collective-permute-start.5 = (f32[2,16]{1,0:T(2,128)S(1)}, f32[2,16]{1,0:T(2,128)S(1)}, u32[]{:S(2)}, u32[]{:S(2)}) collective-permute-start(f32[2,16]{1,0:T(2,128)S(1)} %broadcast_select_fusion.5), channel_id=1, source_target_pairs={{0,1},{1,0},{2,3},{3,2},{4,5},{5,4},{6,7},{7,6},{8,9},{9,8},{10,11... | collective-permute-start | bytes 392 | tf_op jit(solution)/shard_map/ppermute | solution.py:86
  83.5 5.5 %collective-permute-start.6 = (f32[2,16]{1,0:T(2,128)S(1)}, f32[2,16]{1,0:T(2,128)S(1)}, u32[]{:S(2)}, u32[]{:S(2)}) collective-permute-start(f32[2,16]{1,0:T(2,128)S(1)} %select_add_fusion.2), channel_id=1, source_target_pairs={{0,64},{64,0},{128,192},{192,128},{256,320},{320,256},{384,448},{4... | collective-permute-start | bytes 392 | tf_op jit(solution)/shard_map/ppermute | solution.py:92
  89.0 6.4 %collective-permute-start.7 = (f32[2,16]{1,0:T(2,128)S(1)}, f32[2,16]{1,0:T(2,128)S(1)}, u32[]{:S(2)}, u32[]{:S(2)}) collective-permute-start(f32[2,16]{1,0:T(2,128)S(1)} %add.120), channel_id=1, source_target_pairs={{0,128},{64,192},{128,0},{192,64},{256,384},{320,448},{384,256},{4... | collective-permute-start | bytes 392 | tf_op jit(solution)/shard_map/ppermute | solution.py:92
  95.4 9.8 %collective-permute-start.9 = (f32[2,16]{1,0:T(2,128)S(1)}, f32[2,16]{1,0:T(2,128)S(1)}, u32[]{:S(2)}, u32[]{:S(2)}) collective-permute-start(f32[2,16]{1,0:T(2,128)S(1)} %add.121), channel_id=1, source_target_pairs={{0,512},{64,576},{128,640},{192,704},{256,0},{320,64},{384,128},{4... | collective-permute-start | bytes 392 | tf_op jit(solution)/shard_map/ppermute | solution.py:96
  103.1 9.4 %collective-permute-start.8 = (f32[2,16]{1,0:T(2,128)S(1)}, f32[2,16]{1,0:T(2,128)S(1)}, u32[]{:S(2)}, u32[]{:S(2)}) collective-permute-start(f32[2,16]{1,0:T(2,128)S(1)} %add.121), channel_id=1, source_target_pairs={{0,256},{64,320},{128,384},{192,448},{256,512},{320,576},{384,640}... | collective-permute-start | bytes 392 | tf_op jit(solution)/shard_map/ppermute | solution.py:96
  (2 other events, 1.8 us)

commit v10 on v3

--- a/solution.py
+++ b/solution.py
@@ -79,59 +79,61 @@
 
 
 def normalize_rows(rows, gain_row):
-    values = rows.astype(jnp.float32).reshape(rows.shape[0], HEADS, HD)
+    values = rows.astype(jnp.float32)
     centred = values - jnp.mean(values, -1, keepdims=True)
     inv_scale = lax.rsqrt(jnp.mean(centred * centred, -1, keepdims=True) + epsilon)
     normed = centred * inv_scale
-    return (normed, inv_scale, (normed * gain_row).astype(jnp.bfloat16))
+    return (normed, inv_scale, (normed * gain_row[:, None, :]).astype(jnp.bfloat16))
 
 
 def row_norm_back(d_hat, normed, inv_scale, gain_row, live_rows):
-    d_norm = d_hat * gain_row
+    d_norm = d_hat * gain_row[:, None, :]
     d_input = inv_scale * (
         d_norm
         - jnp.mean(d_norm, -1, keepdims=True)
         - normed * jnp.mean(d_norm * normed, -1, keepdims=True)
     )
-    gain_term = jnp.sum(d_hat * normed * live_rows[:, None, None], 0)
+    gain_term = jnp.sum(d_hat * normed * live_rows[None, :, None], 1)
     return (d_input, gain_term.reshape(-1))
 
 
+def head_major(rows):
+    return jnp.transpose(rows.reshape(rows.shape[0], HEADS, HD), (1, 0, 2))
+
+
+def row_major(heads):
+    return jnp.transpose(heads, (1, 0, 2)).reshape(heads.shape[1], HEADS * HD)
+
+
 def block_grads(query_rows, key_rows, value_rows, cotangent, piece_of, image_num, gains, live_rows):
-    rows = query_rows.shape[0]
-    three = (rows, HEADS, HD)
     gain_query = gains[0].reshape(HEADS, HD)
     gain_key = gains[1].reshape(HEADS, HD)
-    q_norm, q_scale, q_hat = normalize_rows(query_rows, gain_query)
-    k_norm, k_scale, k_hat = normalize_rows(key_rows, gain_key)
-    values = value_rows.reshape(three)
-    cot = cotangent.reshape(three)
+    q_norm, q_scale, q_hat = normalize_rows(head_major(query_rows), gain_query)
+    k_norm, k_scale, k_hat = normalize_rows(head_major(key_rows), gain_key)
+    values = head_major(value_rows)
+    cot = head_major(cotangent)
     factor = HD ** (-0.5)
     f32 = jnp.float32
-    scores = jnp.einsum("ihd,jhd->hij", q_hat, k_hat, preferred_element_type=f32) * factor
+    scores = jnp.einsum("hid,hjd->hij", q_hat, k_hat, preferred_element_type=f32) * factor
     same = (piece_of[:, None] == piece_of[None, :]) & (image_num[:, None] == image_num[None, :])
     weights = jnp.where(same[None], jnp.exp(scores), 0.0)
     probs = weights / jnp.sum(weights, -1, keepdims=True)
     probs_b = probs.astype(jnp.bfloat16)
-    attended = jnp.einsum("hij,jhd->ihd", probs_b, values, preferred_element_type=f32)
+    attended = jnp.einsum("hij,hjd->hid", probs_b, values, preferred_element_type=f32)
     row_delta = jnp.sum(cot.astype(f32) * attended, -1)
-    d_value = jnp.einsum("hij,ihd->jhd", probs_b, cot, preferred_element_type=f32)
-    d_prob = jnp.einsum("ihd,jhd->hij", cot, values, preferred_element_type=f32)
-    d_score = (probs * (d_prob - jnp.transpose(row_delta)[..., None]) * factor).astype(
-        jnp.bfloat16
-    )
-    d_qhat = jnp.einsum("hij,jhd->ihd", d_score, k_hat, preferred_element_type=f32)
-    d_khat = jnp.einsum("hij,ihd->jhd", d_score, q_hat, preferred_element_type=f32)
+    d_value = jnp.einsum("hij,hid->hjd", probs_b, cot, preferred_element_type=f32)
+    d_prob = jnp.einsum("hid,hjd->hij", cot, values, preferred_element_type=f32)
+    d_score = (probs * (d_prob - row_delta[..., None]) * factor).astype(jnp.bfloat16)
+    d_qhat = jnp.einsum("hij,hjd->hid", d_score, k_hat, preferred_element_type=f32)
+    d_khat = jnp.einsum("hij,hid->hjd", d_score, q_hat, preferred_element_type=f32)
     d_query, term_query = row_norm_back(d_qhat, q_norm, q_scale, gain_query, live_rows)
     d_key, term_key = row_norm_back(d_khat, k_norm, k_scale, gain_key, live_rows)
-    flat = (rows, HEADS * HD)
     return (
-        d_query.reshape(flat).astype(jnp.bfloat16),
-        d_key.reshape(flat).astype(jnp.bfloat16),
-        d_value.reshape(flat).astype(jnp.bfloat16),
+        row_major(d_query.astype(jnp.bfloat16)),
+        row_major(d_key.astype(jnp.bfloat16)),
+        row_major(d_value.astype(jnp.bfloat16)),
         jnp.stack([term_query, term_key]),
     )
-
 
 def send_slots(own_plan, enc_count, per_slot):
     owner_hit = (own_plan[:, None] == jnp.arange(enc_count, dtype=jnp.int32)[None, :]).astype(

time: 104 us -> 108 us (1.038)
  other arithmetic: 5.07 us -> 8.35 us
    another operation x0 -> x3, local copies, waits for them, and re-layouts: none -> 1.6 us  [the longest x1 0.53 us: local(): d_value = d_value.reshape(piece_shape)]
    reshape x2 -> x0, local copies, waits for them, and re-layouts: 1.4 us -> none  [normalize_rows(): values = rows.astype(jnp.float32).reshape(rows.shape[0], HEADS, HD)]
    unnamed x22 -> x24, local copies, waits for them, and re-layouts: 4.77 us -> 3.63 us
    convert_element_type x6 -> x5, local copies, waits for them, and re-layouts: 4.57 us -> 4.56 us  [the longest x1 1.69 us: block_grads(): d_value.astype(jnp.bfloat16)]
  transfers between devices with their start and end apart: 2 -> 2, of which waited for: 1 -> 1; matrix products, arithmetic and copies ran while one was open for 11% -> 10% of each run, Pallas kernels for 0% -> 0%
where the time goes in v10:
time: 108 us; the launch traced here: 107 us
  waiting for transfers between devices  46.3 us (43%)
  starting transfers between devices  25.4 us (24%)
  local copies, waits for them, and re-layouts  16.3 us (15%)
  matrix products  9.66 us (9%)
  other arithmetic  8.35 us (8%)
    all_to_all x1, waiting for transfers between devices, local(): lax.all_to_all(packed, 'enc', split_axis=0, concat_axis=0, tiled=True)  46.3 us
    all_to_all x1, starting transfers between devices, local(): lax.all_to_all(packed, 'enc', split_axis=0, concat_axis=0, tiled=True)  14.8 us
    all_to_all x1, starting transfers between devices, local(): lax.all_to_all(by_grp, 'grp', split_axis=0, concat_axis=0, tiled=True)  10.7 us
    dot_general x1, matrix products, block_grads(): jnp.einsum('hij,hid->hjd', probs_b, cot, preferred_element_type=f32)  3.67 us
    unnamed x24, local copies, waits for them, and re-layouts  3.63 us
  transfers between devices with their start and end apart: 2, of which 1 were waited for; matrix products, arithmetic and copies ran while one was open for 10% of the time, Pallas kernels for 0%

profile of v10, /device:TPU:66, one launch (start us, length us, event | category | flops | bytes accessed | tf_op | source)
XLA Modules:
  0.0 107.0 jit_solution(2614163191924253887)
XLA Ops:
  0.6 1.2 %compare_convert_fusion.2 = (f32[12]{0:T(128)S(1)}, s32[12]{0:T(128)}) fusion(s32[1,12,12]{2,0,1:T(1,128)} %param.12, s32[]{:T(128)S(6)} %select_n.17), kind=kLoop, calls=%fused_computation.79 | loop fusion | flops 24 | bytes 148 | tf_op jit(solution)/shard_map/convert_element_type | solution.py:188
  2.0 0.6 mul.194
  2.6 0.7 eq.84
  3.3 0.8 slice_reduce_fusion
  4.2 1.2 %copy.51 = bf16[192,1024]{0,1:T(8,128)(2,1)S(1)} copy(bf16[192,1024]{1,0:T(8,128)(2,1)} %param.9) | data formatting | bytes 786432 | tf_op args[2]
  5.4 1.2 %copy.50 = bf16[192,1024]{0,1:T(8,128)(2,1)S(1)} copy(bf16[192,1024]{1,0:T(8,128)(2,1)} %param.10) | data formatting | bytes 786432 | tf_op args[3]
  6.6 1.4 %copy.48 = f32[192,1024]{0,1:T(8,128)S(1)} copy(bf16[192,1024]{1,0:T(8,128)(2,1)} %param.7) | data formatting | bytes 1179648 | tf_op jit(solution)/shard_map/convert_element_type | solution.py:82
  10.5 0.9 compare_and_fusion
  11.3 1.0 fusion.10
  12.4 1.2 %fusion.1 = (f32[16,192]{1,0:T(8,128)S(1)}, f32[16,192,192]{1,2,0:T(8,128)S(1)}) fusion(pred[192,192]{0,1:T(8,128)(4,1)S(1)} %compare_and_fusion, f32[16,192,64]{1,2,0:T(8,128)S(1)} %get-tuple-element.36, f32[16,64]{1,0:T(8,128)S(1)} %mul.171, f32[16,192,64]{1,2,0:T(8,128)S(1)} %get-tuple-element.35, f32[16,64]{1,0:T(8,128)S(1)} %mul.165), kind=kOutput, calls=%fused_computation.5 | convolution fusion | flops 78050304 | bytes 3989504 | tf_op jit(solution)/shard_map/hid,hjd->hij/dot_general | solution.py:117
  13.6 0.9 fusion.2
  14.5 0.7 copy-done.1
  15.2 1.2 %multiply_convert_fusion = bf16[16,192,192]{1,2,0:T(8,128)(2,1)S(1)} fusion(bf16[16,192,64]{1,2,0:T(8,128)(2,1)S(1)} %bitcast.78, bf16[16,192,64]{1,2,0:T(8,128)(2,1)S(1)} %bitcast.81, f32[16,192]{1,0:T(8,128)S(1)} %fusion.2, f32[16,192]{1,0:T(8,128)S(1)} %get-tuple-element.32, f32[16,192,192]{1,2,0:T(8,128)S(1)} %get-tuple-element.33, ...), kind=kOutput, calls=%fused_computation.2 | convolution fusion | flops 79626240 | bytes 4386816 | tf_op jit(solution)/shard_map/hid,hjd->hij/dot_general | solution.py:125
  17.1 2.1 %multiply_reduce_fusion.3 = (f32[16,192]{1,0:T(8,128)S(1)}, f32[16,64]{1,0:T(8,128)S(1)}, f32[16,192]{1,0:T(8,128)S(1)}, f32[16,192]{1,0:T(8,128)S(1)}, f32[16,6...) fusion(f32[16,192,64]{1,2,0:T(8,128)S(1)} %get-tuple-element.35, f32[16,64]{1,0:T(8,128)S(1)} %mul.165, ...), kind=kOutput, calls=%fused_computation.26 | convolution fusion | flops 78628864 | bytes 4391680 | tf_op jit(solution)/shard_map/hij,hjd->hid/dot_general | solution.py:127
  19.3 0.7 copy.60
  20.0 10.7 %all-to-all-start = ((f32[64,2,16]{2,1,0:T(2,128)}), f32[64,2,16]{2,1,0:T(2,128)S(1)}, u32[]{:S(2)}, u32[]{:S(2)}) async-start(f32[64,2,16]{2,1,0:T(2,128)} %copy.60), calls=%async_computation | async-start | bytes 131072 | tf_op jit(solution)/shard_map/all_to_all | solution.py:200
  30.7 3.7 %fusion.3 = bf16[192,16,64]{0,2,1:T(8,128)(2,1)} fusion(bf16[16,192,64]{1,2,0:T(8,128)(2,1)} %bitcast.79, f32[16,192,192]{1,2,0:T(8,128)} %copy-done.1, f32[16,192]{1,0:T(8,128)S(1)} %get-tuple-element.32, pred[192,192]{0,1:T(8,128)(4,1)S(1)} %compare_and_fusion), kind=kOutput, calls=%fused_computation.9 | convolution fusion | flops 78053376 | bytes 3194880 | tf_op jit(solution)/shard_map/hij,hid->hjd/dot_general | solution.py:124
  34.8 1.2 %fusion.6 = bf16[192,16,64]{0,2,1:T(8,128)(2,1)} fusion(f32[192,16,64]{0,2,1:T(8,128)S(1)} %bitcast.75, f32[16,192,64]{1,2,0:T(8,128)S(1)} %fusion.14, f32[192,16]{0,1:T(8,128)S(1)} %multiply_bitcast_fusion, f32[192,16]{0,1:T(8,128)S(1)} %get-tuple-element.23, f32[192,16]{0,1:T(8,128)S(1)} %multiply_bitcast_fusion.1, f32[192,16]{0,1:T(8,128)S(1)} %get-tuple-element.21, ...), kind=kLoop, calls=%fused_computation.14 | loop fusion | flops 1572864 | bytes 2019328 | tf_op jit(solution)/shard_map/convert_element_type | solution.py:133
  36.5 1.7 %copy.59 = bf16[192,16,64]{2,1,0:T(8,128)(2,1)S(1)} copy(bf16[192,16,64]{0,2,1:T(8,128)(2,1)} %fusion.3) | data formatting | bytes 786432 | tf_op jit(solution)/shard_map/convert_element_type | solution.py:134
  38.7 0.6 copy.57
  41.3 1.7 %gather_fusion = bf16[12,16,3200]{2,1,0:T(8,128)(2,1)} fusion(bf16[12,16,3200]{2,1,0:T(8,128)(2,1)S(1)} %pad_maximum_fusion, s32[1024]{0:T(1024)S(1)} %pad_clamp_fusion.1), kind=kCustom, calls=%fused_computation | custom fusion | bytes 2457648 | tf_op jit(solution)/shard_map/jit(_take)/gather | solution.py:209
  43.1 14.8 %all-to-all-start.1 = ((bf16[12,16,3200]{2,1,0:T(8,128)(2,1)}), bf16[12,16,3200]{2,1,0:T(8,128)(2,1)S(1)}, u32[]{:S(2)}, u32[]{:S(2)}) async-start(bf16[12,16,3200]{2,1,0:T(8,128)(2,1)} %gather_fusion), calls=%async_computation.1 | async-start | bytes 2457600 | tf_op jit(solution)/shard_map/all_to_all | solution.py:210
  58.5 46.3 %all-to-all-done.1 = bf16[12,16,3200]{2,1,0:T(8,128)(2,1)S(1)} async-done(((bf16[12,16,3200]{2,1,0:T(8,128)(2,1)}), bf16[12,16,3200]{2,1,0:T(8,128)(2,1)S(1)}, u32[]{:S(2)}, u32[]{:S(2)}) %all-to-all-start.1) | async-done | bytes 1228832 | tf_op jit(solution)/shard_map/all_to_all | solution.py:210
  106.2 0.9 fusion.36
  (70 shorter events, 8.7 us)
Async XLA Ops:
  0.6 9.3 %copy-start.4 = (bf16[192,1024]{1,0:T(8,128)(2,1)S(1)}, bf16[192,1024]{1,0:T(8,128)(2,1)}, u32[]{:S(2)}) copy-start(bf16[192,1024]{1,0:T(8,128)(2,1)} %param.8) | copy-start | bytes 1179652
  6.6 7.9 %copy-start.3 = (bf16[192,1024]{0,1:T(8,128)(2,1)}, bf16[192,1024]{0,1:T(8,128)(2,1)S(1)}, u32[]{:S(2)}) copy-start(bf16[192,1024]{0,1:T(8,128)(2,1)S(1)} %copy.50) | copy-start | bytes 1179652
  8.7 0.6 copy-start.5
  13.6 1.7 %copy-start.1 = (f32[16,192,192]{1,2,0:T(8,128)}, f32[16,192,192]{1,2,0:T(8,128)S(1)}, u32[]{:S(2)}) copy-start(f32[16,192,192]{1,2,0:T(8,128)S(1)} %get-tuple-element.33) | copy-start | bytes 7077892
  16.4 0.7 copy-start.10
  20.0 21.1 %all-to-all-start = ((f32[64,2,16]{2,1,0:T(2,128)}), f32[64,2,16]{2,1,0:T(2,128)S(1)}, u32[]{:S(2)}, u32[]{:S(2)}) async-start(f32[64,2,16]{2,1,0:T(2,128)} %copy.60), calls=%async_computation | async-start | bytes 131072 | tf_op jit(solution)/shard_map/all_to_all | solution.py:200
  30.7 3.7 %copy-start.9 = (s32[12]{0:T(128)S(1)}, s32[12]{0:T(128)}, u32[]{:S(2)}) copy-start(s32[12]{0:T(128)} %get-tuple-element.13) | copy-start | bytes 148
  30.7 5.3 %copy-start.6 = (f32[192,16]{0,1:T(8,128)S(1)}, f32[192,16]{0,1:T(8,128)}, u32[]{:S(2)}) copy-start(f32[192,16]{0,1:T(8,128)} %get-tuple-element.19) | copy-start | bytes 36868
  30.7 5.3 %copy-start.7 = (f32[192,16]{0,1:T(8,128)S(1)}, f32[192,16]{0,1:T(8,128)}, u32[]{:S(2)}) copy-start(f32[192,16]{0,1:T(8,128)} %get-tuple-element.17) | copy-start | bytes 36868
  34.5 1.5 %copy-start = (f32[16,192,64]{1,2,0:T(8,128)S(1)}, f32[16,192,64]{1,2,0:T(8,128)}, u32[]{:S(2)}) copy-start(f32[16,192,64]{1,2,0:T(8,128)} %get-tuple-element.34) | copy-start | bytes 2359300
  36.0 2.7 %copy-start.2 = (bf16[192,16,64]{0,2,1:T(8,128)(2,1)S(1)}, bf16[192,16,64]{0,2,1:T(8,128)(2,1)}, u32[]{:S(2)}) copy-start(bf16[192,16,64]{0,2,1:T(8,128)(2,1)} %fusion.6) | copy-start | bytes 1179652
  41.2 16.6 %copy-start.8 = (s32[1,12,12]{2,0,1:T(1,128)S(1)}, s32[1,12,12]{2,0,1:T(1,128)}, u32[]{:S(2)}) copy-start(s32[1,12,12]{2,0,1:T(1,128)} %param.12) | copy-start | bytes 1732
  43.1 61.8 %all-to-all-start.1 = ((bf16[12,16,3200]{2,1,0:T(8,128)(2,1)}), bf16[12,16,3200]{2,1,0:T(8,128)(2,1)S(1)}, u32[]{:S(2)}, u32[]{:S(2)}) async-start(bf16[12,16,3200]{2,1,0:T(8,128)(2,1)} %gather_fusion), calls=%async_computation.1 | async-start | bytes 2457600 | tf_op jit(solution)/shard_map/all_to_all | solution.py:210

commit v11 on v3

--- a/solution.py
+++ b/solution.py
@@ -193,22 +193,21 @@
     d_key = d_key.reshape(piece_shape)
     d_value = d_value.reshape(piece_shape)
     cols = feat // grp_count
-    by_grp = jnp.transpose(gain_terms.reshape(2, grp_count, cols), (1, 0, 2))
-    grp_sum = jnp.sum(
-        lax.all_to_all(by_grp, "grp", split_axis=0, concat_axis=0, tiled=True), axis=0
-    )
-    grp_top = lax.reduce_precision(grp_sum, exponent_bits=8, mantissa_bits=7)
-    grp_hi = grp_top.astype(jnp.bfloat16)
-    grp_lo = (grp_sum - grp_top).astype(jnp.bfloat16)
-    extra = jnp.concatenate((grp_hi, grp_lo), axis=0)
-    extra = jnp.pad(extra, ((0, PIECE - 4), (0, 128 - cols)))
-    extra = jnp.broadcast_to(extra[None], (PMAX, PIECE, 128))
+    term_top = lax.reduce_precision(gain_terms, exponent_bits=8, mantissa_bits=7)
+    term_hi = term_top.astype(jnp.bfloat16)
+    term_lo = (gain_terms - term_top).astype(jnp.bfloat16)
+    extra = jnp.concatenate((term_hi, term_lo), axis=0).reshape(PIECE, 256)
+    extra = jnp.broadcast_to(extra[None], (PMAX, PIECE, 256))
     grads = jnp.concatenate((d_query, d_key, d_value, extra), axis=-1)
     packed = jnp.take(grads, slot_source, axis=0, mode="clip")
     received = lax.all_to_all(packed, "enc", split_axis=0, concat_axis=0, tiled=True)
     mine = from_slots(received[:, :, : 3 * feat], arrival_order)
-    parts = received[:, 0:4, 3 * feat : 3 * feat + cols].astype(jnp.float32)
-    shares = jnp.sum(parts[:, 0:2] + parts[:, 2:4], axis=0)
+    parts = received[:, :, 3 * feat :].astype(jnp.float32).reshape(enc_count, 4, feat)
+    group_total = jnp.sum(parts[:, 0:2] + parts[:, 2:4], axis=0)
+    by_grp = jnp.transpose(group_total.reshape(2, grp_count, cols), (1, 0, 2))
+    shares = jnp.sum(
+        lax.all_to_all(by_grp, "grp", split_axis=0, concat_axis=0, tiled=True), axis=0
+    )
     total_live = enc_count * grp_count * P_OWN * PIECE
     gain_grad = shares / math.sqrt(total_live)
     own_rows = P_OWN * PIECE

time: 104 us -> 129 us (1.24)
  the two profiles are of different devices: /device:TPU:66 before, /device:TPU:1 now
where the time goes in v11:
time: 129 us; the launch traced here: 128 us
  waiting for transfers between devices  52.9 us (41%)
  starting transfers between devices  28.9 us (22%)
  local copies, waits for them, and re-layouts  22.1 us (17%)
  other arithmetic  11.8 us (9%)
  matrix products  10.9 us (8%)
    all_to_all x1, waiting for transfers between devices, local(): lax.all_to_all(packed, 'enc', split_axis=0, concat_axis=0, tiled=True)  44.5 us
    all_to_all x1, starting transfers between devices, local(): lax.all_to_all(packed, 'enc', split_axis=0, concat_axis=0, tiled=True)  15.7 us
    all_to_all x1, starting transfers between devices, local(): lax.all_to_all(by_grp, 'grp', split_axis=0, concat_axis=0, tiled=True)  13.2 us
    all_to_all x1, waiting for transfers between devices, local(): lax.all_to_all(by_grp, 'grp', split_axis=0, concat_axis=0, tiled=True)  8.46 us
    unnamed x28, local copies, waits for them, and re-layouts  5.13 us
    dot_general x1, matrix products, block_grads(): jnp.einsum('hij,jhd->ihd', d_score, k_hat, preferred_element_type=f32)  3.37 us
    convert_element_type x2, local copies, waits for them, and re-layouts, block_grads(): d_key.reshape(flat).astype(jnp.bfloat16)  3.06 us
    another operation x2, local copies, waits for them, and re-layouts, block_grads(): jnp.stack([term_query, term_key])  2.72 us
  transfers between devices with their start and end apart: 2, of which 2 were waited for; matrix products, arithmetic and copies ran while one was open for 2% of the time, Pallas kernels for 0%

profile of v11, /device:TPU:1, one launch (start us, length us, event | category | flops | bytes accessed | tf_op | source)
XLA Modules:
  0.0 127.6 jit_solution(13337514627518546844)
XLA Ops:
  4.1 2.0 %copy.50 = bf16[192,1024]{0,1:T(8,128)(2,1)} copy(bf16[192,1024]{1,0:T(8,128)(2,1)} %param.9) | data formatting | bytes 786432 | tf_op args[2]
  6.1 2.0 %copy.49 = bf16[192,1024]{0,1:T(8,128)(2,1)} copy(bf16[192,1024]{1,0:T(8,128)(2,1)} %param.10) | data formatting | bytes 786432 | tf_op args[3]
  8.1 1.2 copy.47
  10.7 0.9 copy-done
  11.6 1.2 fusion.1
  12.8 0.9 fusion.4
  13.9 0.9 fusion.3
  14.8 2.3 %multiply_convert_fusion = bf16[16,192,192]{1,2,0:T(8,128)(2,1)} fusion(bf16[192,16,64]{0,2,1:T(8,128)(2,1)S(1)} %bitcast.49, bf16[192,16,64]{0,2,1:T(8,128)(2,1)S(1)} %bitcast.46, f32[16,192]{1,0:T(8,128)S(1)} %bitcast.51, f32[16,192]{1,0:T(8,128)S(1)} %get-tuple-element.24, f32[16,192,192]{1,2,0:T(8,128)S(1)} %get-tuple-element.25, ...), kind=kOutput, calls=%fused_computation.2 | convolution fusion | flops 79626240 | bytes 4386816 | tf_op jit(solution)/shard_map/ihd,jhd->hij/dot_general | solution.py:119
  18.3 2.2 %convolution_bitcast_fusion.1 = f32[192,16,64]{0,2,1:T(8,128)S(1)} fusion(bf16[16,192,192]{1,2,0:T(8,128)(2,1)} %multiply_convert_fusion, f32[192,16,64]{0,2,1:T(8,128)S(1)} %get-tuple-element.27, f32[16,64]{1,0:T(8,128)S(1)} %mul.148), kind=kOutput, calls=%fused_computation.8 | convolution fusion | flops 75890688 | bytes 2756608 | tf_op jit(solution)/shard_map/hij,ihd->jhd/dot_general | solution.py:124
  20.5 3.4 %multiply_reduce_fusion.3 = (f32[192,16]{0,1:T(8,128)S(1)}, f32[16,64]{1,0:T(8,128)}, f32[192,16]{0,1:T(8,128)}, f32[192,16]{0,1:T(8,128)}, f32[16,64]{1,0:T(8,1...) fusion(f32[192,16,64]{0,2,1:T(8,128)S(1)} %get-tuple-element.27, f32[16,64]{1,0:T(8,128)S(1)} %mul.148, f32[192]{0:T(256)} %mul.166, ...), kind=kOutput, calls=%fused_computation.23 | convolution fusion | flops 78628864 | bytes 4391680 | tf_op jit(solution)/shard_map/hij,jhd->ihd/dot_general | solution.py:123
  24.5 1.4 %stack_reshape.6 = f32[1,1024]{1,0:T(1,128)} reshape(f32[16,64]{1,0:T(8,128)} %get-tuple-element.5) | data formatting | bytes 8192 | tf_op jit(solution)/shard_map/stack;reshape | solution.py:132
  25.8 1.4 %stack_reshape.7 = f32[1,1024]{1,0:T(1,128)} reshape(f32[16,64]{1,0:T(8,128)} %get-tuple-element.20) | data formatting | bytes 8192 | tf_op jit(solution)/shard_map/stack;reshape | solution.py:132
  28.5 1.3 %broadcast_in_dim.36 = bf16[16,256]{1,0:T(8,128)(2,1)} reshape(bf16[4,1024]{1,0:T(4,128)(2,1)} %pad_maximum_fusion.2) | data formatting | bytes 16384 | tf_op jit(solution)/shard_map/broadcast_in_dim | solution.py:200
  29.8 1.3 %broadcast_multiply_fusion.3 = f32[192,16]{0,1:T(8,128)} fusion(f32[192,16]{0,1:T(8,128)} %get-tuple-element.8), kind=kLoop, calls=%fused_computation.55 | loop fusion | flops 3072 | bytes 24576 | tf_op jit(solution)/shard_map/div | solution.py:93
  32.6 1.9 %multiply_convert_fusion.1 = bf16[192,16,64]{0,2,1:T(8,128)(2,1)} fusion(f32[192,16,64]{0,2,1:T(8,128)S(1)} %copy-done.1, f32[192,16,64]{0,2,1:T(8,128)S(1)} %convolution_bitcast_fusion.1, f32[192,16]{0,1:T(8,128)S(1)} %broadcast_multiply_fusion, f32[192,16]{0,1:T(8,128)S(1)} %broadcast_multiply_fusion.1, f32[16,64]{1,0:T(8,128)S(1)} %mul.144, ...), kind=kLoop, calls=%fused_computation.20 | loop fusion | flops 1179648 | bytes 2007040 | tf_op jit(solution)/shard_map/convert_element_type | solution.py:130
  34.4 1.8 %copy.56 = bf16[192,16,64]{2,1,0:T(8,128)(2,1)S(1)} copy(bf16[192,16,64]{0,2,1:T(8,128)(2,1)} %multiply_convert_fusion.1) | data formatting | bytes 786432 | tf_op jit(solution)/shard_map/convert_element_type | solution.py:130
  36.2 1.3 %convert_element_type.89 = bf16[12,16,1024]{2,1,0:T(8,128)(2,1)} reshape(bf16[192,16,64]{2,1,0:T(8,128)(2,1)S(1)} %copy.56) | data formatting | bytes 786432 | tf_op jit(solution)/shard_map/convert_element_type | solution.py:130
  37.5 1.1 multiply_convert_fusion.2
  39.9 2.0 %gather_fusion = bf16[12,16,3328]{2,1,0:T(8,128)(2,1)} fusion(bf16[12,16,3328]{2,1,0:T(8,128)(2,1)S(1)} %pad_maximum_fusion, s32[1024]{0:T(1024)} %pad_clamp_fusion.1), kind=kCustom, calls=%fused_computation | custom fusion | bytes 2555952 | tf_op jit(solution)/shard_map/jit(_take)/gather | solution.py:202
  41.9 15.7 %all-to-all-start = ((bf16[12,16,3328]{2,1,0:T(8,128)(2,1)}), bf16[12,16,3328]{2,1,0:T(8,128)(2,1)S(1)}, u32[]{:S(2)}, u32[]{:S(2)}) async-start(bf16[12,16,3328]{2,1,0:T(8,128)(2,1)} %gather_fusion), calls=%async_computation | async-start | bytes 2555904 | tf_op jit(solution)/shard_map/all_to_all | solution.py:203
  58.3 44.5 %all-to-all-done = bf16[12,16,3328]{2,1,0:T(8,128)(2,1)S(1)} async-done(((bf16[12,16,3328]{2,1,0:T(8,128)(2,1)}), bf16[12,16,3328]{2,1,0:T(8,128)(2,1)S(1)}, u32[]{:S(2)}, u32[]{:S(2)}) %all-to-all-start) | async-done | bytes 1277984 | tf_op jit(solution)/shard_map/all_to_all | solution.py:203
  103.7 13.2 %all-to-all-start.1 = ((f32[64,2,16]{2,1,0:T(2,128)}), f32[64,2,16]{2,1,0:T(2,128)S(1)}, u32[]{:S(2)}, u32[]{:S(2)}) async-start(f32[64,2,16]{2,1,0:T(2,128)} %copy.59), calls=%async_computation.1 | async-start | bytes 131072 | tf_op jit(solution)/shard_map/all_to_all | solution.py:209
  117.6 0.9 fusion.19
  118.5 8.5 %all-to-all-done.1 = f32[64,2,16]{2,1,0:T(2,128)S(1)} async-done(((f32[64,2,16]{2,1,0:T(2,128)}), f32[64,2,16]{2,1,0:T(2,128)S(1)}, u32[]{:S(2)}, u32[]{:S(2)}) %all-to-all-start.1) | async-done | bytes 8224 | tf_op jit(solution)/shard_map/all_to_all | solution.py:209
  (76 shorter events, 13.6 us)
Async XLA Ops:
  0.6 9.0 %copy-start.7 = (bf16[192,1024]{1,0:T(8,128)(2,1)S(1)}, bf16[192,1024]{1,0:T(8,128)(2,1)}, u32[]{:S(2)}) copy-start(bf16[192,1024]{1,0:T(8,128)(2,1)} %param.8) | copy-start | bytes 1179652
  9.3 0.8 copy-start.12
  9.6 4.1 %copy-start.8 = (f32[192,16]{0,1:T(8,128)}, f32[192,16]{0,1:T(8,128)S(1)}, u32[]{:S(2)}) copy-start(f32[192,16]{0,1:T(8,128)S(1)} %add_rsqrt_fusion.1) | copy-start | bytes 36868
  10.2 3.5 %copy-start.9 = (f32[192,16]{0,1:T(8,128)}, f32[192,16]{0,1:T(8,128)S(1)}, u32[]{:S(2)}) copy-start(f32[192,16]{0,1:T(8,128)S(1)} %add_rsqrt_fusion) | copy-start | bytes 36868
  10.7 1.0 copy-start
  10.7 2.1 %copy-start.6 = (bf16[192,1024]{0,1:T(8,128)(2,1)S(1)}, bf16[192,1024]{0,1:T(8,128)(2,1)}, u32[]{:S(2)}) copy-start(bf16[192,1024]{0,1:T(8,128)(2,1)} %copy.49) | copy-start | bytes 1179652
  12.8 1.0 copy-start.5
  17.1 3.4 %copy-start.1 = (f32[192,16,64]{0,2,1:T(8,128)S(1)}, f32[192,16,64]{0,2,1:T(8,128)}, u32[]{:S(2)}) copy-start(f32[192,16,64]{0,2,1:T(8,128)} %copy-done) | copy-start | bytes 2359300
  18.3 2.2 %copy-start.2 = (bf16[16,192,192]{1,2,0:T(8,128)(2,1)S(1)}, bf16[16,192,192]{1,2,0:T(8,128)(2,1)}, u32[]{:S(2)}) copy-start(bf16[16,192,192]{1,2,0:T(8,128)(2,1)} %multiply_convert_fusion) | copy-start | bytes 3538948
  34.4 3.1 %copy-start.3 = (f32[192,16,64]{0,2,1:T(8,128)S(1)}, f32[192,16,64]{0,2,1:T(8,128)}, u32[]{:S(2)}) copy-start(f32[192,16,64]{0,2,1:T(8,128)} %get-tuple-element.26) | copy-start | bytes 2359300
  36.2 3.6 %copy-start.10 = (bf16[16,256]{1,0:T(8,128)(2,1)S(1)}, bf16[16,256]{1,0:T(8,128)(2,1)}, u32[]{:S(2)}) copy-start(bf16[16,256]{1,0:T(8,128)(2,1)} %broadcast_in_dim.36) | copy-start | bytes 24580
  37.5 2.3 %copy-start.4 = (bf16[12,16,1024]{2,1,0:T(8,128)(2,1)S(1)}, bf16[12,16,1024]{2,1,0:T(8,128)(2,1)}, u32[]{:S(2)}) copy-start(bf16[12,16,1024]{2,1,0:T(8,128)(2,1)} %convert_element_type.89) | copy-start | bytes 1179652
  39.9 17.7 %copy-start.11 = (s32[1,12,12]{2,0,1:T(1,128)S(1)}, s32[1,12,12]{2,0,1:T(1,128)}, u32[]{:S(2)}) copy-start(s32[1,12,12]{2,0,1:T(1,128)} %param.12) | copy-start | bytes 1732
  41.9 60.8 %all-to-all-start = ((bf16[12,16,3328]{2,1,0:T(8,128)(2,1)}), bf16[12,16,3328]{2,1,0:T(8,128)(2,1)S(1)}, u32[]{:S(2)}, u32[]{:S(2)}) async-start(bf16[12,16,3328]{2,1,0:T(8,128)(2,1)} %gather_fusion), calls=%async_computation | async-start | bytes 2555904 | tf_op jit(solution)/shard_map/all_to_all | solution.py:203
  103.7 23.3 %all-to-all-start.1 = ((f32[64,2,16]{2,1,0:T(2,128)}), f32[64,2,16]{2,1,0:T(2,128)S(1)}, u32[]{:S(2)}, u32[]{:S(2)}) async-start(f32[64,2,16]{2,1,0:T(2,128)} %copy.59), calls=%async_computation.1 | async-start | bytes 131072 | tf_op jit(solution)/shard_map/all_to_all | solution.py:209

commit v12 on v3

--- a/solution.py
+++ b/solution.py
@@ -169,7 +169,7 @@
 
 
 def from_slots(received, arrival_order):
-    return jnp.take(received, arrival_order, axis=0, mode="clip")
+    return received.at[arrival_order].get(mode="promise_in_bounds")
 
 
 def local(query_raw, key_raw, value_rows, out_cotangent, image_ids, owners, gains):
@@ -204,7 +204,7 @@
     extra = jnp.pad(extra, ((0, PIECE - 4), (0, 128 - cols)))
     extra = jnp.broadcast_to(extra[None], (PMAX, PIECE, 128))
     grads = jnp.concatenate((d_query, d_key, d_value, extra), axis=-1)
-    packed = jnp.take(grads, slot_source, axis=0, mode="clip")
+    packed = grads.at[slot_source].get(mode="promise_in_bounds")
     received = lax.all_to_all(packed, "enc", split_axis=0, concat_axis=0, tiled=True)
     mine = from_slots(received[:, :, : 3 * feat], arrival_order)
     parts = received[:, 0:4, 3 * feat : 3 * feat + cols].astype(jnp.float32)

time: 104 us -> 104 us (level)
  no operation moved by 1% of the time
where the time goes in v12:
time: 104 us
  waiting for transfers between devices  46.3 us (45%)
  starting transfers between devices  25.4 us (24%)
  local copies, waits for them, and re-layouts  16.1 us (15%)
  matrix products  9.75 us (9%)
  other arithmetic  5.08 us (5%)
    all_to_all x1, waiting for transfers between devices, local(): lax.all_to_all(packed, 'enc', split_axis=0, concat_axis=0, tiled=True)  46.3 us
    all_to_all x1, starting transfers between devices, local(): lax.all_to_all(packed, 'enc', split_axis=0, concat_axis=0, tiled=True)  14.8 us
    all_to_all x1, starting transfers between devices, local(): lax.all_to_all(by_grp, 'grp', split_axis=0, concat_axis=0, tiled=True)  10.7 us
    unnamed x22, local copies, waits for them, and re-layouts  4.77 us
    dot_general x1, matrix products, block_grads(): jnp.einsum('hij,ihd->jhd', probs_b, cot, preferred_element_type=f32)  3.74 us
    convert_element_type x2, local copies, waits for them, and re-layouts, block_grads(): d_value.reshape(flat).astype(jnp.bfloat16)  2.22 us
  transfers between devices with their start and end apart: 2, of which 1 were waited for; matrix products, arithmetic and copies ran while one was open for 11% of the time, Pallas kernels for 0%

profile of v12, /device:TPU:66, one launch (start us, length us, event | category | flops | bytes accessed | tf_op | source)
XLA Modules:
  0.0 103.7 jit_solution(15324571655174381448)
XLA Ops:
  0.6 0.7 compare_convert_fusion.2
  1.6 0.8 slice_reduce_fusion
  2.5 2.0 %copy.52 = bf16[192,1024]{0,1:T(8,128)(2,1)} copy(bf16[192,1024]{1,0:T(8,128)(2,1)} %param.9) | data formatting | bytes 786432 | tf_op args[2]
  4.5 2.0 %copy.51 = bf16[192,1024]{0,1:T(8,128)(2,1)} copy(bf16[192,1024]{1,0:T(8,128)(2,1)} %param.10) | data formatting | bytes 786432 | tf_op args[3]
  6.5 1.2 %copy.49 = f32[192,1024]{0,1:T(8,128)S(1)} copy(bf16[192,1024]{1,0:T(8,128)(2,1)} %param.7) | data formatting | bytes 1179648 | tf_op jit(solution)/shard_map/reshape | solution.py:82
  9.1 1.2 %fusion.1 = (f32[16,192]{1,0:T(8,128)S(1)}, f32[16,192,192]{1,2,0:T(8,128)S(1)}) fusion(pred[192,192]{0,1:T(8,128)(4,1)S(1)} %compare_and_fusion, f32[192,16,64]{0,2,1:T(8,128)S(1)} %get-tuple-element.28, f32[16,64]{1,0:T(8,128)S(1)} %mul.144, f32[192,16,64]{0,2,1:T(8,128)S(1)} %get-tuple-element.27, f32[16,64]{1,0:T(8,128)S(1)} %mul.148), kind=kOutput, calls=%fused_computation.5 | convolution fusion | flops 78050304 | bytes 3989504 | tf_op jit(solution)/shard_map/ihd,jhd->hij/dot_general | solution.py:111
  10.6 0.9 fusion.3
  11.9 1.2 %multiply_convert_fusion = bf16[16,192,192]{1,2,0:T(8,128)(2,1)S(1)} fusion(bf16[192,16,64]{0,2,1:T(8,128)(2,1)S(1)} %bitcast.56, bf16[192,16,64]{0,2,1:T(8,128)(2,1)S(1)} %bitcast.58, f32[16,192]{1,0:T(8,128)S(1)} %bitcast.59, f32[16,192]{1,0:T(8,128)S(1)} %get-tuple-element.24, f32[16,192,192]{1,2,0:T(8,128)S(1)} %get-tuple-element.25, ...), kind=kOutput, calls=%fused_computation.2 | convolution fusion | flops 79626240 | bytes 4386816 | tf_op jit(solution)/shard_map/ihd,jhd->hij/dot_general | solution.py:119
  13.1 0.7 convolution_bitcast_fusion.1
  13.8 2.1 %multiply_reduce_fusion.3 = (f32[192,16]{0,1:T(8,128)S(1)}, f32[16,64]{1,0:T(8,128)S(1)}, f32[192,16]{0,1:T(8,128)S(1)}, f32[192,16]{0,1:T(8,128)S(1)}, f32[16,6...) fusion(f32[192,16,64]{0,2,1:T(8,128)S(1)} %get-tuple-element.27, f32[16,64]{1,0:T(8,128)S(1)} %mul.148, ...), kind=kOutput, calls=%fused_computation.23 | convolution fusion | flops 78628864 | bytes 4391680 | tf_op jit(solution)/shard_map/hij,jhd->ihd/dot_general | solution.py:123
  16.0 0.7 copy.61
  16.7 10.7 %all-to-all-start = ((f32[64,2,16]{2,1,0:T(2,128)}), f32[64,2,16]{2,1,0:T(2,128)S(1)}, u32[]{:S(2)}, u32[]{:S(2)}) async-start(f32[64,2,16]{2,1,0:T(2,128)} %copy.61), calls=%async_computation | async-start | bytes 131072 | tf_op jit(solution)/shard_map/all_to_all | solution.py:198
  27.4 3.7 %fusion.4 = bf16[192,16,64]{0,2,1:T(8,128)(2,1)} fusion(bf16[192,16,64]{0,2,1:T(8,128)(2,1)} %bitcast.54, f32[16,192,192]{1,2,0:T(8,128)} %copy-done.3, f32[16,192]{1,0:T(8,128)S(1)} %get-tuple-element.24, pred[192,192]{0,1:T(8,128)(4,1)S(1)} %compare_and_fusion), kind=kOutput, calls=%fused_computation.12 | convolution fusion | flops 78053376 | bytes 3194880 | tf_op jit(solution)/shard_map/hij,ihd->jhd/dot_general | solution.py:118
  31.6 1.2 %multiply_convert_fusion.1 = bf16[192,16,64]{0,2,1:T(8,128)(2,1)} fusion(f32[192,16,64]{0,2,1:T(8,128)S(1)} %copy-done.1, f32[192,16,64]{0,2,1:T(8,128)S(1)} %convolution_bitcast_fusion.1, f32[192,16]{0,1:T(8,128)S(1)} %broadcast_multiply_fusion, f32[192,16]{0,1:T(8,128)S(1)} %broadcast_multiply_fusion.1, f32[16,64]{1,0:T(8,128)S(1)} %mul.144, ...), kind=kLoop, calls=%fused_computation.20 | loop fusion | flops 1179648 | bytes 2007040 | tf_op jit(solution)/shard_map/convert_element_type | solution.py:130
  33.1 1.7 %copy.60 = bf16[192,16,64]{2,1,0:T(8,128)(2,1)S(1)} copy(bf16[192,16,64]{0,2,1:T(8,128)(2,1)} %fusion.4) | data formatting | bytes 786432 | tf_op jit(solution)/shard_map/convert_element_type | solution.py:131
  34.8 0.5 convert_element_type.96
  35.4 0.6 copy.58
  36.6 0.6 copy.56
  38.0 1.7 %gather_fusion = bf16[12,16,3200]{2,1,0:T(8,128)(2,1)} fusion(bf16[12,16,3200]{2,1,0:T(8,128)(2,1)S(1)} %pad_maximum_fusion, s32[1024]{0:T(1024)S(1)} %pad_clamp_fusion.1), kind=kCustom, calls=%fused_computation | custom fusion | bytes 2457648 | tf_op jit(solution)/shard_map/gather | solution.py:207
  39.7 14.8 %all-to-all-start.1 = ((bf16[12,16,3200]{2,1,0:T(8,128)(2,1)}), bf16[12,16,3200]{2,1,0:T(8,128)(2,1)S(1)}, u32[]{:S(2)}, u32[]{:S(2)}) async-start(bf16[12,16,3200]{2,1,0:T(8,128)(2,1)} %gather_fusion), calls=%async_computation.1 | async-start | bytes 2457600 | tf_op jit(solution)/shard_map/all_to_all | solution.py:208
  55.2 46.3 %all-to-all-done.1 = bf16[12,16,3200]{2,1,0:T(8,128)(2,1)S(1)} async-done(((bf16[12,16,3200]{2,1,0:T(8,128)(2,1)}), bf16[12,16,3200]{2,1,0:T(8,128)(2,1)S(1)}, u32[]{:S(2)}, u32[]{:S(2)}) %all-to-all-start.1) | async-done | bytes 1228832 | tf_op jit(solution)/shard_map/all_to_all | solution.py:208
  101.5 0.6 broadcast_multiply_fusion.6
  102.2 0.6 gather_fusion.1
  102.8 0.9 fusion.27
  (70 shorter events, 5.3 us)
Async XLA Ops:
  0.6 7.4 %copy-start.7 = (bf16[192,1024]{1,0:T(8,128)(2,1)S(1)}, bf16[192,1024]{1,0:T(8,128)(2,1)}, u32[]{:S(2)}) copy-start(bf16[192,1024]{1,0:T(8,128)(2,1)} %param.8) | copy-start | bytes 1179652
  7.8 0.8 copy-start.9
  9.0 4.7 %copy-start = (f32[192,16,64]{0,2,1:T(8,128)}, f32[192,16,64]{0,2,1:T(8,128)S(1)}, u32[]{:S(2)}) copy-start(f32[192,16,64]{0,2,1:T(8,128)S(1)} %get-tuple-element.28) | copy-start | bytes 2359300
  9.1 1.4 %copy-start.5 = (bf16[192,1024]{0,1:T(8,128)(2,1)S(1)}, bf16[192,1024]{0,1:T(8,128)(2,1)}, u32[]{:S(2)}) copy-start(bf16[192,1024]{0,1:T(8,128)(2,1)} %copy.51) | copy-start | bytes 1179652
  9.1 1.6 %copy-start.6 = (bf16[192,1024]{0,1:T(8,128)(2,1)S(1)}, bf16[192,1024]{0,1:T(8,128)(2,1)}, u32[]{:S(2)}) copy-start(bf16[192,1024]{0,1:T(8,128)(2,1)} %copy.52) | copy-start | bytes 1179652
  10.3 1.7 %copy-start.3 = (f32[16,192,192]{1,2,0:T(8,128)}, f32[16,192,192]{1,2,0:T(8,128)S(1)}, u32[]{:S(2)}) copy-start(f32[16,192,192]{1,2,0:T(8,128)S(1)} %get-tuple-element.25) | copy-start | bytes 7077892
  16.7 21.1 %all-to-all-start = ((f32[64,2,16]{2,1,0:T(2,128)}), f32[64,2,16]{2,1,0:T(2,128)S(1)}, u32[]{:S(2)}, u32[]{:S(2)}) async-start(f32[64,2,16]{2,1,0:T(2,128)} %copy.61), calls=%async_computation | async-start | bytes 131072 | tf_op jit(solution)/shard_map/all_to_all | solution.py:198
  27.3 4.2 %copy-start.1 = (f32[192,16,64]{0,2,1:T(8,128)S(1)}, f32[192,16,64]{0,2,1:T(8,128)}, u32[]{:S(2)}) copy-start(f32[192,16,64]{0,2,1:T(8,128)} %copy-done) | copy-start | bytes 2359300
  31.2 1.5 %copy-start.2 = (f32[192,16,64]{0,2,1:T(8,128)S(1)}, f32[192,16,64]{0,2,1:T(8,128)}, u32[]{:S(2)}) copy-start(f32[192,16,64]{0,2,1:T(8,128)} %get-tuple-element.26) | copy-start | bytes 2359300
  32.7 2.6 %copy-start.4 = (bf16[192,16,64]{0,2,1:T(8,128)(2,1)S(1)}, bf16[192,16,64]{0,2,1:T(8,128)(2,1)}, u32[]{:S(2)}) copy-start(bf16[192,16,64]{0,2,1:T(8,128)(2,1)} %multiply_convert_fusion.1) | copy-start | bytes 1179652
  37.9 16.6 %copy-start.8 = (s32[1,12,12]{2,0,1:T(1,128)S(1)}, s32[1,12,12]{2,0,1:T(1,128)}, u32[]{:S(2)}) copy-start(s32[1,12,12]{2,0,1:T(1,128)} %param.12) | copy-start | bytes 1732
  39.7 61.8 %all-to-all-start.1 = ((bf16[12,16,3200]{2,1,0:T(8,128)(2,1)}), bf16[12,16,3200]{2,1,0:T(8,128)(2,1)S(1)}, u32[]{:S(2)}, u32[]{:S(2)}) async-start(bf16[12,16,3200]{2,1,0:T(8,128)(2,1)} %gather_fusion), calls=%async_computation.1 | async-start | bytes 2457600 | tf_op jit(solution)/shard_map/all_to_all | solution.py:208
